TPU v7x, 256 devices: a whole 4x4x8 slice. The times are simulated.
256 devices in a mesh: tm: 8 (over y, core), node: 32 (over z, x).
Axes of the slice: x: 4, y: 4, z: 8, core: 2. Of those that a mesh axis runs over, the one named last changes fastest.
Arguments:
- inputs: bfloat16 [32768, 2048], P('node', 'tm'), may hold values from -6 to 6
- conv_weight: bfloat16 [3, 64, 256], replicated, may hold values from -0.4375 to 0.4375
- conv_bias: float32 [256], replicated, may hold values from -3 to 3
- tile_values: bfloat16 [256, 4, 128, 128], P('node'), may hold values from -0.25 to 0.25
- tile_cols: int32 [256, 4], P('node'), may hold values from -2 to 257, as said below
- tile_count: int32 [256], P('node'), may hold values from 1 to 4, as said below
- cheb_weight: bfloat16 [3, 128, 128], replicated, may hold values from -0.3125 to 0.3125
- cheb_bias: float32 [128], replicated, may hold values from -3 to 3
Outputs:
- graph_out: bfloat16 [32768, 32, 128], P('node', 'tm')
Inputs may be any that keep to these rules, and one draw needn't show every extreme that they name: `tile_cols`: tile 0 of block b names b itself; tiles 1 to 3 name b plus distinct nonzero offsets in -2 to 2. Tile slots at or after tile_count[b] are unused.
All inputs are finite; a program needn't handle non-finite values.
Results may differ from a plain program's by a relative error of at most 0.0056.
Values may be sent and summed in bfloat16 or wider, within the bound.
No kernel may reach another device: no remote copies, remote signals or barrier semaphores. Data moves between devices by JAX's collectives and lax.ppermute only.
A program may use at most 64 MiB of HBM per device.

v0:
```python
import jax
import jax.numpy as jnp
from jax import lax
from jax.sharding import PartitionSpec as P

HB = 2
TPB = 4


def with_halo(cells, sides, width):
    for axis, dim in sides:
        count = lax.axis_size(axis)
        ends = count - 1
        head = lax.slice_in_dim(cells, 0, width, axis=dim)
        tail = lax.slice_in_dim(cells, cells.shape[dim] - width, cells.shape[dim], axis=dim)
        cells = jnp.concatenate(
            [
                lax.ppermute(tail, axis, [(i, (i + 1) % count) for i in range(ends)]),
                cells,
                lax.ppermute(head, axis, [((i + 1) % count, i) for i in range(ends)]),
            ],
            axis=dim,
        )
    return cells


def passed_along(value, axis, by):
    length = lax.axis_size(axis)
    pairs = [(i, i + by) for i in range(length) if 0 <= i + by < length]
    return lax.ppermute(value, axis, pairs)


def build_band(tile_set, col_ids, live_count, first_block):
    block_count = tile_set.shape[0]
    row_ids = first_block + jnp.arange(block_count, dtype=jnp.int32)
    offset = col_ids - row_ids[:, None] + HB
    live_mask = jnp.arange(TPB, dtype=jnp.int32)[None, :] < live_count[:, None]
    one_hot = (
        offset[:, :, None] == jnp.arange(2 * HB + 1, dtype=jnp.int32)[None, None, :]
    ) & live_mask[:, :, None]
    band_tiles = jnp.einsum(
        "bjo,bjpq->bopq", one_hot.astype(jnp.bfloat16), tile_set, preferred_element_type=jnp.float32
    )
    return band_tiles.astype(jnp.bfloat16)


def band_product(band_tiles, extended):
    block_count = band_tiles.shape[0]
    total = jnp.einsum(
        "bpq,bqf->bpf",
        band_tiles[:, 0],
        extended[0:block_count],
        preferred_element_type=jnp.float32,
    )
    for offset in range(1, 2 * HB + 1):
        total = total + jnp.einsum(
            "bpq,bqf->bpf",
            band_tiles[:, offset],
            extended[offset : offset + block_count],
            preferred_element_type=jnp.float32,
        )
    return total


def fetch_rim(values, block_rows):
    return with_halo(values, (("node", 0),), HB * block_rows)


def shards(
    inputs, conv_weight, conv_bias, tile_values, tile_cols, tile_count, cheb_weight, cheb_bias
):
    row_count, flat_width = inputs.shape
    chan_in = conv_weight.shape[1]
    chan_out = cheb_weight.shape[2]
    steps_dev = flat_width // chan_in
    pair_count = steps_dev // 2
    block_count, block_rows = (tile_values.shape[0], tile_values.shape[2])
    feat_width = steps_dev * chan_out
    earlier = passed_along(inputs, "tm", 1)
    widened = jnp.concatenate([earlier, inputs], axis=1).reshape(
        row_count, pair_count + 2, 2 * chan_in
    )
    pair_eye = jnp.eye(2, dtype=jnp.bfloat16)
    rows_in = jnp.arange(2 * chan_in, dtype=jnp.int32)[:, None]
    cols_out = jnp.arange(4 * chan_out, dtype=jnp.int32)[None, :]
    placement = (cols_out == rows_in // chan_in * (2 * chan_out) + rows_in % chan_in).astype(
        jnp.bfloat16
    )
    newest = widened[:, 2:].reshape(row_count * pair_count, 2 * chan_in)
    middle = widened[:, 1 : pair_count + 1].reshape(row_count * pair_count, 2 * chan_in)
    oldest = widened[:, :pair_count].reshape(row_count * pair_count, 2 * chan_in)
    mixed_out = jnp.dot(
        newest, jnp.kron(pair_eye, conv_weight[0]), preferred_element_type=jnp.float32
    )
    mixed_out = mixed_out + jnp.dot(
        middle, jnp.kron(pair_eye, conv_weight[1]), preferred_element_type=jnp.float32
    )
    mixed_out = mixed_out + jnp.dot(
        oldest, jnp.kron(pair_eye, conv_weight[2]), preferred_element_type=jnp.float32
    )
    carried = jnp.dot(newest, placement, preferred_element_type=jnp.float32)
    mixed_out = mixed_out.reshape(row_count, steps_dev, 2 * chan_out) + conv_bias
    carried = carried.reshape(row_count, steps_dev, 2 * chan_out)[..., :chan_out]
    linear = mixed_out[..., :chan_out] + carried
    features = (linear * jax.nn.sigmoid(mixed_out[..., chan_out:])).astype(jnp.bfloat16)
    flat_features = features.reshape(row_count, feat_width)
    first_block = lax.axis_index("node") * block_count

    def own_product(extended, band_tiles):
        return band_product(band_tiles, extended)

    band_tiles = build_band(tile_values, tile_cols, tile_count, first_block)
    extended = fetch_rim(flat_features, block_rows).reshape(
        block_count + 2 * HB, block_rows, feat_width
    )
    order_one = own_product(extended, band_tiles).astype(jnp.bfloat16)
    one_ext = fetch_rim(order_one.reshape(row_count, feat_width), block_rows).reshape(
        block_count + 2 * HB, block_rows, feat_width
    )
    order_two = own_product(one_ext, band_tiles)
    by_block = flat_features.reshape(block_count, block_rows, feat_width)
    cheb_two = (2.0 * order_two - by_block.astype(jnp.float32)).astype(jnp.bfloat16)
    result = jnp.dot(
        flat_features.reshape(row_count * steps_dev, chan_out),
        cheb_weight[0],
        preferred_element_type=jnp.float32,
    )
    result = result + jnp.dot(
        order_one.reshape(row_count * steps_dev, chan_out),
        cheb_weight[1],
        preferred_element_type=jnp.float32,
    )
    result = result + jnp.dot(
        cheb_two.reshape(row_count * steps_dev, chan_out),
        cheb_weight[2],
        preferred_element_type=jnp.float32,
    )
    result = result + cheb_bias
    return jax.nn.relu(result).astype(jnp.bfloat16).reshape(row_count, steps_dev, chan_out)


def solution(mesh):
    placed = (
        P("node", "tm"),
        P(),
        P(),
        P("node", None, None, None),
        P("node", None),
        P("node"),
        P(),
        P(),
    )
    return jax.shard_map(
        shards, mesh=mesh, in_specs=placed, out_specs=P("node", "tm", None), check_vma=False
    )
```

profile of v0, /device:TPU:128, one launch (start us, length us, event | category | flops | bytes accessed | tf_op | source)
XLA Modules:
  0.0 86.8 jit_solution(17174669756349299980)
XLA Ops:
  0.0 2.7 %collective-permute-start = (bf16[1024,256]{1,0:T(8,128)(2,1)}, bf16[1024,256]{1,0:T(8,128)(2,1)}, u32[]{:S(2)}, u32[]{:S(2)}) collective-permute-start(bf16[1024,256]{1,0:T(8,128)(2,1)} %param.8), channel_id=1, source_target_pairs={{0,32},{32,64},{64,96},{96,128},{128,160},{160,192},{192,224},{1,3... | collective-permute-start | bytes 1572872 | tf_op jit(solution)/shard_map/ppermute | solution.py:30
  5.4 1.3 %convolution_convert_fusion = bf16[8,5,128,128]{3,1,2,0:T(8,128)(2,1)S(1)} fusion(bf16[8,4,128,128]{3,2,1,0:T(8,128)(2,1)S(1)} %copy-done, s32[8,4]{1,0:T(8,128)S(1)} %copy.11, pred[8,4]{1,0:T(8,128)(4,1)S(1)} %iota_compare_fusion.3), kind=kOutput, calls=%fused_computation.15 | convolution fusion | flops 5898560 | bytes 2359456 | tf_op jit(solution)/shard_map/bjo,bjpq->bopq/dot_general | solution.py:41
  6.7 3.4 %fusion.56 = (bf16[8,1,128,128]{3,1,2,0:T(2,128)(2,1)}, bf16[8,1,128,128]{3,1,2,0:T(2,128)(2,1)}, bf16[8,1,128,128]{3,1,2,0:T(2,128)(2,1)}, bf16[8,1,128,128]{3,1,2,0:T(2,128)(2,1)S(1)}, bf16[8,1,128,128]{3,1,2,0:T(2,128)(2,1)S(1)}) fusion(bf16[8,5,128,128]{3,1,2,0:T(8,128)(2,1)S(1)} %convolution_convert_fusion), kind=kLoop, calls=%fused_computation.93 | loop fusion | bytes 2621440 | tf_op jit(solution)/shard_map/slice | solution.py:58
  10.2 1.5 %pad_maximum_fusion.2 = bf16[1024,512]{1,0:T(8,128)(2,1)S(1)} fusion(bf16[1024,256]{1,0:T(8,128)(2,1)S(1)} %copy-done.13, bf16[1024,256]{1,0:T(8,128)(2,1)} %collective-permute-done), kind=kLoop, calls=%fused_computation.26 | loop fusion | flops 2097152 | bytes 2097152 | tf_op jit(solution)/shard_map/concatenate | solution.py:80
  12.0 1.1 %fusion.61 = (bf16[1024,2,128]{2,1,0:T(2,128)(2,1)S(1)}, bf16[1024,2,128]{2,1,0:T(2,128)(2,1)S(1)}, bf16[1024,2,128]{2,1,0:T(2,128)(2,1)S(1)}) fusion(bf16[1024,4,128]{2,1,0:T(4,128)(2,1)S(1)} %reshape.188), kind=kLoop, calls=%fused_computation.98 | loop fusion | bytes 3145728 | tf_op jit(solution)/shard_map/slice | solution.py:91
  14.4 2.7 %add_add_fusion = f32[2048,512]{1,0:T(8,128)} fusion(f32[2048,512]{1,0:T(8,128)S(1)} %fusion.62, f32[2048,512]{1,0:T(8,128)S(1)} %fusion.63, bf16[2048,128]{1,0:T(8,128)(2,1)S(1)} %bitcast.117, bf16[128,512]{1,0:T(8,128)(2,1)S(1)} %bitcast.121), kind=kOutput, calls=%fused_computation.5 | convolution fusion | flops 270532608 | bytes 13238272 | tf_op jit(solution)/shard_map/dot_general | solution.py:98
  17.1 5.6 %reshape.192 = f32[1024,4,256]{2,1,0:T(4,128)} reshape(f32[2048,512]{1,0:T(8,128)} %add_add_fusion) | data formatting | bytes 8388608 | tf_op jit(solution)/shard_map/reshape | solution.py:102
  22.8 2.8 %fusion.30 = f32[2048,512]{1,0:T(8,128)} fusion(bf16[2048,128]{1,0:T(8,128)(2,1)S(1)} %bitcast.108, s32[128]{0:T(128)S(1)} %fusion.54), kind=kOutput, calls=%fused_computation.50 | convolution fusion | flops 268500992 | bytes 4719104 | tf_op jit(solution)/shard_map/dot_general | solution.py:101
  25.5 5.7 %reshape.193 = f32[1024,4,256]{2,1,0:T(4,128)} reshape(f32[2048,512]{1,0:T(8,128)} %fusion.30) | data formatting | bytes 8388608 | tf_op jit(solution)/shard_map/reshape | solution.py:103
  31.3 3.1 %broadcast_add_fusion = f32[1024,4,256]{2,1,0:T(4,128)S(1)} fusion(f32[1024,4,256]{2,1,0:T(4,128)} %reshape.192, f32[256]{0:T(256)S(1)} %copy-done.15), kind=kLoop, calls=%fused_computation.13 | loop fusion | flops 1048576 | bytes 8389632 | tf_op jit(solution)/shard_map/add | solution.py:102
  34.7 1.1 %fusion.5 = bf16[1024,4,128]{2,1,0:T(4,128)(2,1)S(1)} fusion(f32[1024,4,256]{2,1,0:T(4,128)S(1)} %broadcast_add_fusion, f32[1024,4,256]{2,1,0:T(4,128)S(1)} %copy-done.2), kind=kLoop, calls=%fused_computation.14 | loop fusion | flops 3145728 | bytes 7340032 | tf_op jit(solution)/shard_map/convert_element_type | solution.py:105
  37.2 1.0 %copy.72 = bf16[32,8,4,128]{3,1,2,0:T(8,128)(2,1)S(1)} copy(bf16[32,8,4,128]{3,2,1,0:T(4,128)(2,1)} %bitcast.120) | data formatting | bytes 524288
  38.2 4.2 %collective-permute-start.2 = (bf16[256,512]{1,0:T(8,128)(2,1)S(1)}, bf16[256,512]{1,0:T(8,128)(2,1)S(1)}, u32[]{:S(2)}, u32[]{:S(2)}) collective-permute-start(bf16[256,512]{1,0:T(8,128)(2,1)S(1)} %bitcast.127), channel_id=1, source_target_pairs={{1,0},{2,1},{3,2},{4,3},{5,4},{6,5},{7,6},{8,7},{9,8},{10,9},{11,1... | collective-permute-start | bytes 786440 | tf_op jit(solution)/shard_map/ppermute | solution.py:20
  42.4 2.1 %collective-permute-start.1 = (bf16[256,512]{1,0:T(8,128)(2,1)S(1)}, bf16[256,512]{1,0:T(8,128)(2,1)S(1)}, u32[]{:S(2)}, u32[]{:S(2)}) collective-permute-start(bf16[256,512]{1,0:T(8,128)(2,1)S(1)} %bitcast.128), channel_id=1, source_target_pairs={{0,1},{1,2},{2,3},{3,4},{4,5},{5,6},{6,7},{7,8},{8,9},{9,10},{10,1... | collective-permute-start | bytes 786440 | tf_op jit(solution)/shard_map/ppermute | solution.py:18
  44.5 1.5 %fusion.20 = f32[8,128,512]{2,1,0:T(8,128)S(1)} fusion(bf16[8,128,512]{2,1,0:T(8,128)(2,1)S(1)} %slice.161, bf16[8,1,128,128]{3,1,2,0:T(2,128)(2,1)} %get-tuple-element.7), kind=kOutput, calls=%fused_computation.39 | convolution fusion | flops 134217728 | bytes 3407872 | tf_op jit(solution)/shard_map/bpq,bqf->bpf/dot_general | solution.py:56
  46.0 1.8 %fusion.44 = f32[4096,128]{1,0:T(8,128)} fusion(bf16[4096,128]{1,0:T(8,128)(2,1)S(1)} %bitcast.104, bf16[3,128,128]{2,1,0:T(8,128)(2,1)S(1)} %copy-done.14), kind=kOutput, calls=%fused_computation.67 | convolution fusion | flops 134217728 | bytes 3178496 | tf_op jit(solution)/shard_map/dot_general | solution.py:123
  47.8 8.9 %collective-permute-done.1 = bf16[256,512]{1,0:T(8,128)(2,1)S(1)} collective-permute-done((bf16[256,512]{1,0:T(8,128)(2,1)S(1)}, bf16[256,512]{1,0:T(8,128)(2,1)S(1)}, u32[]{:S(2)}, u32[]{:S(2)}) %collective-permute-start.1) | collective-permute-done | bytes 262176 | tf_op jit(solution)/shard_map/ppermute | solution.py:18
  61.3 1.9 %collective-permute-start.4 = (bf16[256,512]{1,0:T(8,128)(2,1)}, bf16[256,512]{1,0:T(8,128)(2,1)S(1)}, u32[]{:S(2)}, u32[]{:S(2)}) collective-permute-start(bf16[256,512]{1,0:T(8,128)(2,1)} %bitcast.130), channel_id=1, source_target_pairs={{1,0},{2,1},{3,2},{4,3},{5,4},{6,5},{7,6},{8,7},{9,8},{10,9},{11,1... | collective-permute-start | bytes 786440 | tf_op jit(solution)/shard_map/ppermute | solution.py:20
  63.2 4.1 %collective-permute-start.3 = (bf16[256,512]{1,0:T(8,128)(2,1)S(1)}, bf16[256,512]{1,0:T(8,128)(2,1)S(1)}, u32[]{:S(2)}, u32[]{:S(2)}) collective-permute-start(bf16[256,512]{1,0:T(8,128)(2,1)S(1)} %bitcast.129), channel_id=1, source_target_pairs={{0,1},{1,2},{2,3},{3,4},{4,5},{5,6},{6,7},{7,8},{8,9},{9,10},{10,1... | collective-permute-start | bytes 786440 | tf_op jit(solution)/shard_map/ppermute | solution.py:18
  67.3 3.4 %convolution_add_fusion.1 = f32[4096,128]{1,0:T(8,128)} fusion(f32[4096,128]{1,0:T(8,128)} %fusion.44, bf16[4096,128]{1,0:T(8,128)(2,1)S(1)} %reshape.195, bf16[3,128,128]{2,1,0:T(8,128)(2,1)S(1)} %copy-done.14), kind=kOutput, calls=%fused_computation.3 | convolution fusion | flops 134742016 | bytes 5275648 | tf_op jit(solution)/shard_map/dot_general | solution.py:128
  71.5 5.2 %collective-permute-done.3 = bf16[256,512]{1,0:T(8,128)(2,1)S(1)} collective-permute-done((bf16[256,512]{1,0:T(8,128)(2,1)S(1)}, bf16[256,512]{1,0:T(8,128)(2,1)S(1)}, u32[]{:S(2)}, u32[]{:S(2)}) %collective-permute-start.3) | collective-permute-done | bytes 262176 | tf_op jit(solution)/shard_map/ppermute | solution.py:18
  79.7 1.8 %subtract_convert_fusion = bf16[8,128,512]{2,1,0:T(8,128)(2,1)} fusion(bf16[8,128,512]{2,1,0:T(8,128)(2,1)S(1)} %slice.161, f32[8,128,512]{2,1,0:T(8,128)S(1)} %fusion.14, f32[8,128,512]{2,1,0:T(8,128)S(1)} %fusion.18, f32[8,128,512]{2,1,0:T(8,128)S(1)} %fusion.26, f32[8,128,512]{2,1,0:T(8,128)S(1)} %fusion.22, bf16[8,128,512]{2,1,0:T(8,128)(2,1)S(1)} %bitcast.109, ...), kind=kOutput, calls=%fused_computation.11 | convolution fusion | flops 138412032 | bytes 11796480 | tf_op jit(solution)/shard_map/bpq,bqf->bpf/dot_general | solution.py:56
  81.5 2.6 %reshape.197 = bf16[4096,128]{1,0:T(8,128)(2,1)} reshape(bf16[8,128,512]{2,1,0:T(8,128)(2,1)} %subtract_convert_fusion) | data formatting | bytes 2097152 | tf_op jit(solution)/shard_map/reshape | solution.py:134
  84.1 2.6 %fusion.2 = bf16[4096,128]{1,0:T(8,128)(2,1)} fusion(f32[4096,128]{1,0:T(8,128)S(1)} %copy-done.3, bf16[4096,128]{1,0:T(8,128)(2,1)} %reshape.197, f32[128]{0:T(128)S(1)} %copy-done.16, bf16[3,128,128]{2,1,0:T(8,128)(2,1)S(1)} %copy-done.14), kind=kOutput, calls=%fused_computation.4 | convolution fusion | flops 136314880 | bytes 4227584 | tf_op jit(solution)/shard_map/dot_general | solution.py:133
  (70 shorter events, 14.5 us)
Async XLA Ops:
  0.0 5.4 %copy-start = (bf16[8,4,128,128]{3,2,1,0:T(8,128)(2,1)S(1)}, bf16[8,4,128,128]{3,2,1,0:T(8,128)(2,1)}, u32[]{:S(2)}) copy-start(bf16[8,4,128,128]{3,2,1,0:T(8,128)(2,1)} %param.11) | copy-start | bytes 3145732
  0.0 10.1 %collective-permute-start = (bf16[1024,256]{1,0:T(8,128)(2,1)}, bf16[1024,256]{1,0:T(8,128)(2,1)}, u32[]{:S(2)}, u32[]{:S(2)}) collective-permute-start(bf16[1024,256]{1,0:T(8,128)(2,1)} %param.8), channel_id=1, source_target_pairs={{0,32},{32,64},{64,96},{96,128},{128,160},{160,192},{192,224},{1,3... | collective-permute-start | bytes 1572872 | tf_op jit(solution)/shard_map/ppermute | solution.py:30
  6.7 3.4 %copy-start.13 = (bf16[1024,256]{1,0:T(8,128)(2,1)S(1)}, bf16[1024,256]{1,0:T(8,128)(2,1)}, u32[]{:S(2)}) copy-start(bf16[1024,256]{1,0:T(8,128)(2,1)} %param.8) | copy-start | bytes 1572868
  10.1 47.1 %copy-start.6 = (bf16[8,1,128,128]{3,1,2,0:T(2,128)(2,1)}, bf16[8,1,128,128]{3,1,2,0:T(2,128)(2,1)S(1)}, u32[]{:S(2)}) copy-start(bf16[8,1,128,128]{3,1,2,0:T(2,128)(2,1)S(1)} %get-tuple-element.9) | copy-start | bytes 786436
  10.1 47.6 %copy-start.4 = (bf16[8,1,128,128]{3,1,2,0:T(2,128)(2,1)}, bf16[8,1,128,128]{3,1,2,0:T(2,128)(2,1)S(1)}, u32[]{:S(2)}) copy-start(bf16[8,1,128,128]{3,1,2,0:T(2,128)(2,1)S(1)} %get-tuple-element.8) | copy-start | bytes 786436
  25.5 5.7 %copy-start.15 = (f32[256]{0:T(256)S(1)}, f32[256]{0:T(256)}, u32[]{:S(2)}) copy-start(f32[256]{0:T(256)} %param.10) | copy-start | bytes 3076
  31.3 3.4 %copy-start.2 = (f32[1024,4,256]{2,1,0:T(4,128)S(1)}, f32[1024,4,256]{2,1,0:T(4,128)}, u32[]{:S(2)}) copy-start(f32[1024,4,256]{2,1,0:T(4,128)} %reshape.193) | copy-start | bytes 12582916
  38.1 7.9 %copy-start.14 = (bf16[3,128,128]{2,1,0:T(8,128)(2,1)S(1)}, bf16[3,128,128]{2,1,0:T(8,128)(2,1)}, u32[]{:S(2)}) copy-start(bf16[3,128,128]{2,1,0:T(8,128)(2,1)} %param.14) | copy-start | bytes 294916
  38.2 18.9 %collective-permute-start.2 = (bf16[256,512]{1,0:T(8,128)(2,1)S(1)}, bf16[256,512]{1,0:T(8,128)(2,1)S(1)}, u32[]{:S(2)}, u32[]{:S(2)}) collective-permute-start(bf16[256,512]{1,0:T(8,128)(2,1)S(1)} %bitcast.127), channel_id=1, source_target_pairs={{1,0},{2,1},{3,2},{4,3},{5,4},{6,5},{7,6},{8,7},{9,8},{10,9},{11,1... | collective-permute-start | bytes 786440 | tf_op jit(solution)/shard_map/ppermute | solution.py:20
  42.4 14.2 %collective-permute-start.1 = (bf16[256,512]{1,0:T(8,128)(2,1)S(1)}, bf16[256,512]{1,0:T(8,128)(2,1)S(1)}, u32[]{:S(2)}, u32[]{:S(2)}) collective-permute-start(bf16[256,512]{1,0:T(8,128)(2,1)S(1)} %bitcast.128), channel_id=1, source_target_pairs={{0,1},{1,2},{2,3},{3,4},{4,5},{5,6},{6,7},{7,8},{8,9},{9,10},{10,1... | collective-permute-start | bytes 786440 | tf_op jit(solution)/shard_map/ppermute | solution.py:18
  57.7 1.0 %copy-start.8 = (bf16[8,1,128,128]{3,1,2,0:T(2,128)(2,1)S(1)}, bf16[8,1,128,128]{3,1,2,0:T(2,128)(2,1)}, u32[]{:S(2)}) copy-start(bf16[8,1,128,128]{3,1,2,0:T(2,128)(2,1)} %get-tuple-element.6) | copy-start | bytes 786436
  58.1 1.1 %copy-start.11 = (bf16[8,1,128,128]{3,1,2,0:T(2,128)(2,1)S(1)}, bf16[8,1,128,128]{3,1,2,0:T(2,128)(2,1)}, u32[]{:S(2)}) copy-start(bf16[8,1,128,128]{3,1,2,0:T(2,128)(2,1)} %get-tuple-element.5) | copy-start | bytes 786436
  61.3 10.3 %collective-permute-start.4 = (bf16[256,512]{1,0:T(8,128)(2,1)}, bf16[256,512]{1,0:T(8,128)(2,1)S(1)}, u32[]{:S(2)}, u32[]{:S(2)}) collective-permute-start(bf16[256,512]{1,0:T(8,128)(2,1)} %bitcast.130), channel_id=1, source_target_pairs={{1,0},{2,1},{3,2},{4,3},{5,4},{6,5},{7,6},{8,7},{9,8},{10,9},{11,1... | collective-permute-start | bytes 786440 | tf_op jit(solution)/shard_map/ppermute | solution.py:20
  63.2 7.4 %copy-start.10 = (bf16[8,1,128,128]{3,1,2,0:T(2,128)(2,1)S(1)}, bf16[8,1,128,128]{3,1,2,0:T(2,128)(2,1)}, u32[]{:S(2)}) copy-start(bf16[8,1,128,128]{3,1,2,0:T(2,128)(2,1)} %get-tuple-element.7) | copy-start | bytes 786436
  63.2 13.5 %collective-permute-start.3 = (bf16[256,512]{1,0:T(8,128)(2,1)S(1)}, bf16[256,512]{1,0:T(8,128)(2,1)S(1)}, u32[]{:S(2)}, u32[]{:S(2)}) collective-permute-start(bf16[256,512]{1,0:T(8,128)(2,1)S(1)} %bitcast.129), channel_id=1, source_target_pairs={{0,1},{1,2},{2,3},{3,4},{4,5},{5,6},{6,7},{7,8},{8,9},{9,10},{10,1... | collective-permute-start | bytes 786440 | tf_op jit(solution)/shard_map/ppermute | solution.py:18
  76.7 1.0 %copy-start.9 = (bf16[8,1,128,128]{3,1,2,0:T(2,128)(2,1)S(1)}, bf16[8,1,128,128]{3,1,2,0:T(2,128)(2,1)}, u32[]{:S(2)}) copy-start(bf16[8,1,128,128]{3,1,2,0:T(2,128)(2,1)} %get-tuple-element.6) | copy-start | bytes 786436
  77.0 1.2 %copy-start.7 = (bf16[8,1,128,128]{3,1,2,0:T(2,128)(2,1)S(1)}, bf16[8,1,128,128]{3,1,2,0:T(2,128)(2,1)}, u32[]{:S(2)}) copy-start(bf16[8,1,128,128]{3,1,2,0:T(2,128)(2,1)} %copy-done.6) | copy-start | bytes 786436
  78.2 1.0 %copy-start.5 = (bf16[8,1,128,128]{3,1,2,0:T(2,128)(2,1)S(1)}, bf16[8,1,128,128]{3,1,2,0:T(2,128)(2,1)}, u32[]{:S(2)}) copy-start(bf16[8,1,128,128]{3,1,2,0:T(2,128)(2,1)} %copy-done.4) | copy-start | bytes 786436
  78.6 1.1 %copy-start.12 = (bf16[8,1,128,128]{3,1,2,0:T(2,128)(2,1)S(1)}, bf16[8,1,128,128]{3,1,2,0:T(2,128)(2,1)}, u32[]{:S(2)}) copy-start(bf16[8,1,128,128]{3,1,2,0:T(2,128)(2,1)} %get-tuple-element.5) | copy-start | bytes 786436
  79.7 4.4 %copy-start.16 = (f32[128]{0:T(128)S(1)}, f32[128]{0:T(128)}, u32[]{:S(2)}) copy-start(f32[128]{0:T(128)} %param.15) | copy-start | bytes 1540
  81.5 2.6 %copy-start.3 = (f32[4096,128]{1,0:T(8,128)S(1)}, f32[4096,128]{1,0:T(8,128)}, u32[]{:S(2)}) copy-start(f32[4096,128]{1,0:T(8,128)} %convolution_add_fusion.1) | copy-start | bytes 6291460
  81.5 5.3 %copy-start.1 = (bf16[8,4,128,128]{3,2,1,0:T(8,128)(2,1)S(1)}, bf16[8,4,128,128]{3,2,1,0:T(8,128)(2,1)}, u32[]{:S(2)}) copy-start(bf16[8,4,128,128]{3,2,1,0:T(8,128)(2,1)} %param.11) | copy-start | bytes 3145732
where the time goes:
time: 87.5 us; the launch traced here: 86.8 us
  local copies, waits for them, and re-layouts  26.4 us (30%)
  matrix products  22.7 us (26%)
  starting transfers between devices  15 us (17%)
  waiting for transfers between devices  14.6 us (17%)
  other arithmetic  7.78 us (9%)
    ppermute x2, waiting for transfers between devices, with_halo(): lax.ppermute(tail, axis, [(i, (i + 1) % count) for i in range(ends)])  14.1 us
    ppermute x2, starting transfers between devices, with_halo(): lax.ppermute(tail, axis, [(i, (i + 1) % count) for i in range(ends)])  6.15 us
    ppermute x2, starting transfers between devices, with_halo(): lax.ppermute(head, axis, [((i + 1) % count, i) for i in range(ends)])  6.14 us
    dot_general x8, matrix products, band_product(): jnp.einsum('bpq,bqf->bpf', band_tiles[:, offset], extended[offset:offset...  5.98 us
    reshape x1, local copies, waits for them, and re-layouts, shards(): carried.reshape(row_count, steps_dev, 2 * chan_out)[..., :chan_out]  5.73 us
    reshape x1, local copies, waits for them, and re-layouts, shards(): mixed_out.reshape(row_count, steps_dev, 2 * chan_out) + conv_bias  5.6 us
    unnamed x40, local copies, waits for them, and re-layouts  3.57 us
    slice x1, local copies, waits for them, and re-layouts, band_product(): band_tiles[:, offset]  3.39 us
  transfers between devices with their start and end apart: 5, of which 3 were waited for; matrix products, arithmetic and copies ran while one was open for 17% of the time, Pallas kernels for 0%

commit v1 on v0

v1 whole, which is shorter than its diff:
```python
import jax
import jax.numpy as jnp
from jax import lax
from jax.sharding import PartitionSpec as P

HB = 2
TPB = 4


def with_halo(cells, sides, width):
    for axis, dim in sides:
        count = lax.axis_size(axis)
        ends = count - 1
        head = lax.slice_in_dim(cells, 0, width, axis=dim)
        tail = lax.slice_in_dim(cells, cells.shape[dim] - width, cells.shape[dim], axis=dim)
        cells = jnp.concatenate(
            [
                lax.ppermute(tail, axis, [(i, (i + 1) % count) for i in range(ends)]),
                cells,
                lax.ppermute(head, axis, [((i + 1) % count, i) for i in range(ends)]),
            ],
            axis=dim,
        )
    return cells


def passed_along(value, axis, by):
    length = lax.axis_size(axis)
    pairs = [(i, i + by) for i in range(length) if 0 <= i + by < length]
    return lax.ppermute(value, axis, pairs)


def build_band(tile_set, col_ids, live_count, first_block):
    block_count = tile_set.shape[0]
    row_ids = first_block + jnp.arange(block_count, dtype=jnp.int32)
    offset = col_ids - row_ids[:, None] + HB
    live_mask = jnp.arange(TPB, dtype=jnp.int32)[None, :] < live_count[:, None]
    one_hot = (
        offset[:, :, None] == jnp.arange(2 * HB + 1, dtype=jnp.int32)[None, None, :]
    ) & live_mask[:, :, None]
    band_tiles = jnp.einsum(
        "bjo,bjpq->bopq", one_hot.astype(jnp.bfloat16), tile_set, preferred_element_type=jnp.float32
    )
    return band_tiles.astype(jnp.bfloat16)


def band_product(band_tiles, extended):
    block_count = band_tiles.shape[0]
    total = jnp.einsum(
        "bpq,bqf->bpf",
        band_tiles[:, 0],
        extended[0:block_count],
        preferred_element_type=jnp.float32,
    )
    for offset in range(1, 2 * HB + 1):
        total = total + jnp.einsum(
            "bpq,bqf->bpf",
            band_tiles[:, offset],
            extended[offset : offset + block_count],
            preferred_element_type=jnp.float32,
        )
    return total


def fetch_rim(values, block_rows):
    return with_halo(values, (("node", 0),), HB * block_rows)


def pair_weight(conv_weight):
    taps, chan_in, width = conv_weight.shape
    eye = jnp.eye(2, dtype=conv_weight.dtype)
    blocks = [jnp.kron(eye, conv_weight[k]) for k in range(taps)]
    rows_in = jnp.arange(2 * chan_in, dtype=jnp.int32)[:, None]
    cols_out = jnp.arange(2 * width, dtype=jnp.int32)[None, :]
    place = (cols_out == rows_in // chan_in * width + rows_in % chan_in).astype(conv_weight.dtype)
    return jnp.concatenate(blocks + [place], axis=0)


def block_diag(weight, steps):
    return jnp.kron(jnp.eye(steps, dtype=weight.dtype), weight)


def shards(
    inputs, conv_weight, conv_bias, tile_values, tile_cols, tile_count, cheb_weight, cheb_bias
):
    row_count, flat_width = inputs.shape
    chan_in = conv_weight.shape[1]
    chan_out = cheb_weight.shape[2]
    steps_dev = flat_width // chan_in
    block_count, block_rows = (tile_values.shape[0], tile_values.shape[2])
    feat_width = steps_dev * chan_out
    earlier = passed_along(inputs, "tm", 1)
    window = jnp.concatenate([earlier, inputs], axis=1)
    wpair = pair_weight(conv_weight)
    pair_w = 2 * chan_in
    pieces = []
    for p in range(steps_dev // 2):
        base = steps_dev * chan_in + p * pair_w
        newest = window[:, base : base + pair_w]
        middle = window[:, base - pair_w : base]
        oldest = window[:, base - 2 * pair_w : base - pair_w]
        lhs = jnp.concatenate([newest, middle, oldest, newest], axis=1)
        mixed = jnp.dot(lhs, wpair, preferred_element_type=jnp.float32)
        for tt in range(2):
            lo = tt * 2 * chan_out
            linear = mixed[:, lo : lo + chan_out] + conv_bias[:chan_out]
            gate = mixed[:, lo + chan_out : lo + 2 * chan_out] + conv_bias[chan_out:]
            pieces.append(linear * jax.nn.sigmoid(gate))
    flat_features = jnp.concatenate(pieces, axis=1).astype(jnp.bfloat16)
    first_block = lax.axis_index("node") * block_count

    band_tiles = build_band(tile_values, tile_cols, tile_count, first_block)
    extended = fetch_rim(flat_features, block_rows).reshape(
        block_count + 2 * HB, block_rows, feat_width
    )
    order_one = band_product(band_tiles, extended).astype(jnp.bfloat16)
    one_ext = fetch_rim(order_one.reshape(row_count, feat_width), block_rows).reshape(
        block_count + 2 * HB, block_rows, feat_width
    )
    order_two = band_product(band_tiles, one_ext)
    by_block = flat_features.reshape(block_count, block_rows, feat_width)
    cheb_two = (2.0 * order_two - by_block.astype(jnp.float32)).astype(jnp.bfloat16)
    joined = jnp.concatenate(
        [flat_features, order_one.reshape(row_count, feat_width), cheb_two.reshape(row_count, feat_width)],
        axis=1,
    )
    wfinal = jnp.concatenate([block_diag(cheb_weight[k], steps_dev) for k in range(3)], axis=0)
    result = jnp.dot(joined, wfinal, preferred_element_type=jnp.float32)
    result = result + jnp.tile(cheb_bias, steps_dev)
    return jax.nn.relu(result).astype(jnp.bfloat16).reshape(row_count, steps_dev, chan_out)


def solution(mesh):
    placed = (
        P("node", "tm"),
        P(),
        P(),
        P("node", None, None, None),
        P("node", None),
        P("node"),
        P(),
        P(),
    )
    return jax.shard_map(
        shards, mesh=mesh, in_specs=placed, out_specs=P("node", "tm", None), check_vma=False
    )
```

time: 87.5 us -> 58 us (0.66)
  the two profiles are of different devices: /device:TPU:128 before, /device:TPU:110 now
where the time goes in v1:
time: 58 us; the launch traced here: 57.7 us
  waiting for transfers between devices  20.7 us (36%)
  starting transfers between devices  15 us (26%)
  matrix products  9.35 us (16%)
  local copies, waits for them, and re-layouts  6.86 us (12%)
  other arithmetic  5.44 us (9%)
    ppermute x2, waiting for transfers between devices, with_halo(): lax.ppermute(head, axis, [((i + 1) % count, i) for i in range(ends)])  12.7 us
    ppermute x2, starting transfers between devices, with_halo(): lax.ppermute(tail, axis, [(i, (i + 1) % count) for i in range(ends)])  6.87 us
    ppermute x2, waiting for transfers between devices, with_halo(): lax.ppermute(tail, axis, [(i, (i + 1) % count) for i in range(ends)])  6.86 us
    ppermute x2, starting transfers between devices, with_halo(): lax.ppermute(head, axis, [((i + 1) % count, i) for i in range(ends)])  6.02 us
    dot_general x8, matrix products, band_product(): jnp.einsum('bpq,bqf->bpf', band_tiles[:, offset], extended[offset:offset...  3.96 us
    concatenate x2, other arithmetic, with_halo(): jnp.concatenate([lax.ppermute(tail, axis, [(i, (i + 1) % count) for i in...  3.42 us
    slice x1, local copies, waits for them, and re-layouts, band_product(): band_tiles[:, offset]  2.65 us
    ppermute x1, starting transfers between devices, passed_along(): return lax.ppermute(value, axis, pairs)  2.05 us
  transfers between devices with their start and end apart: 5, of which 5 were waited for; matrix products, arithmetic and copies ran while one was open for 14% of the time, Pallas kernels for 0%

profile of v1, /device:TPU:110, one launch (start us, length us, event | category | flops | bytes accessed | tf_op | source)
XLA Modules:
  0.0 57.7 jit_solution(7097964536288935712)
XLA Ops:
  0.0 2.1 %collective-permute-start = (bf16[1024,256]{1,0:T(8,128)(2,1)}, bf16[1024,256]{1,0:T(8,128)(2,1)S(1)}, u32[]{:S(2)}, u32[]{:S(2)}) collective-permute-start(bf16[1024,256]{1,0:T(8,128)(2,1)} %param.8), channel_id=1, source_target_pairs={{0,32},{32,64},{64,96},{96,128},{128,160},{160,192},{192,224},{1,3... | collective-permute-start | bytes 1572872 | tf_op jit(solution)/shard_map/ppermute | solution.py:30
  2.1 1.1 %fusion.100 = (bf16[1024,128]{1,0:T(8,128)(2,1)S(1)}, bf16[1024,128]{1,0:T(8,128)(2,1)S(1)}) fusion(bf16[1024,256]{1,0:T(8,128)(2,1)} %param.8), kind=kLoop, calls=%fused_computation.153 | loop fusion | bytes 1048576 | tf_op jit(solution)/shard_map/slice | solution.py:99
  3.2 0.8 %slice_bitcast_fusion.5 = (bf16[64,256]{1,0:T(8,128)(2,1)S(1)}, bf16[64,256]{1,0:T(8,128)(2,1)S(1)}, bf16[64,256]{1,0:T(8,128)(2,1)S(1)}) fusion(bf16[3,64,256]{2,1,0:T(8,128)(2,1)} %param.9), kind=kLoop, calls=%fused_computation.119 | loop fusion | bytes 196608 | tf_op jit(solution)/shard_map/jit(kron)/mul | solution.py:72
  4.8 0.7 %broadcast_multiply_fusion.2 = (bf16[4,128,4,128]{3,2,1,0:T(4,128)(2,1)S(1)}, bf16[4,128,4,128]{3,2,1,0:T(4,128)(2,1)S(1)}, bf16[4,128,4,128]{3,2,1,0:T(4,128)(2,1)S(1)}) fusion(bf16[128,128]{1,0:T(8,128)(2,1)S(1)} %get-tuple-element.39, bf16[4,4]{1,0:T(4,128)(2,1)S(1)} %fusion.85, bf16[128,128]{1,0:T(8,128)(2,1)S(1)} %get-tuple-element.41, ...), kind=kLoop, calls=%fused_computation.98 | loop fusion | flops 786432 | bytes 1671200 | tf_op jit(solution)/shard_map/jit(kron)/mul | solution.py:80
  5.7 1.3 %convolution_convert_fusion = bf16[8,5,128,128]{3,1,2,0:T(8,128)(2,1)S(1)} fusion(bf16[8,4,128,128]{3,2,1,0:T(8,128)(2,1)S(1)} %copy-done, s32[8,4]{1,0:T(8,128)S(1)} %copy.12, pred[8,4]{1,0:T(8,128)(4,1)S(1)} %iota_compare_fusion.2), kind=kOutput, calls=%fused_computation.3 | convolution fusion | flops 5898560 | bytes 2359456 | tf_op jit(solution)/shard_map/bjo,bjpq->bopq/dot_general | solution.py:41
  7.0 2.6 %fusion.96 = (bf16[8,1,128,128]{3,1,2,0:T(2,128)(2,1)S(1)}, bf16[8,1,128,128]{3,1,2,0:T(2,128)(2,1)S(1)}, bf16[8,1,128,128]{3,1,2,0:T(2,128)(2,1)S(1)}, bf16[8,1...) fusion(bf16[8,5,128,128]{3,1,2,0:T(8,128)(2,1)S(1)} %convolution_convert_fusion), kind=kLoop, calls=%fused_computation.149 | loop fusion | bytes 2621440 | tf_op jit(solution)/shard_map/slice | solution.py:58
  9.7 1.2 %collective-permute-done = bf16[1024,256]{1,0:T(8,128)(2,1)S(1)} collective-permute-done((bf16[1024,256]{1,0:T(8,128)(2,1)}, bf16[1024,256]{1,0:T(8,128)(2,1)S(1)}, u32[]{:S(2)}, u32[]{:S(2)}) %collective-permute-start) | collective-permute-done | bytes 524320 | tf_op jit(solution)/shard_map/ppermute | solution.py:30
  10.9 0.7 %fusion.10 = f32[1024,512]{1,0:T(8,128)S(1)} fusion(bf16[1024,128]{1,0:T(8,128)(2,1)S(1)} %get-tuple-element.36, bf16[1024,128]{1,0:T(8,128)(2,1)S(1)} %get-tuple-element.38, bf16[1024,128]{1,0:T(8,128)(2,1)S(1)} %get-tuple-element.37, bf16[128,512]{1,0:T(8,128)(2,1)S(1)} %fusion.69, bf16[128,512]{1,0:T(8,128)(2,1)S(1)} %bitcast.125, ...), kind=kOutput, calls=%fused_computation.20 | convolution fusion | flops 543162368 | bytes 3407872 | tf_op jit(solution)/shard_map/dot_general | solution.py:103
  12.0 0.7 %fusion.18 = f32[1024,512]{1,0:T(8,128)S(1)} fusion(bf16[1024,128]{1,0:T(8,128)(2,1)S(1)} %get-tuple-element.35, bf16[1024,128]{1,0:T(8,128)(2,1)S(1)} %get-tuple-element.37, bf16[1024,128]{1,0:T(8,128)(2,1)S(1)} %get-tuple-element.36, bf16[128,512]{1,0:T(8,128)(2,1)S(1)} %fusion.69, bf16[128,512]{1,0:T(8,128)(2,1)S(1)} %bitcast.126, ...), kind=kOutput, calls=%fused_computation.28 | convolution fusion | flops 543162368 | bytes 3407872 | tf_op jit(solution)/shard_map/dot_general | solution.py:103
  13.1 5.0 %collective-permute-start.1 = (bf16[256,512]{1,0:T(8,128)(2,1)S(1)}, bf16[256,512]{1,0:T(8,128)(2,1)S(1)}, u32[]{:S(2)}, u32[]{:S(2)}) collective-permute-start(bf16[256,512]{1,0:T(8,128)(2,1)S(1)} %get-tuple-element.33), channel_id=1, source_target_pairs={{0,1},{1,2},{2,3},{3,4},{4,5},{5,6},{6,7},{7,8},{8,9},{9,10},{10,1... | collective-permute-start | bytes 786440 | tf_op jit(solution)/shard_map/ppermute | solution.py:18
  18.1 1.9 %collective-permute-start.2 = (bf16[256,512]{1,0:T(8,128)(2,1)S(1)}, bf16[256,512]{1,0:T(8,128)(2,1)S(1)}, u32[]{:S(2)}, u32[]{:S(2)}) collective-permute-start(bf16[256,512]{1,0:T(8,128)(2,1)S(1)} %get-tuple-element.34), channel_id=1, source_target_pairs={{1,0},{2,1},{3,2},{4,3},{5,4},{6,5},{7,6},{8,7},{9,8},{10,9},{11,1... | collective-permute-start | bytes 786440 | tf_op jit(solution)/shard_map/ppermute | solution.py:20
  20.4 3.9 %collective-permute-done.1 = bf16[256,512]{1,0:T(8,128)(2,1)S(1)} collective-permute-done((bf16[256,512]{1,0:T(8,128)(2,1)S(1)}, bf16[256,512]{1,0:T(8,128)(2,1)S(1)}, u32[]{:S(2)}, u32[]{:S(2)}) %collective-permute-start.1) | collective-permute-done | bytes 262176 | tf_op jit(solution)/shard_map/ppermute | solution.py:18
  24.3 7.4 %collective-permute-done.2 = bf16[256,512]{1,0:T(8,128)(2,1)S(1)} collective-permute-done((bf16[256,512]{1,0:T(8,128)(2,1)S(1)}, bf16[256,512]{1,0:T(8,128)(2,1)S(1)}, u32[]{:S(2)}, u32[]{:S(2)}) %collective-permute-start.2) | collective-permute-done | bytes 262176 | tf_op jit(solution)/shard_map/ppermute | solution.py:20
  31.7 2.9 %maximum_maximum_fusion = (bf16[1280,512]{1,0:T(8,128)(2,1)S(1)}, bf16[1280,512]{1,0:T(8,128)(2,1)S(1)}) fusion(bf16[1024,128]{1,0:T(8,128)(2,1)S(1)} %get-tuple-element.6, bf16[1024,128]{1,0:T(8,128)(2,1)S(1)} %get-tuple-element.8, bf16[1024,128]{1,0:T(8,128)(2,1)S(1)} %get-tuple-element.10, bf16[1024,128]{1,0:T(8,128)(2,1)S(1)} %get-tuple-element.12, ...), kind=kLoop, calls=%fused_computation.10 | loop fusion | flops 13107200 | bytes 4194304 | tf_op jit(solution)/shard_map/concatenate | solution.py:16
  35.0 0.4 fusion.55
  36.3 0.7 %add_convert_fusion = bf16[8,128,512]{2,1,0:T(8,128)(2,1)S(1)} fusion(f32[8,128,512]{2,1,0:T(8,128)S(1)} %fusion.55, f32[8,128,512]{2,1,0:T(8,128)S(1)} %fusion.59, f32[8,128,512]{2,1,0:T(8,128)S(1)} %fusion.67, f32[8,128,512]{2,1,0:T(8,128)S(1)} %fusion.63, bf16[8,128,512]{2,1,0:T(8,128)(2,1)S(1)} %bitcast.110, ...), kind=kOutput, calls=%fused_computation.2 | convolution fusion | flops 136839168 | bytes 10747904 | tf_op jit(solution)/shard_map/bpq,bqf->bpf/dot_general | solution.py:56
  37.0 1.9 %collective-permute-start.3 = (bf16[256,512]{1,0:T(8,128)(2,1)S(1)}, bf16[256,512]{1,0:T(8,128)(2,1)S(1)}, u32[]{:S(2)}, u32[]{:S(2)}) collective-permute-start(bf16[256,512]{1,0:T(8,128)(2,1)S(1)} %bitcast.120), channel_id=1, source_target_pairs={{0,1},{1,2},{2,3},{3,4},{4,5},{5,6},{6,7},{7,8},{8,9},{9,10},{10,1... | collective-permute-start | bytes 786440 | tf_op jit(solution)/shard_map/ppermute | solution.py:18
  38.9 4.1 %collective-permute-start.4 = (bf16[256,512]{1,0:T(8,128)(2,1)S(1)}, bf16[256,512]{1,0:T(8,128)(2,1)S(1)}, u32[]{:S(2)}, u32[]{:S(2)}) collective-permute-start(bf16[256,512]{1,0:T(8,128)(2,1)S(1)} %bitcast.119), channel_id=1, source_target_pairs={{1,0},{2,1},{3,2},{4,3},{5,4},{6,5},{7,6},{8,7},{9,8},{10,9},{11,1... | collective-permute-start | bytes 786440 | tf_op jit(solution)/shard_map/ppermute | solution.py:20
  43.4 3.0 %collective-permute-done.3 = bf16[256,512]{1,0:T(8,128)(2,1)S(1)} collective-permute-done((bf16[256,512]{1,0:T(8,128)(2,1)S(1)}, bf16[256,512]{1,0:T(8,128)(2,1)S(1)}, u32[]{:S(2)}, u32[]{:S(2)}) %collective-permute-start.3) | collective-permute-done | bytes 262176 | tf_op jit(solution)/shard_map/ppermute | solution.py:18
  46.5 5.2 %collective-permute-done.4 = bf16[256,512]{1,0:T(8,128)(2,1)S(1)} collective-permute-done((bf16[256,512]{1,0:T(8,128)(2,1)S(1)}, bf16[256,512]{1,0:T(8,128)(2,1)S(1)}, u32[]{:S(2)}, u32[]{:S(2)}) %collective-permute-start.4) | collective-permute-done | bytes 262176 | tf_op jit(solution)/shard_map/ppermute | solution.py:20
  51.7 0.6 pad_maximum_fusion.1
  53.5 0.7 %subtract_convert_fusion = bf16[8,128,512]{2,1,0:T(8,128)(2,1)S(1)} fusion(f32[8,128,512]{2,1,0:T(8,128)S(1)} %fusion.53, f32[8,128,512]{2,1,0:T(8,128)S(1)} %fusion.57, f32[8,128,512]{2,1,0:T(8,128)S(1)} %fusion.65, f32[8,128,512]{2,1,0:T(8,128)S(1)} %fusion.61, bf16[8,128,512]{2,1,0:T(8,128)(2,1)S(1)} %bitcast.95, bf16[8,128,128]{2,1,0:T(8,128)(2,1)S(1)} %bitcast.103, ...), kind=kOutput, calls=%fused_computation.1 | convolution fusion | flops 142082048 | bytes 11796480 | tf_op jit(solution)/shard_map/bpq,bqf->bpf/dot_general | solution.py:56
  54.4 1.9 %maximum_convert_fusion = bf16[1024,512]{0,1:T(8,128)(2,1)S(1)} fusion(bf16[1024,1536]{1,0:T(8,128)(2,1)S(1)} %constant_dynamic-update-slice_fusion, bf16[512,512]{1,0:T(8,128)(2,1)S(1)} %get-tuple-element.55, bf16[512,512]{1,0:T(8,128)(2,1)S(1)} %get-tuple-element.56, bf16[512,512]{1,0:T(8,128)(2,1)S(1)} %bitcast.118, f32[512]{0:T(512)S(1)} %broadcast_bitcast_fusion), kind=kOutput, calls=%fused_computation | convolution fusion | flops 1616904192 | bytes 5769216 | tf_op jit(solution)/shard_map/dot_general | solution.py:128
  56.2 1.4 %copy.14 = bf16[1024,4,128]{2,1,0:T(4,128)(2,1)} copy(bf16[1024,4,128]{0,2,1:T(8,128)(2,1)S(1)} %bitcast.114) | data formatting | bytes 2097152 | tf_op jit(solution)/shard_map/reshape | solution.py:130
  (45 shorter events, 5.2 us)
Async XLA Ops:
  0.0 5.7 %copy-start = (bf16[8,4,128,128]{3,2,1,0:T(8,128)(2,1)S(1)}, bf16[8,4,128,128]{3,2,1,0:T(8,128)(2,1)}, u32[]{:S(2)}) copy-start(bf16[8,4,128,128]{3,2,1,0:T(8,128)(2,1)} %param.11) | copy-start | bytes 3145732
  0.0 4.6 %copy-start.3 = (f32[256]{0:T(256)S(1)}, f32[256]{0:T(256)}, u32[]{:S(2)}) copy-start(f32[256]{0:T(256)} %param.10) | copy-start | bytes 3076
  0.0 4.6 %copy-start.2 = (s32[8,4]{0,1:T(4,128)S(1)}, s32[8,4]{0,1:T(4,128)}, u32[]{:S(2)}) copy-start(s32[8,4]{0,1:T(4,128)} %param.12) | copy-start | bytes 388
  0.0 4.7 %copy-start.5 = (s32[8]{0:T(128)S(1)}, s32[8]{0:T(128)}, u32[]{:S(2)}) copy-start(s32[8]{0:T(128)} %param.13) | copy-start | bytes 100
  0.0 4.8 %copy-start.1 = (bf16[3,128,128]{2,1,0:T(8,128)(2,1)S(1)}, bf16[3,128,128]{2,1,0:T(8,128)(2,1)}, u32[]{:S(2)}) copy-start(bf16[3,128,128]{2,1,0:T(8,128)(2,1)} %param.14) | copy-start | bytes 294916
  0.0 10.8 %collective-permute-start = (bf16[1024,256]{1,0:T(8,128)(2,1)}, bf16[1024,256]{1,0:T(8,128)(2,1)S(1)}, u32[]{:S(2)}, u32[]{:S(2)}) collective-permute-start(bf16[1024,256]{1,0:T(8,128)(2,1)} %param.8), channel_id=1, source_target_pairs={{0,32},{32,64},{64,96},{96,128},{128,160},{160,192},{192,224},{1,3... | collective-permute-start | bytes 1572872 | tf_op jit(solution)/shard_map/ppermute | solution.py:30
  4.0 1.5 %copy-start.4 = (f32[128]{0:T(128)S(1)}, f32[128]{0:T(128)}, u32[]{:S(2)}) copy-start(f32[128]{0:T(128)} %param.15) | copy-start | bytes 1540
  13.1 11.2 %collective-permute-start.1 = (bf16[256,512]{1,0:T(8,128)(2,1)S(1)}, bf16[256,512]{1,0:T(8,128)(2,1)S(1)}, u32[]{:S(2)}, u32[]{:S(2)}) collective-permute-start(bf16[256,512]{1,0:T(8,128)(2,1)S(1)} %get-tuple-element.33), channel_id=1, source_target_pairs={{0,1},{1,2},{2,3},{3,4},{4,5},{5,6},{6,7},{7,8},{8,9},{9,10},{10,1... | collective-permute-start | bytes 786440 | tf_op jit(solution)/shard_map/ppermute | solution.py:18
  18.1 13.6 %collective-permute-start.2 = (bf16[256,512]{1,0:T(8,128)(2,1)S(1)}, bf16[256,512]{1,0:T(8,128)(2,1)S(1)}, u32[]{:S(2)}, u32[]{:S(2)}) collective-permute-start(bf16[256,512]{1,0:T(8,128)(2,1)S(1)} %get-tuple-element.34), channel_id=1, source_target_pairs={{1,0},{2,1},{3,2},{4,3},{5,4},{6,5},{7,6},{8,7},{9,8},{10,9},{11,1... | collective-permute-start | bytes 786440 | tf_op jit(solution)/shard_map/ppermute | solution.py:20
  37.0 9.5 %collective-permute-start.3 = (bf16[256,512]{1,0:T(8,128)(2,1)S(1)}, bf16[256,512]{1,0:T(8,128)(2,1)S(1)}, u32[]{:S(2)}, u32[]{:S(2)}) collective-permute-start(bf16[256,512]{1,0:T(8,128)(2,1)S(1)} %bitcast.120), channel_id=1, source_target_pairs={{0,1},{1,2},{2,3},{3,4},{4,5},{5,6},{6,7},{7,8},{8,9},{9,10},{10,1... | collective-permute-start | bytes 786440 | tf_op jit(solution)/shard_map/ppermute | solution.py:18
  38.9 12.8 %collective-permute-start.4 = (bf16[256,512]{1,0:T(8,128)(2,1)S(1)}, bf16[256,512]{1,0:T(8,128)(2,1)S(1)}, u32[]{:S(2)}, u32[]{:S(2)}) collective-permute-start(bf16[256,512]{1,0:T(8,128)(2,1)S(1)} %bitcast.119), channel_id=1, source_target_pairs={{1,0},{2,1},{3,2},{4,3},{5,4},{6,5},{7,6},{8,7},{9,8},{10,9},{11,1... | collective-permute-start | bytes 786440 | tf_op jit(solution)/shard_map/ppermute | solution.py:20

commit v2 on v1

--- a/solution.py
+++ b/solution.py
@@ -89,8 +89,33 @@
     steps_dev = flat_width // chan_in
     block_count, block_rows = (tile_values.shape[0], tile_values.shape[2])
     feat_width = steps_dev * chan_out
-    earlier = passed_along(inputs, "tm", 1)
-    window = jnp.concatenate([earlier, inputs], axis=1)
+    node = lax.axis_index("node")
+    node_count = lax.axis_size("node")
+    tm_count = lax.axis_size("tm")
+    first_block = node * block_count
+    rim = HB * block_rows
+    head = inputs[:rim]
+    tail = inputs[row_count - rim :]
+    to_right = [(i, i + 1) for i in range(node_count - 1)]
+    to_left = [(i + 1, i) for i in range(node_count - 1)]
+    diag_right = [
+        (j * node_count + i, (j + 1) * node_count + i + 1)
+        for i in range(node_count - 1)
+        for j in range(tm_count - 1)
+    ]
+    diag_left = [
+        (j * node_count + i + 1, (j + 1) * node_count + i)
+        for i in range(node_count - 1)
+        for j in range(tm_count - 1)
+    ]
+    cur_left = lax.ppermute(tail, "node", to_right)
+    cur_right = lax.ppermute(head, "node", to_left)
+    prev_own = passed_along(inputs, "tm", 1)
+    prev_left = lax.ppermute(tail, ("tm", "node"), diag_right)
+    prev_right = lax.ppermute(head, ("tm", "node"), diag_left)
+    cur_ext = jnp.concatenate([cur_left, inputs, cur_right], axis=0)
+    prev_ext = jnp.concatenate([prev_left, prev_own, prev_right], axis=0)
+    window = jnp.concatenate([prev_ext, cur_ext], axis=1)
     wpair = pair_weight(conv_weight)
     pair_w = 2 * chan_in
     pieces = []
@@ -106,13 +131,14 @@
             linear = mixed[:, lo : lo + chan_out] + conv_bias[:chan_out]
             gate = mixed[:, lo + chan_out : lo + 2 * chan_out] + conv_bias[chan_out:]
             pieces.append(linear * jax.nn.sigmoid(gate))
-    flat_features = jnp.concatenate(pieces, axis=1).astype(jnp.bfloat16)
-    first_block = lax.axis_index("node") * block_count
+    ext_rows = row_count + 2 * rim
+    ext_block = first_block - HB + jnp.arange(ext_rows, dtype=jnp.int32) // block_rows
+    inside = (ext_block >= 0) & (ext_block < node_count * block_count)
+    feat_ext = jnp.where(inside[:, None], jnp.concatenate(pieces, axis=1), 0.0).astype(jnp.bfloat16)
+    flat_features = feat_ext[rim : rim + row_count]
 
     band_tiles = build_band(tile_values, tile_cols, tile_count, first_block)
-    extended = fetch_rim(flat_features, block_rows).reshape(
-        block_count + 2 * HB, block_rows, feat_width
-    )
+    extended = feat_ext.reshape(block_count + 2 * HB, block_rows, feat_width)
     order_one = band_product(band_tiles, extended).astype(jnp.bfloat16)
     one_ext = fetch_rim(order_one.reshape(row_count, feat_width), block_rows).reshape(
         block_count + 2 * HB, block_rows, feat_width

time: 58 us -> 102 us (1.76)
  local copies, waits for them, and re-layouts: 6.86 us -> 31.3 us
  matrix products: 9.35 us -> 28.6 us
  waiting for transfers between devices: 20.7 us -> 8.68 us
  starting transfers between devices: 15 us -> 24.8 us
  other arithmetic: 5.44 us -> 7.07 us
    ppermute x0 -> x4, starting transfers between devices: none -> 14 us  [the longest x1 6.24 us: shards(): prev_left = lax.ppermute(tail, ('tm', 'node'), diag_right)]
    dot_general x8, matrix products: 3.96 us -> 17.4 us  [band_product(): jnp.einsum('bpq,bqf->bpf', band_tiles[:, offset], extended[offset:offset...]
    slice x1 -> x8, local copies, waits for them, and re-layouts: 0.35 us -> 12.8 us  [band_product(): extended[offset:offset + block_count]]
    ppermute x2 -> x1, waiting for transfers between devices: 6.86 us -> 0.19 us  [with_halo(): lax.ppermute(tail, axis, [(i, (i + 1) % count) for i in range(ends)])]
    ppermute x2 -> x1, waiting for transfers between devices: 12.7 us -> 8.48 us  [with_halo(): lax.ppermute(head, axis, [((i + 1) % count, i) for i in range(ends)])]
    ppermute x2 -> x1, starting transfers between devices: 6.02 us -> 2.09 us  [with_halo(): lax.ppermute(head, axis, [((i + 1) % count, i) for i in range(ends)])]
    slice x1 -> x5, local copies, waits for them, and re-layouts: 0.04 us -> 3.73 us  [the longest x2 1.85 us: band_product(): extended[0:block_count]]
    reshape x0 -> x2, local copies, waits for them, and re-layouts: none -> 2.99 us  [the longest x1 2.46 us: shards(): cheb_two.reshape(row_count, feat_width)]
  transfers between devices with their start and end apart: 5 -> 7, of which waited for: 5 -> 2; matrix products, arithmetic and copies ran while one was open for 14% -> 16% of each run, Pallas kernels for 0% -> 0%
where the time goes in v2:
time: 102 us; the launch traced here: 101 us
  local copies, waits for them, and re-layouts  31.3 us (31%)
  matrix products  28.6 us (28%)
  starting transfers between devices  24.8 us (24%)
  waiting for transfers between devices  8.68 us (9%)
  other arithmetic  7.07 us (7%)
    dot_general x8, matrix products, band_product(): jnp.einsum('bpq,bqf->bpf', band_tiles[:, offset], extended[offset:offset...  17.4 us
    slice x8, local copies, waits for them, and re-layouts, band_product(): extended[offset:offset + block_count]  12.8 us
    ppermute x1, waiting for transfers between devices, with_halo(): lax.ppermute(head, axis, [((i + 1) % count, i) for i in range(ends)])  8.48 us
    ppermute x1, starting transfers between devices, with_halo(): lax.ppermute(tail, axis, [(i, (i + 1) % count) for i in range(ends)])  6.71 us
    ppermute x1, starting transfers between devices, shards(): prev_left = lax.ppermute(tail, ('tm', 'node'), diag_right)  6.24 us
    dot_general x1, matrix products, shards(): result = jnp.dot(joined, wfinal, preferred_element_type=jnp.float32)  4.58 us
    slice x1, local copies, waits for them, and re-layouts, band_product(): band_tiles[:, offset]  3.41 us
    ppermute x1, starting transfers between devices, shards(): cur_left = lax.ppermute(tail, 'node', to_right)  3.4 us
  transfers between devices with their start and end apart: 7, of which 2 were waited for; matrix products, arithmetic and copies ran while one was open for 16% of the time, Pallas kernels for 0%

profile of v2, /device:TPU:110, one launch (start us, length us, event | category | flops | bytes accessed | tf_op | source)
XLA Modules:
  0.0 101.1 jit_solution(12548873697198004324)
XLA Ops:
  0.0 2.0 %collective-permute-start.3 = (bf16[1024,256]{1,0:T(8,128)(2,1)}, bf16[1024,256]{1,0:T(8,128)(2,1)S(1)}, u32[]{:S(2)}, u32[]{:S(2)}) collective-permute-start(bf16[1024,256]{1,0:T(8,128)(2,1)} %param.8), channel_id=1, source_target_pairs={{0,32},{32,64},{64,96},{96,128},{128,160},{160,192},{192,224},{1,3... | collective-permute-start | bytes 1572872 | tf_op jit(solution)/shard_map/ppermute | solution.py:30
  3.0 6.2 %collective-permute-start.2 = (bf16[256,256]{1,0:T(8,128)(2,1)S(1)}, bf16[256,256]{1,0:T(8,128)(2,1)S(1)}, u32[]{:S(2)}, u32[]{:S(2)}) collective-permute-start(bf16[256,256]{1,0:T(8,128)(2,1)S(1)} %get-tuple-element.32), channel_id=1, source_target_pairs={{0,33},{32,65},{64,97},{96,129},{128,161},{160,193},{192,225},{1,3... | collective-permute-start | bytes 393224 | tf_op jit(solution)/shard_map/ppermute | solution.py:114
  9.3 3.4 %collective-permute-start = (bf16[256,256]{1,0:T(8,128)(2,1)S(1)}, bf16[256,256]{1,0:T(8,128)(2,1)S(1)}, u32[]{:S(2)}, u32[]{:S(2)}) collective-permute-start(bf16[256,256]{1,0:T(8,128)(2,1)S(1)} %get-tuple-element.32), channel_id=1, source_target_pairs={{0,1},{1,2},{2,3},{3,4},{4,5},{5,6},{6,7},{7,8},{8,9},{9,10},{10,1... | collective-permute-start | bytes 393224 | tf_op jit(solution)/shard_map/ppermute | solution.py:111
  12.7 1.9 %collective-permute-start.4 = (bf16[256,256]{1,0:T(8,128)(2,1)S(1)}, bf16[256,256]{1,0:T(8,128)(2,1)S(1)}, u32[]{:S(2)}, u32[]{:S(2)}) collective-permute-start(bf16[256,256]{1,0:T(8,128)(2,1)S(1)} %get-tuple-element.31), channel_id=1, source_target_pairs={{1,32},{33,64},{65,96},{97,128},{129,160},{161,192},{193,224},{2,3... | collective-permute-start | bytes 393224 | tf_op jit(solution)/shard_map/ppermute | solution.py:115
  14.6 2.4 %collective-permute-start.1 = (bf16[256,256]{1,0:T(8,128)(2,1)S(1)}, bf16[256,256]{1,0:T(8,128)(2,1)S(1)}, u32[]{:S(2)}, u32[]{:S(2)}) collective-permute-start(bf16[256,256]{1,0:T(8,128)(2,1)S(1)} %get-tuple-element.31), channel_id=1, source_target_pairs={{1,0},{2,1},{3,2},{4,3},{5,4},{6,5},{7,6},{8,7},{9,8},{10,9},{11,1... | collective-permute-start | bytes 393224 | tf_op jit(solution)/shard_map/ppermute | solution.py:112
  20.8 3.4 %fusion.102 = (bf16[8,1,128,128]{3,1,2,0:T(2,128)(2,1)}, bf16[8,1,128,128]{3,1,2,0:T(2,128)(2,1)}, bf16[8,1,128,128]{3,1,2,0:T(2,128)(2,1)}, bf16[8,1,128,128]{3,1,2,0:T(2,128)(2,1)}, bf16[8,1,128,128]{3,1,2,0:T(2,128)(2,1)}) fusion(bf16[8,5,128,128]{3,1,2,0:T(8,128)(2,1)S(1)} %convolution_convert_fusion), kind=kLoop, calls=%fused_computation.155 | loop fusion | bytes 2621440 | tf_op jit(solution)/shard_map/slice | solution.py:58
  31.5 2.1 %fusion.103 = (bf16[1024,512]{0,1:T(8,128)(2,1)S(1)}, bf16[1024,512]{0,1:T(8,128)(2,1)S(1)}, bf16[1024,512]{0,1:T(8,128)(2,1)}, bf16[1024,512]{0,1:T(8,128)(2,1)}, bf16[1024,512]{0,1:T(8,128)(2,1)S(1)}) fusion(bf16[1536,512]{0,1:T(8,128)(2,1)S(1)} %fusion), kind=kLoop, calls=%fused_computation.156 | loop fusion | bytes 10485760 | tf_op jit(solution)/shard_map/slice | solution.py:59
  35.5 2.4 %copy.45 = bf16[1024,512]{1,0:T(8,128)(2,1)} copy(bf16[1024,512]{0,1:T(8,128)(2,1)} %get-tuple-element.16) | data formatting | bytes 2097152 | tf_op jit(solution)/shard_map/slice | solution.py:59
  39.2 1.4 %copy.47 = bf16[1024,512]{1,0:T(8,128)(2,1)} copy(bf16[1024,512]{0,1:T(8,128)(2,1)S(1)} %get-tuple-element.14) | data formatting | bytes 2097152 | tf_op jit(solution)/shard_map/slice | solution.py:59
  40.5 1.5 %fusion.59 = f32[8,128,512]{2,1,0:T(8,128)S(1)} fusion(bf16[8,128,512]{2,1,0:T(8,128)(2,1)S(1)} %bitcast.95, bf16[8,1,128,128]{3,1,2,0:T(2,128)(2,1)} %get-tuple-element.10), kind=kOutput, calls=%fused_computation.78 | convolution fusion | flops 134217728 | bytes 3407872 | tf_op jit(solution)/shard_map/bpq,bqf->bpf/dot_general | solution.py:56
  46.8 6.7 %collective-permute-start.5 = (bf16[256,512]{0,1:T(8,128)(2,1)}, bf16[256,512]{0,1:T(8,128)(2,1)S(1)}, u32[]{:S(2)}, u32[]{:S(2)}) collective-permute-start(bf16[256,512]{0,1:T(8,128)(2,1)} %copy.49), channel_id=1, source_target_pairs={{0,1},{1,2},{2,3},{3,4},{4,5},{5,6},{6,7},{7,8},{8,9},{9,10},{10,1... | collective-permute-start | bytes 786440 | tf_op jit(solution)/shard_map/ppermute | solution.py:18
  54.3 2.1 %collective-permute-start.6 = (bf16[256,512]{0,1:T(8,128)(2,1)}, bf16[256,512]{0,1:T(8,128)(2,1)}, u32[]{:S(2)}, u32[]{:S(2)}) collective-permute-start(bf16[256,512]{0,1:T(8,128)(2,1)} %copy.52), channel_id=1, source_target_pairs={{1,0},{2,1},{3,2},{4,3},{5,4},{6,5},{7,6},{8,7},{9,8},{10,9},{11,1... | collective-permute-start | bytes 786440 | tf_op jit(solution)/shard_map/ppermute | solution.py:20
  57.0 3.2 %fusion.61 = f32[8,128,512]{2,1,0:T(8,128)} fusion(bf16[8,128,512]{2,1,0:T(8,128)(2,1)S(1)} %add_convert_fusion, bf16[8,1,128,128]{3,1,2,0:T(2,128)(2,1)} %get-tuple-element.11), kind=kOutput, calls=%fused_computation.80 | convolution fusion | flops 134217728 | bytes 3407872 | tf_op jit(solution)/shard_map/bpq,bqf->bpf/dot_general | solution.py:56
  60.4 8.5 %collective-permute-done.6 = bf16[256,512]{0,1:T(8,128)(2,1)} collective-permute-done((bf16[256,512]{0,1:T(8,128)(2,1)}, bf16[256,512]{0,1:T(8,128)(2,1)}, u32[]{:S(2)}, u32[]{:S(2)}) %collective-permute-start.6) | collective-permute-done | bytes 262176 | tf_op jit(solution)/shard_map/ppermute | solution.py:20
  68.8 3.0 %pad_maximum_fusion = (bf16[1024,512]{0,1:T(8,128)(2,1)}, bf16[1024,512]{0,1:T(8,128)(2,1)}, bf16[1024,512]{0,1:T(8,128)(2,1)}, bf16[1024,512]{0,1:T(8,128)(2,1)}) fusion(bf16[256,512]{0,1:T(8,128)(2,1)} %collective-permute-done.6, bf16[1024,512]{0,1:T(8,128)(2,1)S(1)} %copy.48, bf16[256,512]{0,1:T(8,128)(2,1)S(1)} %collective-permute-done.5), kind=kLoop, calls=%fused_computation.39 | loop fusion | flops 8388608 | bytes 5767168 | tf_op jit(solution)/shard_map/concatenate | solution.py:16
  71.8 1.5 %copy.51 = bf16[1024,512]{1,0:T(8,128)(2,1)S(1)} copy(bf16[1024,512]{0,1:T(8,128)(2,1)} %get-tuple-element.24) | data formatting | bytes 2097152 | tf_op jit(solution)/shard_map/slice | solution.py:59
  73.3 2.9 %fusion.65 = f32[8,128,512]{2,1,0:T(8,128)} fusion(bf16[8,128,512]{2,1,0:T(8,128)(2,1)S(1)} %bitcast.98, bf16[8,1,128,128]{3,1,2,0:T(2,128)(2,1)} %get-tuple-element.12), kind=kOutput, calls=%fused_computation.84 | convolution fusion | flops 134217728 | bytes 3407872 | tf_op jit(solution)/shard_map/bpq,bqf->bpf/dot_general | solution.py:56
  76.8 2.9 %fusion.69 = f32[8,128,512]{2,1,0:T(8,128)} fusion(bf16[8,128,512]{2,1,0:T(8,128)(2,1)S(1)} %bitcast.99, bf16[8,1,128,128]{3,1,2,0:T(2,128)(2,1)} %get-tuple-element.13), kind=kOutput, calls=%fused_computation.88 | convolution fusion | flops 134217728 | bytes 3407872 | tf_op jit(solution)/shard_map/bpq,bqf->bpf/dot_general | solution.py:49
  81.0 3.4 %fusion.57 = f32[8,128,512]{2,1,0:T(8,128)} fusion(bf16[8,128,512]{2,1,0:T(8,128)(2,1)} %bitcast.100, bf16[8,1,128,128]{3,1,2,0:T(2,128)(2,1)} %get-tuple-element.10), kind=kOutput, calls=%fused_computation.76 | convolution fusion | flops 134217728 | bytes 3407872 | tf_op jit(solution)/shard_map/bpq,bqf->bpf/dot_general | solution.py:56
  84.4 2.3 %copy.54 = bf16[1024,512]{1,0:T(8,128)(2,1)} copy(bf16[1024,512]{0,1:T(8,128)(2,1)} %get-tuple-element.19) | data formatting | bytes 2097152 | tf_op jit(solution)/shard_map/slice | solution.py:59
  86.7 5.0 %subtract_convert_fusion = bf16[8,128,512]{2,1,0:T(8,128)(2,1)} fusion(bf16[8,128,512]{2,1,0:T(8,128)(2,1)S(1)} %bitcast.92, f32[8,128,512]{2,1,0:T(8,128)} %fusion.57, f32[8,128,512]{2,1,0:T(8,128)S(1)} %copy-done.2, f32[8,128,512]{2,1,0:T(8,128)} %fusion.69, f32[8,128,512]{2,1,0:T(8,128)} %fusion.65, bf16[8,128,512]{2,1,0:T(8,128)(2,1)} %bitcast.93, ...), kind=kOutput, calls=%fused_computation.9 | convolution fusion | flops 138412032 | bytes 11796480 | tf_op jit(solution)/shard_map/bpq,bqf->bpf/dot_general | solution.py:56
  91.6 2.5 %copy.55 = bf16[1024,512]{0,1:T(8,128)(2,1)} copy(bf16[1024,512]{1,0:T(8,128)(2,1)} %bitcast.94) | data formatting | bytes 2097152 | tf_op jit(solution)/shard_map/reshape | solution.py:150
  94.1 4.6 %maximum_convert_fusion = bf16[1024,512]{0,1:T(8,128)(2,1)} fusion(f32[512]{0:T(512)S(1)} %broadcast_bitcast_fusion, bf16[512,512]{1,0:T(8,128)(2,1)} %get-tuple-element.49, bf16[512,512]{1,0:T(8,128)(2,1)} %get-tuple-element.50, bf16[512,512]{1,0:T(8,128)(2,1)} %bitcast.111, bf16[1024,512]{0,1:T(8,128)(2,1)} %copy.55, bf16[1024,512]{0,1:T(8,128)(2,1)S(1)} %copy-done.10, ...), kind=kOutput, calls=%fused_computation.8 | convolution fusion | flops 1626341376 | bytes 5769216 | tf_op jit(solution)/shard_map/dot_general | solution.py:154
  98.7 2.4 %copy.42 = bf16[1024,4,128]{2,1,0:T(4,128)(2,1)} copy(bf16[1024,4,128]{0,2,1:T(8,128)(2,1)} %bitcast.105) | data formatting | bytes 2097152 | tf_op jit(solution)/shard_map/reshape | solution.py:156
  (97 shorter events, 23.0 us)
Async XLA Ops:
  0.0 19.5 %copy-start = (bf16[8,4,128,128]{3,2,1,0:T(8,128)(2,1)S(1)}, bf16[8,4,128,128]{3,2,1,0:T(8,128)(2,1)}, u32[]{:S(2)}) copy-start(bf16[8,4,128,128]{3,2,1,0:T(8,128)(2,1)} %param.11) | copy-start | bytes 3145732
  0.0 27.7 %collective-permute-start.3 = (bf16[1024,256]{1,0:T(8,128)(2,1)}, bf16[1024,256]{1,0:T(8,128)(2,1)S(1)}, u32[]{:S(2)}, u32[]{:S(2)}) collective-permute-start(bf16[1024,256]{1,0:T(8,128)(2,1)} %param.8), channel_id=1, source_target_pairs={{0,32},{32,64},{64,96},{96,128},{128,160},{160,192},{192,224},{1,3... | collective-permute-start | bytes 1572872 | tf_op jit(solution)/shard_map/ppermute | solution.py:30
  3.0 24.6 %collective-permute-start.2 = (bf16[256,256]{1,0:T(8,128)(2,1)S(1)}, bf16[256,256]{1,0:T(8,128)(2,1)S(1)}, u32[]{:S(2)}, u32[]{:S(2)}) collective-permute-start(bf16[256,256]{1,0:T(8,128)(2,1)S(1)} %get-tuple-element.32), channel_id=1, source_target_pairs={{0,33},{32,65},{64,97},{96,129},{128,161},{160,193},{192,225},{1,3... | collective-permute-start | bytes 393224 | tf_op jit(solution)/shard_map/ppermute | solution.py:114
  9.3 18.2 %collective-permute-start = (bf16[256,256]{1,0:T(8,128)(2,1)S(1)}, bf16[256,256]{1,0:T(8,128)(2,1)S(1)}, u32[]{:S(2)}, u32[]{:S(2)}) collective-permute-start(bf16[256,256]{1,0:T(8,128)(2,1)S(1)} %get-tuple-element.32), channel_id=1, source_target_pairs={{0,1},{1,2},{2,3},{3,4},{4,5},{5,6},{6,7},{7,8},{8,9},{9,10},{10,1... | collective-permute-start | bytes 393224 | tf_op jit(solution)/shard_map/ppermute | solution.py:111
  12.7 15.1 %collective-permute-start.4 = (bf16[256,256]{1,0:T(8,128)(2,1)S(1)}, bf16[256,256]{1,0:T(8,128)(2,1)S(1)}, u32[]{:S(2)}, u32[]{:S(2)}) collective-permute-start(bf16[256,256]{1,0:T(8,128)(2,1)S(1)} %get-tuple-element.31), channel_id=1, source_target_pairs={{1,32},{33,64},{65,96},{97,128},{129,160},{161,192},{193,224},{2,3... | collective-permute-start | bytes 393224 | tf_op jit(solution)/shard_map/ppermute | solution.py:115
  14.6 13.0 %collective-permute-start.1 = (bf16[256,256]{1,0:T(8,128)(2,1)S(1)}, bf16[256,256]{1,0:T(8,128)(2,1)S(1)}, u32[]{:S(2)}, u32[]{:S(2)}) collective-permute-start(bf16[256,256]{1,0:T(8,128)(2,1)S(1)} %get-tuple-element.31), channel_id=1, source_target_pairs={{1,0},{2,1},{3,2},{4,3},{5,4},{6,5},{7,6},{8,7},{9,8},{10,9},{11,1... | collective-permute-start | bytes 393224 | tf_op jit(solution)/shard_map/ppermute | solution.py:112
  20.8 3.4 %copy-start.19 = (bf16[3,128,128]{2,1,0:T(8,128)(2,1)S(1)}, bf16[3,128,128]{2,1,0:T(8,128)(2,1)}, u32[]{:S(2)}) copy-start(bf16[3,128,128]{2,1,0:T(8,128)(2,1)} %param.14) | copy-start | bytes 294916
  20.8 3.4 %copy-start.21 = (f32[128]{0:T(128)S(1)}, f32[128]{0:T(128)}, u32[]{:S(2)}) copy-start(f32[128]{0:T(128)} %param.15) | copy-start | bytes 1540
  24.3 2.2 %copy-start.20 = (f32[256]{0:T(256)S(1)}, f32[256]{0:T(256)}, u32[]{:S(2)}) copy-start(f32[256]{0:T(256)} %param.10) | copy-start | bytes 3076
  25.0 2.6 %copy-start.18 = (bf16[1024,256]{1,0:T(8,128)(2,1)S(1)}, bf16[1024,256]{1,0:T(8,128)(2,1)}, u32[]{:S(2)}) copy-start(bf16[1024,256]{1,0:T(8,128)(2,1)} %param.8) | copy-start | bytes 1572868
  33.6 1.9 %copy-start.3 = (bf16[1024,512]{0,1:T(8,128)(2,1)}, bf16[1024,512]{0,1:T(8,128)(2,1)S(1)}, u32[]{:S(2)}) copy-start(bf16[1024,512]{0,1:T(8,128)(2,1)S(1)} %get-tuple-element.18) | copy-start | bytes 3145732
  35.5 2.4 %copy-start.5 = (bf16[1024,512]{0,1:T(8,128)(2,1)S(1)}, bf16[1024,512]{0,1:T(8,128)(2,1)}, u32[]{:S(2)}) copy-start(bf16[1024,512]{0,1:T(8,128)(2,1)} %get-tuple-element.17) | copy-start | bytes 3145732
  40.5 1.5 %copy-start.16 = (bf16[8,1,128,128]{3,1,2,0:T(2,128)(2,1)S(1)}, bf16[8,1,128,128]{3,1,2,0:T(2,128)(2,1)}, u32[]{:S(2)}) copy-start(bf16[8,1,128,128]{3,1,2,0:T(2,128)(2,1)} %get-tuple-element.11) | copy-start | bytes 786436
  42.5 1.5 %copy-start.14 = (bf16[8,1,128,128]{3,1,2,0:T(2,128)(2,1)S(1)}, bf16[8,1,128,128]{3,1,2,0:T(2,128)(2,1)}, u32[]{:S(2)}) copy-start(bf16[8,1,128,128]{3,1,2,0:T(2,128)(2,1)} %get-tuple-element.13) | copy-start | bytes 786436
  43.8 1.4 %copy-start.17 = (bf16[8,1,128,128]{3,1,2,0:T(2,128)(2,1)S(1)}, bf16[8,1,128,128]{3,1,2,0:T(2,128)(2,1)}, u32[]{:S(2)}) copy-start(bf16[8,1,128,128]{3,1,2,0:T(2,128)(2,1)} %get-tuple-element.9) | copy-start | bytes 786436
  46.8 13.6 %collective-permute-start.5 = (bf16[256,512]{0,1:T(8,128)(2,1)}, bf16[256,512]{0,1:T(8,128)(2,1)S(1)}, u32[]{:S(2)}, u32[]{:S(2)}) collective-permute-start(bf16[256,512]{0,1:T(8,128)(2,1)} %copy.49), channel_id=1, source_target_pairs={{0,1},{1,2},{2,3},{3,4},{4,5},{5,6},{6,7},{7,8},{8,9},{9,10},{10,1... | collective-permute-start | bytes 786440 | tf_op jit(solution)/shard_map/ppermute | solution.py:18
  54.3 14.5 %collective-permute-start.6 = (bf16[256,512]{0,1:T(8,128)(2,1)}, bf16[256,512]{0,1:T(8,128)(2,1)}, u32[]{:S(2)}, u32[]{:S(2)}) collective-permute-start(bf16[256,512]{0,1:T(8,128)(2,1)} %copy.52), channel_id=1, source_target_pairs={{1,0},{2,1},{3,2},{4,3},{5,4},{6,5},{7,6},{8,7},{9,8},{10,9},{11,1... | collective-permute-start | bytes 786440 | tf_op jit(solution)/shard_map/ppermute | solution.py:20
  57.0 14.9 %copy-start.9 = (bf16[1024,512]{0,1:T(8,128)(2,1)}, bf16[1024,512]{0,1:T(8,128)(2,1)S(1)}, u32[]{:S(2)}) copy-start(bf16[1024,512]{0,1:T(8,128)(2,1)S(1)} %copy.48) | copy-start | bytes 3145732
  73.3 2.9 %copy-start.12 = (bf16[1024,512]{0,1:T(8,128)(2,1)S(1)}, bf16[1024,512]{0,1:T(8,128)(2,1)}, u32[]{:S(2)}) copy-start(bf16[1024,512]{0,1:T(8,128)(2,1)} %get-tuple-element.23) | copy-start | bytes 3145732
  76.8 2.9 %copy-start.11 = (bf16[1024,512]{0,1:T(8,128)(2,1)S(1)}, bf16[1024,512]{0,1:T(8,128)(2,1)}, u32[]{:S(2)}) copy-start(bf16[1024,512]{0,1:T(8,128)(2,1)} %get-tuple-element.20) | copy-start | bytes 3145732
  81.0 5.6 %copy-start.2 = (f32[8,128,512]{2,1,0:T(8,128)S(1)}, f32[8,128,512]{2,1,0:T(8,128)}, u32[]{:S(2)}) copy-start(f32[8,128,512]{2,1,0:T(8,128)} %fusion.61) | copy-start | bytes 6291460
  91.6 2.5 %copy-start.4 = (bf16[1024,512]{0,1:T(8,128)(2,1)S(1)}, bf16[1024,512]{0,1:T(8,128)(2,1)}, u32[]{:S(2)}) copy-start(bf16[1024,512]{0,1:T(8,128)(2,1)} %copy-done.3) | copy-start | bytes 3145732
  91.6 2.5 %copy-start.10 = (bf16[1024,512]{0,1:T(8,128)(2,1)S(1)}, bf16[1024,512]{0,1:T(8,128)(2,1)}, u32[]{:S(2)}) copy-start(bf16[1024,512]{0,1:T(8,128)(2,1)} %copy-done.9) | copy-start | bytes 3145732
  94.1 7.0 %copy-start.1 = (bf16[8,4,128,128]{3,2,1,0:T(8,128)(2,1)S(1)}, bf16[8,4,128,128]{3,2,1,0:T(8,128)(2,1)}, u32[]{:S(2)}) copy-start(bf16[8,4,128,128]{3,2,1,0:T(8,128)(2,1)} %param.11) | copy-start | bytes 3145732
  (5 other events, 6.6 us)

commit v3 on v1

--- a/solution.py
+++ b/solution.py
@@ -110,14 +110,21 @@
     first_block = lax.axis_index("node") * block_count
 
     band_tiles = build_band(tile_values, tile_cols, tile_count, first_block)
-    extended = fetch_rim(flat_features, block_rows).reshape(
-        block_count + 2 * HB, block_rows, feat_width
+    node_count = lax.axis_size("node")
+    to_right = [(i, i + 1) for i in range(node_count - 1)]
+    to_left = [(i + 1, i) for i in range(node_count - 1)]
+    band_left = lax.ppermute(band_tiles[block_count - HB :], "node", to_right)
+    band_right = lax.ppermute(band_tiles[:HB], "node", to_left)
+    reach = 2 * HB * block_rows
+    feat_left = lax.ppermute(flat_features[row_count - reach :], "node", to_right)
+    feat_right = lax.ppermute(flat_features[:reach], "node", to_left)
+    feat_ext = jnp.concatenate([feat_left, flat_features, feat_right], axis=0).reshape(
+        block_count + 4 * HB, block_rows, feat_width
     )
-    order_one = band_product(band_tiles, extended).astype(jnp.bfloat16)
-    one_ext = fetch_rim(order_one.reshape(row_count, feat_width), block_rows).reshape(
-        block_count + 2 * HB, block_rows, feat_width
-    )
+    band_ext = jnp.concatenate([band_left, band_tiles, band_right], axis=0)
+    one_ext = band_product(band_ext, feat_ext).astype(jnp.bfloat16)
     order_two = band_product(band_tiles, one_ext)
+    order_one = one_ext[HB : HB + block_count]
     by_block = flat_features.reshape(block_count, block_rows, feat_width)
     cheb_two = (2.0 * order_two - by_block.astype(jnp.float32)).astype(jnp.bfloat16)
     joined = jnp.concatenate(

time: 58 us -> 74.2 us (1.28)
  other arithmetic: 5.44 us -> 14.3 us
  waiting for transfers between devices: 20.7 us -> 24.3 us
  local copies, waits for them, and re-layouts: 6.86 us -> 9.67 us
  matrix products: 9.35 us -> 10.3 us
    concatenate x2 -> x4, other arithmetic: 3.42 us -> 11 us  [the longest x2 10.2 us: shards(): jnp.concatenate([feat_left, flat_features, feat_right], axis=0)]
    ppermute x4, waiting for transfers between devices: 19.5 us -> 24.3 us  [the longest x1 8 us: shards(): band_right = lax.ppermute(band_tiles[:HB], 'node', to_left)]
    slice x1 -> x2, local copies, waits for them, and re-layouts: 2.65 us -> 6.87 us  [band_product(): band_tiles[:, offset]]
    ppermute x1, waiting for transfers between devices: 1.19 us -> 0.01 us  [passed_along(): return lax.ppermute(value, axis, pairs)]
    slice x1, local copies, waits for them, and re-layouts: 1.07 us -> 0.04 us  [shards(): newest = window[:, base:base + pair_w]]
    dot_general x8, matrix products: 3.96 us -> 4.76 us  [band_product(): jnp.einsum('bpq,bqf->bpf', band_tiles[:, offset], extended[offset:offset...]
    mul x1, local copies, waits for them, and re-layouts: 0.8 us -> 0.01 us  [pair_weight(): blocks = [jnp.kron(eye, conv_weight[k]) for k in range(taps)]]
  transfers between devices with their start and end apart: 5 -> 5, of which waited for: 5 -> 4; matrix products, arithmetic and copies ran while one was open for 14% -> 16% of each run, Pallas kernels for 0% -> 0%
where the time goes in v3:
time: 74.2 us; the launch traced here: 73.8 us
  waiting for transfers between devices  24.3 us (33%)
  starting transfers between devices  14.9 us (20%)
  other arithmetic  14.3 us (19%)
  matrix products  10.3 us (14%)
  local copies, waits for them, and re-layouts  9.67 us (13%)
    concatenate x2, other arithmetic, shards(): jnp.concatenate([feat_left, flat_features, feat_right], axis=0)  10.2 us
    ppermute x1, waiting for transfers between devices, shards(): band_right = lax.ppermute(band_tiles[:HB], 'node', to_left)  8 us
    slice x2, local copies, waits for them, and re-layouts, band_product(): band_tiles[:, offset]  6.87 us
    ppermute x1, waiting for transfers between devices, shards(): lax.ppermute(flat_features[row_count - reach:], 'node', to_right)  5.71 us
    ppermute x1, waiting for transfers between devices, shards(): band_left = lax.ppermute(band_tiles[block_count - HB:], 'node', to_right)  5.3 us
    ppermute x1, waiting for transfers between devices, shards(): feat_right = lax.ppermute(flat_features[:reach], 'node', to_left)  5.25 us
    ppermute x1, starting transfers between devices, shards(): band_left = lax.ppermute(band_tiles[block_count - HB:], 'node', to_right)  4.95 us
    dot_general x8, matrix products, band_product(): jnp.einsum('bpq,bqf->bpf', band_tiles[:, offset], extended[offset:offset...  4.76 us
  transfers between devices with their start and end apart: 5, of which 4 were waited for; matrix products, arithmetic and copies ran while one was open for 16% of the time, Pallas kernels for 0%

profile of v3, /device:TPU:110, one launch (start us, length us, event | category | flops | bytes accessed | tf_op | source)
XLA Modules:
  0.0 73.8 jit_solution(10960604699627827881)
XLA Ops:
  0.0 2.0 %collective-permute-start = (bf16[1024,256]{1,0:T(8,128)(2,1)}, bf16[1024,256]{1,0:T(8,128)(2,1)S(1)}, u32[]{:S(2)}, u32[]{:S(2)}) collective-permute-start(bf16[1024,256]{1,0:T(8,128)(2,1)} %param.8), channel_id=1, source_target_pairs={{0,32},{32,64},{64,96},{96,128},{128,160},{160,192},{192,224},{1,3... | collective-permute-start | bytes 1572872 | tf_op jit(solution)/shard_map/ppermute | solution.py:30
  2.1 0.7 subtract_add_fusion
  2.8 0.7 iota_compare_fusion.2
  3.6 1.3 %convolution_convert_fusion = bf16[8,5,128,128]{3,1,2,0:T(8,128)(2,1)S(1)} fusion(bf16[8,4,128,128]{3,2,1,0:T(8,128)(2,1)S(1)} %copy-done, s32[8,4]{1,0:T(8,128)S(1)} %copy.12, pred[8,4]{1,0:T(8,128)(4,1)S(1)} %iota_compare_fusion.2), kind=kOutput, calls=%fused_computation.5 | convolution fusion | flops 5898560 | bytes 2359456 | tf_op jit(solution)/shard_map/bjo,bjpq->bopq/dot_general | solution.py:41
  5.0 5.0 %collective-permute-start.1 = (bf16[2,5,128,128]{3,1,2,0:T(8,128)(2,1)S(1)}, bf16[2,5,128,128]{3,1,2,0:T(8,128)(2,1)S(1)}, u32[]{:S(2)}, u32[]{:S(2)}) collective-permute-start(bf16[2,5,128,128]{3,1,2,0:T(8,128)(2,1)S(1)} %get-tuple-element.26), channel_id=1, source_target_pairs={{0,1},{1,2},{2,3},{3,4},{4,5},{5,6},{6,7},{7,8},{8,9},{9,10},{10,1... | collective-permute-start | bytes 983048 | tf_op jit(solution)/shard_map/ppermute | solution.py:116
  10.0 1.9 %collective-permute-start.2 = (bf16[2,5,128,128]{3,1,2,0:T(8,128)(2,1)S(1)}, bf16[2,5,128,128]{3,1,2,0:T(8,128)(2,1)S(1)}, u32[]{:S(2)}, u32[]{:S(2)}) collective-permute-start(bf16[2,5,128,128]{3,1,2,0:T(8,128)(2,1)S(1)} %get-tuple-element.27), channel_id=1, source_target_pairs={{1,0},{2,1},{3,2},{4,3},{5,4},{6,5},{7,6},{8,7},{9,8},{10,9},{11,1... | collective-permute-start | bytes 983048 | tf_op jit(solution)/shard_map/ppermute | solution.py:117
  12.0 2.6 %fusion.99 = (bf16[8,1,128,128]{3,1,2,0:T(2,128)(2,1)S(1)}, bf16[8,1,128,128]{3,1,2,0:T(2,128)(2,1)S(1)}, bf16[8,1,128,128]{3,1,2,0:T(2,128)(2,1)S(1)}, bf16[8,1...) fusion(bf16[8,5,128,128]{3,1,2,0:T(8,128)(2,1)S(1)} %convolution_convert_fusion), kind=kLoop, calls=%fused_computation.144 | loop fusion | bytes 2621440 | tf_op jit(solution)/shard_map/slice | solution.py:58
  15.3 0.7 broadcast_multiply_fusion.2
  16.3 5.3 %collective-permute-done.1 = bf16[2,5,128,128]{3,1,2,0:T(8,128)(2,1)S(1)} collective-permute-done((bf16[2,5,128,128]{3,1,2,0:T(8,128)(2,1)S(1)}, bf16[2,5,128,128]{3,1,2,0:T(8,128)(2,1)S(1)}, u32[]{:S(2)}, u32[]{:S(2)}) %collective-permute-start.1) | collective-permute-done | bytes 327712 | tf_op jit(solution)/shard_map/ppermute | solution.py:116
  21.6 8.0 %collective-permute-done.2 = bf16[2,5,128,128]{3,1,2,0:T(8,128)(2,1)S(1)} collective-permute-done((bf16[2,5,128,128]{3,1,2,0:T(8,128)(2,1)S(1)}, bf16[2,5,128,128]{3,1,2,0:T(8,128)(2,1)S(1)}, u32[]{:S(2)}, u32[]{:S(2)}) %collective-permute-start.2) | collective-permute-done | bytes 327712 | tf_op jit(solution)/shard_map/ppermute | solution.py:117
  29.6 0.7 %pad_maximum_fusion = bf16[12,5,128,128]{3,1,2,0:T(8,128)(2,1)S(1)} fusion(bf16[2,5,128,128]{3,1,2,0:T(8,128)(2,1)S(1)} %collective-permute-done.2, bf16[8,5,128,128]{3,1,2,0:T(8,128)(2,1)S(1)} %convolution_convert_fusion, bf16[2,5,128,128]{3,1,2,0:T(8,128)(2,1)S(1)} %collective-permute-done.1), kind=kLoop, calls=%fused_computation | loop fusion | flops 1966080 | bytes 3932160 | tf_op jit(solution)/shard_map/concatenate | solution.py:124
  30.4 0.7 fusion.15
  31.4 0.7 fusion.23
  32.7 1.9 %collective-permute-start.3 = (bf16[512,512]{1,0:T(8,128)(2,1)S(1)}, bf16[512,512]{1,0:T(8,128)(2,1)S(1)}, u32[]{:S(2)}, u32[]{:S(2)}) collective-permute-start(bf16[512,512]{1,0:T(8,128)(2,1)S(1)} %get-tuple-element.30), channel_id=1, source_target_pairs={{0,1},{1,2},{2,3},{3,4},{4,5},{5,6},{6,7},{7,8},{8,9},{9,10},{10,1... | collective-permute-start | bytes 1572872 | tf_op jit(solution)/shard_map/ppermute | solution.py:119
  34.6 4.1 %collective-permute-start.4 = (bf16[512,512]{1,0:T(8,128)(2,1)S(1)}, bf16[512,512]{1,0:T(8,128)(2,1)S(1)}, u32[]{:S(2)}, u32[]{:S(2)}) collective-permute-start(bf16[512,512]{1,0:T(8,128)(2,1)S(1)} %get-tuple-element.31), channel_id=1, source_target_pairs={{1,0},{2,1},{3,2},{4,3},{5,4},{6,5},{7,6},{8,7},{9,8},{10,9},{11,1... | collective-permute-start | bytes 1572872 | tf_op jit(solution)/shard_map/ppermute | solution.py:120
  38.8 4.2 %fusion.98 = (bf16[12,1,128,128]{3,1,2,0:T(2,128)(2,1)S(1)}, bf16[12,1,128,128]{3,1,2,0:T(2,128)(2,1)S(1)}, bf16[12,1,128,128]{3,1,2,0:T(2,128)(2,1)S(1)}, bf16[...) fusion(bf16[12,5,128,128]{3,1,2,0:T(8,128)(2,1)S(1)} %pad_maximum_fusion), kind=kLoop, calls=%fused_computation.143 | loop fusion | bytes 3932160 | tf_op jit(solution)/shard_map/slice | solution.py:58
  43.0 5.7 %collective-permute-done.3 = bf16[512,512]{1,0:T(8,128)(2,1)S(1)} collective-permute-done((bf16[512,512]{1,0:T(8,128)(2,1)S(1)}, bf16[512,512]{1,0:T(8,128)(2,1)S(1)}, u32[]{:S(2)}, u32[]{:S(2)}) %collective-permute-start.3) | collective-permute-done | bytes 524320 | tf_op jit(solution)/shard_map/ppermute | solution.py:119
  48.7 5.2 %collective-permute-done.4 = bf16[512,512]{1,0:T(8,128)(2,1)S(1)} collective-permute-done((bf16[512,512]{1,0:T(8,128)(2,1)S(1)}, bf16[512,512]{1,0:T(8,128)(2,1)S(1)}, u32[]{:S(2)}, u32[]{:S(2)}) %collective-permute-start.4) | collective-permute-done | bytes 524320 | tf_op jit(solution)/shard_map/ppermute | solution.py:120
  54.0 5.1 %pad_maximum_fusion.1 = bf16[2048,512]{1,0:T(8,128)(2,1)S(1)} fusion(bf16[512,512]{1,0:T(8,128)(2,1)S(1)} %collective-permute-done.4, bf16[1024,128]{1,0:T(8,128)(2,1)S(1)} %get-tuple-element.6, bf16[1024,128]{1,0:T(8,128)(2,1)S(1)} %get-tuple-element.8, bf16[1024,128]{1,0:T(8,128)(2,1)S(1)} %get-tuple-element.10, ...), kind=kLoop, calls=%fused_computation.2 | loop fusion | flops 12582912 | bytes 4194304 | tf_op jit(solution)/shard_map/concatenate | solution.py:121
  59.5 5.0 %pad_maximum_fusion.2 = (bf16[1536,512]{1,0:T(8,128)(2,1)S(1)}, bf16[1536,512]{1,0:T(8,128)(2,1)S(1)}) fusion(bf16[512,512]{1,0:T(8,128)(2,1)S(1)} %collective-permute-done.4, bf16[1024,128]{1,0:T(8,128)(2,1)S(1)} %get-tuple-element.6, bf16[1024,128]{1,0:T(8,128)(2,1)S(1)} %get-tuple-element.8, bf16[1024,128]{1,0:T(8,128)(2,1)S(1)} %get-tuple-element.10, ...), kind=kLoop, calls=%fused_computation.7 | loop fusion | flops 15728640 | bytes 5242880 | tf_op jit(solution)/shard_map/concatenate | solution.py:121
  66.8 0.9 %add_convert_fusion = bf16[12,128,512]{2,1,0:T(8,128)(2,1)S(1)} fusion(f32[12,128,512]{2,1,0:T(8,128)S(1)} %fusion.58, f32[12,128,512]{2,1,0:T(8,128)S(1)} %fusion.61, f32[12,128,512]{2,1,0:T(8,128)S(1)} %fusion.67, f32[12,128,512]{2,1,0:T(8,128)S(1)} %fusion.64, bf16[12,128,512]{2,1,0:T(8,128)(2,1)S(1)} %bitcast.97, ...), kind=kOutput, calls=%fused_computation.1 | convolution fusion | flops 205258752 | bytes 16121856 | tf_op jit(solution)/shard_map/bpq,bqf->bpf/dot_general | solution.py:56
  69.5 0.9 %subtract_convert_fusion = bf16[8,128,512]{2,1,0:T(8,128)(2,1)S(1)} fusion(f32[8,128,512]{2,1,0:T(8,128)S(1)} %fusion.9, f32[8,128,512]{2,1,0:T(8,128)S(1)} %fusion.74, f32[8,128,512]{2,1,0:T(8,128)S(1)} %fusion.13, f32[8,128,512]{2,1,0:T(8,128)S(1)} %fusion.11, bf16[12,128,512]{2,1,0:T(8,128)(2,1)S(1)} %add_convert_fusion, ...), kind=kOutput, calls=%fused_computation.4 | convolution fusion | flops 142082048 | bytes 12058624 | tf_op jit(solution)/shard_map/bpq,bqf->bpf/dot_general | solution.py:56
  70.5 1.9 %maximum_convert_fusion = bf16[1024,512]{0,1:T(8,128)(2,1)S(1)} fusion(bf16[1024,1536]{1,0:T(8,128)(2,1)S(1)} %constant_dynamic-update-slice_fusion, bf16[512,512]{1,0:T(8,128)(2,1)S(1)} %get-tuple-element.50, bf16[512,512]{1,0:T(8,128)(2,1)S(1)} %get-tuple-element.51, bf16[512,512]{1,0:T(8,128)(2,1)S(1)} %bitcast.107, f32[512]{0:T(512)S(1)} %broadcast_bitcast_fusion), kind=kOutput, calls=%fused_computation.3 | convolution fusion | flops 1616904192 | bytes 5769216 | tf_op jit(solution)/shard_map/dot_general | solution.py:135
  72.4 1.4 %copy.14 = bf16[1024,4,128]{2,1,0:T(4,128)(2,1)} copy(bf16[1024,4,128]{0,2,1:T(8,128)(2,1)S(1)} %bitcast.103) | data formatting | bytes 2097152 | tf_op jit(solution)/shard_map/reshape | solution.py:137
  (52 shorter events, 6.6 us)
Async XLA Ops:
  0.0 3.6 %copy-start = (bf16[8,4,128,128]{3,2,1,0:T(8,128)(2,1)S(1)}, bf16[8,4,128,128]{3,2,1,0:T(8,128)(2,1)}, u32[]{:S(2)}) copy-start(bf16[8,4,128,128]{3,2,1,0:T(8,128)(2,1)} %param.11) | copy-start | bytes 3145732
  0.0 30.3 %collective-permute-start = (bf16[1024,256]{1,0:T(8,128)(2,1)}, bf16[1024,256]{1,0:T(8,128)(2,1)S(1)}, u32[]{:S(2)}, u32[]{:S(2)}) collective-permute-start(bf16[1024,256]{1,0:T(8,128)(2,1)} %param.8), channel_id=1, source_target_pairs={{0,32},{32,64},{64,96},{96,128},{128,160},{160,192},{192,224},{1,3... | collective-permute-start | bytes 1572872 | tf_op jit(solution)/shard_map/ppermute | solution.py:30
  3.6 8.4 %copy-start.2 = (bf16[1024,256]{1,0:T(8,128)(2,1)S(1)}, bf16[1024,256]{1,0:T(8,128)(2,1)}, u32[]{:S(2)}) copy-start(bf16[1024,256]{1,0:T(8,128)(2,1)} %param.8) | copy-start | bytes 1572868
  5.0 16.5 %collective-permute-start.1 = (bf16[2,5,128,128]{3,1,2,0:T(8,128)(2,1)S(1)}, bf16[2,5,128,128]{3,1,2,0:T(8,128)(2,1)S(1)}, u32[]{:S(2)}, u32[]{:S(2)}) collective-permute-start(bf16[2,5,128,128]{3,1,2,0:T(8,128)(2,1)S(1)} %get-tuple-element.26), channel_id=1, source_target_pairs={{0,1},{1,2},{2,3},{3,4},{4,5},{5,6},{6,7},{7,8},{8,9},{9,10},{10,1... | collective-permute-start | bytes 983048 | tf_op jit(solution)/shard_map/ppermute | solution.py:116
  10.0 19.6 %collective-permute-start.2 = (bf16[2,5,128,128]{3,1,2,0:T(8,128)(2,1)S(1)}, bf16[2,5,128,128]{3,1,2,0:T(8,128)(2,1)S(1)}, u32[]{:S(2)}, u32[]{:S(2)}) collective-permute-start(bf16[2,5,128,128]{3,1,2,0:T(8,128)(2,1)S(1)} %get-tuple-element.27), channel_id=1, source_target_pairs={{1,0},{2,1},{3,2},{4,3},{5,4},{6,5},{7,6},{8,7},{9,8},{10,9},{11,1... | collective-permute-start | bytes 983048 | tf_op jit(solution)/shard_map/ppermute | solution.py:117
  12.0 2.7 %copy-start.3 = (bf16[3,64,256]{2,1,0:T(8,128)(2,1)S(1)}, bf16[3,64,256]{2,1,0:T(8,128)(2,1)}, u32[]{:S(2)}) copy-start(bf16[3,64,256]{2,1,0:T(8,128)(2,1)} %param.9) | copy-start | bytes 294916
  12.0 2.8 %copy-start.4 = (bf16[3,128,128]{2,1,0:T(8,128)(2,1)S(1)}, bf16[3,128,128]{2,1,0:T(8,128)(2,1)}, u32[]{:S(2)}) copy-start(bf16[3,128,128]{2,1,0:T(8,128)(2,1)} %param.14) | copy-start | bytes 294916
  12.0 2.8 %copy-start.6 = (f32[128]{0:T(128)S(1)}, f32[128]{0:T(128)}, u32[]{:S(2)}) copy-start(f32[128]{0:T(128)} %param.15) | copy-start | bytes 1540
  14.7 1.2 %copy-start.5 = (f32[256]{0:T(256)S(1)}, f32[256]{0:T(256)}, u32[]{:S(2)}) copy-start(f32[256]{0:T(256)} %param.10) | copy-start | bytes 3076
  32.7 16.0 %collective-permute-start.3 = (bf16[512,512]{1,0:T(8,128)(2,1)S(1)}, bf16[512,512]{1,0:T(8,128)(2,1)S(1)}, u32[]{:S(2)}, u32[]{:S(2)}) collective-permute-start(bf16[512,512]{1,0:T(8,128)(2,1)S(1)} %get-tuple-element.30), channel_id=1, source_target_pairs={{0,1},{1,2},{2,3},{3,4},{4,5},{5,6},{6,7},{7,8},{8,9},{9,10},{10,1... | collective-permute-start | bytes 1572872 | tf_op jit(solution)/shard_map/ppermute | solution.py:119
  34.6 19.3 %collective-permute-start.4 = (bf16[512,512]{1,0:T(8,128)(2,1)S(1)}, bf16[512,512]{1,0:T(8,128)(2,1)S(1)}, u32[]{:S(2)}, u32[]{:S(2)}) collective-permute-start(bf16[512,512]{1,0:T(8,128)(2,1)S(1)} %get-tuple-element.31), channel_id=1, source_target_pairs={{1,0},{2,1},{3,2},{4,3},{5,4},{6,5},{7,6},{8,7},{9,8},{10,9},{11,1... | collective-permute-start | bytes 1572872 | tf_op jit(solution)/shard_map/ppermute | solution.py:120
  70.5 3.3 %copy-start.1 = (bf16[8,4,128,128]{3,2,1,0:T(8,128)(2,1)S(1)}, bf16[8,4,128,128]{3,2,1,0:T(8,128)(2,1)}, u32[]{:S(2)}) copy-start(bf16[8,4,128,128]{3,2,1,0:T(8,128)(2,1)} %param.11) | copy-start | bytes 3145732

commit v4 on v1

--- a/solution.py
+++ b/solution.py
@@ -2,6 +2,8 @@
 import jax.numpy as jnp
 from jax import lax
 from jax.sharding import PartitionSpec as P
+from jax.experimental import pallas as pl
+from jax.experimental.pallas import tpu as pltpu
 
 HB = 2
 TPB = 4
@@ -60,6 +62,82 @@
             preferred_element_type=jnp.float32,
         )
     return total
+
+
+def _source(b, o, nb, left_ref, own_ref, right_ref, rows):
+    j = b + o - HB
+    if j < 0:
+        return left_ref, (j + HB) * rows
+    if j >= nb:
+        return right_ref, (j - nb) * rows
+    return own_ref, j * rows
+
+
+def _band_sum(b, band_ref, left_ref, own_ref, right_ref):
+    nb = band_ref.shape[0]
+    rows = band_ref.shape[2]
+    acc = None
+    for o in range(2 * HB + 1):
+        src, r0 = _source(b, o, nb, left_ref, own_ref, right_ref, rows)
+        term = jnp.dot(band_ref[b, o], src[r0 : r0 + rows, :], preferred_element_type=jnp.float32)
+        acc = term if acc is None else acc + term
+    return acc
+
+
+def _first_kernel(band_ref, left_ref, own_ref, right_ref, out_ref):
+    nb, rows = band_ref.shape[0], band_ref.shape[2]
+    for b in range(nb):
+        acc = _band_sum(b, band_ref, left_ref, own_ref, right_ref)
+        out_ref[b * rows : (b + 1) * rows, :] = acc.astype(out_ref.dtype)
+
+
+def _second_kernel(band_ref, left_ref, own_ref, right_ref, feat_ref, weight_ref, bias_ref, out_ref):
+    nb, rows = band_ref.shape[0], band_ref.shape[2]
+    chan = weight_ref.shape[1]
+    steps = own_ref.shape[1] // chan
+    bias = bias_ref[...]
+    for b in range(nb):
+        acc = _band_sum(b, band_ref, left_ref, own_ref, right_ref)
+        lo, hi = b * rows, (b + 1) * rows
+        feat = feat_ref[lo:hi, :]
+        cheb_two = (2.0 * acc - feat.astype(jnp.float32)).astype(jnp.bfloat16)
+        one = own_ref[lo:hi, :]
+        for t in range(steps):
+            cols = slice(t * chan, (t + 1) * chan)
+            joined = jnp.concatenate([feat[:, cols], one[:, cols], cheb_two[:, cols]], axis=1)
+            res = jnp.dot(joined, weight_ref[...], preferred_element_type=jnp.float32) + bias
+            out_ref[lo:hi, cols] = jnp.maximum(res, 0.0).astype(out_ref.dtype)
+
+
+def _vmem_specs(count):
+    return [pl.BlockSpec(memory_space=pltpu.VMEM) for _ in range(count)]
+
+
+def first_product(band_tiles, left, own, right):
+    rows, width = own.shape
+    flops = 2 * band_tiles.shape[0] * (2 * HB + 1) * band_tiles.shape[2] ** 2 * width
+    return pl.pallas_call(
+        _first_kernel,
+        out_shape=jax.ShapeDtypeStruct((rows, width), jnp.bfloat16),
+        in_specs=_vmem_specs(4),
+        out_specs=pl.BlockSpec(memory_space=pltpu.VMEM),
+        cost_estimate=pl.CostEstimate(flops=flops, transcendentals=0, bytes_accessed=6 * rows * width),
+    )(band_tiles, left, own, right)
+
+
+def second_product(band_tiles, left, own, right, features, cheb_weight, cheb_bias):
+    rows, width = own.shape
+    weight = cheb_weight.reshape(-1, cheb_weight.shape[2])
+    bias = cheb_bias.reshape(1, -1)
+    flops = 2 * band_tiles.shape[0] * (2 * HB + 1) * band_tiles.shape[2] ** 2 * width
+    flops += 2 * rows * width * weight.shape[0]
+    return pl.pallas_call(
+        _second_kernel,
+        out_shape=jax.ShapeDtypeStruct((rows, width), jnp.bfloat16),
+        in_specs=_vmem_specs(7),
+        out_specs=pl.BlockSpec(memory_space=pltpu.VMEM),
+        cost_estimate=pl.CostEstimate(flops=flops, transcendentals=0, bytes_accessed=8 * rows * width),
+    )(band_tiles, left, own, right, features, weight, bias)
 
 
 def fetch_rim(values, block_rows):
@@ -110,24 +188,19 @@
     first_block = lax.axis_index("node") * block_count
 
     band_tiles = build_band(tile_values, tile_cols, tile_count, first_block)
-    extended = fetch_rim(flat_features, block_rows).reshape(
-        block_count + 2 * HB, block_rows, feat_width
-    )
-    order_one = band_product(band_tiles, extended).astype(jnp.bfloat16)
-    one_ext = fetch_rim(order_one.reshape(row_count, feat_width), block_rows).reshape(
-        block_count + 2 * HB, block_rows, feat_width
-    )
-    order_two = band_product(band_tiles, one_ext)
-    by_block = flat_features.reshape(block_count, block_rows, feat_width)
-    cheb_two = (2.0 * order_two - by_block.astype(jnp.float32)).astype(jnp.bfloat16)
-    joined = jnp.concatenate(
-        [flat_features, order_one.reshape(row_count, feat_width), cheb_two.reshape(row_count, feat_width)],
-        axis=1,
-    )
-    wfinal = jnp.concatenate([block_diag(cheb_weight[k], steps_dev) for k in range(3)], axis=0)
-    result = jnp.dot(joined, wfinal, preferred_element_type=jnp.float32)
-    result = result + jnp.tile(cheb_bias, steps_dev)
-    return jax.nn.relu(result).astype(jnp.bfloat16).reshape(row_count, steps_dev, chan_out)
+    node_count = lax.axis_size("node")
+    to_right = [(i, i + 1) for i in range(node_count - 1)]
+    to_left = [(i + 1, i) for i in range(node_count - 1)]
+    rim = HB * block_rows
+    feat_left = lax.ppermute(flat_features[row_count - rim :], "node", to_right)
+    feat_right = lax.ppermute(flat_features[:rim], "node", to_left)
+    order_one = first_product(band_tiles, feat_left, flat_features, feat_right)
+    one_left = lax.ppermute(order_one[row_count - rim :], "node", to_right)
+    one_right = lax.ppermute(order_one[:rim], "node", to_left)
+    result = second_product(
+        band_tiles, one_left, order_one, one_right, flat_features, cheb_weight, cheb_bias
+    )
+    return result.reshape(row_count, steps_dev, chan_out)
 
 
 def solution(mesh):

time: 58 us -> 59.6 us (1.028)
  Pallas kernels: 0 us -> 10.5 us
  matrix products: 9.35 us -> 2.68 us
  other arithmetic: 5.44 us -> 2.55 us
  local copies, waits for them, and re-layouts: 6.86 us -> 8.94 us
  waiting for transfers between devices: 20.7 us -> 19.5 us
    pallas_call x0 -> x2, Pallas kernels: none -> 10.5 us  [the longest x1 6.28 us: second_product(): pl.pallas_call(_second_kernel, out_shape=jax.ShapeDtypeStruct((rows, widt...]
    dot_general x11 -> x0, matrix products: 6.67 us -> none  [the longest x8 3.96 us: band_product(): jnp.einsum('bpq,bqf->bpf', band_tiles[:, offset], extended[offset:offset...]
    ppermute x4, waiting for transfers between devices: 19.5 us -> 15.4 us  [the longest x1 7.43 us: shards(): feat_right = lax.ppermute(flat_features[:rim], 'node', to_left)]
    concatenate x2 -> x1, other arithmetic: 3.42 us -> 0.12 us  [shards(): flat_features = jnp.concatenate(pieces, axis=1).astype(jnp.bfloat16)]
    ppermute x1, waiting for transfers between devices: 1.19 us -> 4.09 us  [passed_along(): return lax.ppermute(value, axis, pairs)]
    slice x4 -> x3, local copies, waits for them, and re-layouts: 3.07 us -> 1.13 us  [the longest x1 1.06 us: shards(): one_right = lax.ppermute(order_one[:rim], 'node', to_left)]
    dot_general x0 -> x1, local copies, waits for them, and re-layouts: none -> 1.47 us  [build_band(): jnp.einsum('bjo,bjpq->bopq', one_hot.astype(jnp.bfloat16), tile_set, pref...]
    unnamed x16 -> x15, local copies, waits for them, and re-layouts: 0.15 us -> 1.5 us
  transfers between devices with their start and end apart: 5 -> 5, of which waited for: 5 -> 5; matrix products, arithmetic and copies ran while one was open for 14% -> 12% of each run, Pallas kernels for 0% -> 0%
where the time goes in v4:
time: 59.6 us; the launch traced here: 59.1 us
  waiting for transfers between devices  19.5 us (33%)
  starting transfers between devices  14.8 us (25%)
  Pallas kernels  10.5 us (18%)
  local copies, waits for them, and re-layouts  8.94 us (15%)
  matrix products  2.68 us (4%)
  other arithmetic  2.55 us (4%)
    ppermute x1, waiting for transfers between devices, shards(): feat_right = lax.ppermute(flat_features[:rim], 'node', to_left)  7.43 us
    pallas_call x1, Pallas kernels, second_product(): pl.pallas_call(_second_kernel, out_shape=jax.ShapeDtypeStruct((rows, widt...  6.28 us
    ppermute x1, waiting for transfers between devices, shards(): one_right = lax.ppermute(order_one[:rim], 'node', to_left)  5.25 us
    ppermute x1, starting transfers between devices, shards(): feat_left = lax.ppermute(flat_features[row_count - rim:], 'node', to_right)  4.95 us
    pallas_call x1, Pallas kernels, first_product(): pl.pallas_call(_first_kernel, out_shape=jax.ShapeDtypeStruct((rows, width...  4.21 us
    ppermute x1, waiting for transfers between devices, passed_along(): return lax.ppermute(value, axis, pairs)  4.09 us
    ppermute x1, starting transfers between devices, shards(): one_right = lax.ppermute(order_one[:rim], 'node', to_left)  3.92 us
    ppermute x1, waiting for transfers between devices, shards(): one_left = lax.ppermute(order_one[row_count - rim:], 'node', to_right)  2.43 us
  transfers between devices with their start and end apart: 5, of which 5 were waited for; matrix products, arithmetic and copies ran while one was open for 12% of the time, Pallas kernels for 0%

profile of v4, /device:TPU:110, one launch (start us, length us, event | category | flops | bytes accessed | tf_op | source)
XLA Modules:
  0.0 59.1 jit_solution(16427284967559498203)
XLA Ops:
  0.0 2.0 %collective-permute-start = (bf16[1024,256]{1,0:T(8,128)(2,1)}, bf16[1024,256]{1,0:T(8,128)(2,1)S(1)}, u32[]{:S(2)}, u32[]{:S(2)}) collective-permute-start(bf16[1024,256]{1,0:T(8,128)(2,1)} %param.8), channel_id=1, source_target_pairs={{0,32},{32,64},{64,96},{96,128},{128,160},{160,192},{192,224},{1,3... | collective-permute-start | bytes 1572872 | tf_op jit(solution)/shard_map/ppermute | solution.py:32
  2.1 0.8 %slice_bitcast_fusion.2 = (bf16[64,256]{1,0:T(8,128)(2,1)S(1)}, bf16[64,256]{1,0:T(8,128)(2,1)S(1)}, bf16[64,256]{1,0:T(8,128)(2,1)S(1)}) fusion(bf16[3,64,256]{2,1,0:T(8,128)(2,1)} %param.9), kind=kLoop, calls=%fused_computation.60 | loop fusion | bytes 196608 | tf_op jit(solution)/shard_map/jit(kron)/mul | solution.py:150
  2.9 0.8 %fusion.56 = (f32[128]{0:T(128)S(1)}, f32[128]{0:T(128)S(1)}) fusion(f32[256]{0:T(256)} %param.10), kind=kLoop, calls=%fused_computation.83 | loop fusion | bytes 2048 | tf_op jit(solution)/shard_map/slice | solution.py:184
  3.6 0.7 %iota_compare_fusion.2 = pred[8,4]{1,0:T(8,128)(4,1)S(1)} fusion(s32[8]{0:T(128)} %param.13), kind=kLoop, calls=%fused_computation.66 | loop fusion | flops 32 | bytes 64 | tf_op jit(solution)/shard_map/lt | solution.py:39
  4.4 0.7 %subtract_add_fusion = s32[8,4]{0,1:T(4,128)S(1)} fusion(s32[8,4]{0,1:T(4,128)} %param.12, s32[8]{0:T(128)S(1)} %iota_add_fusion), kind=kLoop, calls=%fused_computation.67 | loop fusion | flops 64 | bytes 288 | tf_op jit(solution)/shard_map/add | solution.py:38
  5.7 1.1 %fusion.55 = (bf16[1024,128]{1,0:T(8,128)(2,1)S(1)}, bf16[1024,128]{1,0:T(8,128)(2,1)S(1)}) fusion(bf16[1024,256]{1,0:T(8,128)(2,1)} %param.8), kind=kLoop, calls=%fused_computation.82 | loop fusion | bytes 1048576 | tf_op jit(solution)/shard_map/slice | solution.py:177
  6.7 4.1 %collective-permute-done = bf16[1024,256]{1,0:T(8,128)(2,1)S(1)} collective-permute-done((bf16[1024,256]{1,0:T(8,128)(2,1)}, bf16[1024,256]{1,0:T(8,128)(2,1)S(1)}, u32[]{:S(2)}, u32[]{:S(2)}) %collective-permute-start) | collective-permute-done | bytes 524320 | tf_op jit(solution)/shard_map/ppermute | solution.py:32
  10.9 0.7 %fusion = f32[1024,512]{1,0:T(8,128)S(1)} fusion(bf16[1024,128]{1,0:T(8,128)(2,1)S(1)} %get-tuple-element.15, bf16[1024,128]{1,0:T(8,128)(2,1)S(1)} %get-tuple-element.13, bf16[1024,128]{1,0:T(8,128)(2,1)S(1)} %get-tuple-element.14, bf16[128,512]{1,0:T(8,128)(2,1)S(1)} %fusion.42, bf16[128,512]{1,0:T(8,128)(2,1)S(1)} %bitcast.29, ...), kind=kOutput, calls=%fused_computation.1 | convolution fusion | flops 543162368 | bytes 3407872 | tf_op jit(solution)/shard_map/dot_general | solution.py:181
  11.6 0.7 %fusion.8 = f32[1024,512]{1,0:T(8,128)S(1)} fusion(bf16[1024,128]{1,0:T(8,128)(2,1)S(1)} %get-tuple-element.16, bf16[1024,128]{1,0:T(8,128)(2,1)S(1)} %get-tuple-element.14, bf16[1024,128]{1,0:T(8,128)(2,1)S(1)} %get-tuple-element.15, bf16[128,512]{1,0:T(8,128)(2,1)S(1)} %fusion.42, bf16[128,512]{1,0:T(8,128)(2,1)S(1)} %bitcast.30, ...), kind=kOutput, calls=%fused_computation.9 | convolution fusion | flops 543162368 | bytes 3407872 | tf_op jit(solution)/shard_map/dot_general | solution.py:181
  13.0 4.9 %collective-permute-start.1 = (bf16[256,512]{1,0:T(8,128)(2,1)S(1)}, bf16[256,512]{1,0:T(8,128)(2,1)S(1)}, u32[]{:S(2)}, u32[]{:S(2)}) collective-permute-start(bf16[256,512]{1,0:T(8,128)(2,1)S(1)} %get-tuple-element.12), channel_id=1, source_target_pairs={{0,1},{1,2},{2,3},{3,4},{4,5},{5,6},{6,7},{7,8},{8,9},{9,10},{10,1... | collective-permute-start | bytes 786440 | tf_op jit(solution)/shard_map/ppermute | solution.py:195
  18.0 1.9 %collective-permute-start.2 = (bf16[256,512]{1,0:T(8,128)(2,1)S(1)}, bf16[256,512]{1,0:T(8,128)(2,1)S(1)}, u32[]{:S(2)}, u32[]{:S(2)}) collective-permute-start(bf16[256,512]{1,0:T(8,128)(2,1)S(1)} %get-tuple-element.11), channel_id=1, source_target_pairs={{1,0},{2,1},{3,2},{4,3},{5,4},{6,5},{7,6},{8,7},{9,8},{10,9},{11,1... | collective-permute-start | bytes 786440 | tf_op jit(solution)/shard_map/ppermute | solution.py:196
  19.9 1.3 %fusion.16 = bf16[8,5,128,128]{3,1,2,0:T(8,128)(2,1)S(1)} fusion(bf16[8,4,128,128]{3,2,1,0:T(8,128)(2,1)S(1)} %copy-done, s32[8,4]{1,0:T(8,128)S(1)} %copy.9, pred[8,4]{1,0:T(8,128)(4,1)S(1)} %iota_compare_fusion.2), kind=kOutput, calls=%fused_computation.18 | convolution fusion | flops 5243200 | bytes 2359456 | tf_op jit(solution)/shard_map/bjo,bjpq->bopq/dot_general | solution.py:43
  21.2 1.5 %copy.29.band_ref = bf16[8,5,128,128]{3,2,1,0:T(8,128)(2,1)} copy(bf16[8,5,128,128]{3,1,2,0:T(8,128)(2,1)S(1)} %fusion.16) | data formatting | bytes 2621440 | tf_op jit(solution)/shard_map/bjo,bjpq->bopq/dot_general | solution.py:43
  23.0 7.4 %collective-permute-done.2.right_ref = bf16[256,512]{1,0:T(8,128)(2,1)S(1)} collective-permute-done((bf16[256,512]{1,0:T(8,128)(2,1)S(1)}, bf16[256,512]{1,0:T(8,128)(2,1)S(1)}, u32[]{:S(2)}, u32[]{:S(2)}) %collective-permute-start.2) | collective-permute-done | bytes 262176 | tf_op jit(solution)/shard_map/ppermute | solution.py:196
  30.5 0.7 %copy-done.4 = bf16[256,512]{1,0:T(8,128)(2,1)} copy-done((bf16[256,512]{1,0:T(8,128)(2,1)}, bf16[256,512]{1,0:T(8,128)(2,1)S(1)}, u32[]{:S(2)}) %copy-start.4) | copy-done | bytes 262168
  31.2 4.2 %shard_map.82.own_ref = bf16[1024,512]{1,0:T(8,128)(2,1)} custom-call(bf16[8,5,128,128]{3,2,1,0:T(8,128)(2,1)} %copy.29.band_ref, bf16[256,512]{1,0:T(8,128)(2,1)} %copy-done.2, bf16[1024,512]{1,0:T(8,128)(2,1)} %copy-done.1, bf16[256,512]{1,0:T(8,128)(2,1)} %copy-done.4), custom_call_target="tpu_custom_call" | custom-call | flops 671088640 | bytes 3145728 | tf_op jit(solution)/shard_map/pallas_call | solution.py:119
  35.4 1.1 %fusion.52 = (bf16[256,512]{1,0:T(8,128)(2,1)S(1)}, bf16[256,512]{1,0:T(8,128)(2,1)S(1)}) fusion(bf16[1024,512]{1,0:T(8,128)(2,1)} %shard_map.82.own_ref), kind=kLoop, calls=%fused_computation.79 | loop fusion | bytes 1048576 | tf_op jit(solution)/shard_map/slice | solution.py:199
  36.5 1.9 %collective-permute-start.3 = (bf16[256,512]{1,0:T(8,128)(2,1)S(1)}, bf16[256,512]{1,0:T(8,128)(2,1)S(1)}, u32[]{:S(2)}, u32[]{:S(2)}) collective-permute-start(bf16[256,512]{1,0:T(8,128)(2,1)S(1)} %get-tuple-element.10), channel_id=1, source_target_pairs={{0,1},{1,2},{2,3},{3,4},{4,5},{5,6},{6,7},{7,8},{8,9},{9,10},{10,1... | collective-permute-start | bytes 786440 | tf_op jit(solution)/shard_map/ppermute | solution.py:198
  38.4 3.9 %collective-permute-start.4 = (bf16[256,512]{1,0:T(8,128)(2,1)S(1)}, bf16[256,512]{1,0:T(8,128)(2,1)S(1)}, u32[]{:S(2)}, u32[]{:S(2)}) collective-permute-start(bf16[256,512]{1,0:T(8,128)(2,1)S(1)} %get-tuple-element.9), channel_id=1, source_target_pairs={{1,0},{2,1},{3,2},{4,3},{5,4},{6,5},{7,6},{8,7},{9,8},{10,9},{11,1... | collective-permute-start | bytes 786440 | tf_op jit(solution)/shard_map/ppermute | solution.py:199
  42.3 2.4 %collective-permute-done.3.left_ref = bf16[256,512]{1,0:T(8,128)(2,1)S(1)} collective-permute-done((bf16[256,512]{1,0:T(8,128)(2,1)S(1)}, bf16[256,512]{1,0:T(8,128)(2,1)S(1)}, u32[]{:S(2)}, u32[]{:S(2)}) %collective-permute-start.3) | collective-permute-done | bytes 262176 | tf_op jit(solution)/shard_map/ppermute | solution.py:198
  44.8 5.2 %collective-permute-done.4.right_ref = bf16[256,512]{1,0:T(8,128)(2,1)S(1)} collective-permute-done((bf16[256,512]{1,0:T(8,128)(2,1)S(1)}, bf16[256,512]{1,0:T(8,128)(2,1)S(1)}, u32[]{:S(2)}, u32[]{:S(2)}) %collective-permute-start.4) | collective-permute-done | bytes 262176 | tf_op jit(solution)/shard_map/ppermute | solution.py:199
  50.0 0.7 %copy-done.5 = bf16[256,512]{1,0:T(8,128)(2,1)} copy-done((bf16[256,512]{1,0:T(8,128)(2,1)}, bf16[256,512]{1,0:T(8,128)(2,1)S(1)}, u32[]{:S(2)}) %copy-start.5) | copy-done | bytes 262168
  50.7 6.3 %shard_map.83 = bf16[1024,512]{1,0:T(8,128)(2,1)} custom-call(bf16[8,5,128,128]{3,2,1,0:T(8,128)(2,1)} %copy.29.band_ref, bf16[256,512]{1,0:T(8,128)(2,1)} %copy-done.3, bf16[1024,512]{1,0:T(8,128)(2,1)} %shard_map.82.own_ref, bf16[256,512]{1,0:T(8,128)(2,1)} %copy-done.5, bf16[1024,512]{1,0:T(8,128)(2,1)} %copy-done.1, bf16[384,128]{1,0:T(8,128)(2,1)} %bitcast.31, ...), custom_call_target="tpu_custom_call" | custom-call | flops 1073741824 | bytes 4194304 | tf_op jit(solution)/shard_map/pallas_call | solution.py:134
  57.0 2.1 %reshape.121 = bf16[1024,4,128]{2,1,0:T(4,128)(2,1)} reshape(bf16[1024,512]{1,0:T(8,128)(2,1)} %shard_map.83) | data formatting | bytes 2097152 | tf_op jit(solution)/shard_map/reshape | solution.py:203
  (24 shorter events, 1.7 us)
Async XLA Ops:
  0.0 19.9 %copy-start = (bf16[8,4,128,128]{3,2,1,0:T(8,128)(2,1)S(1)}, bf16[8,4,128,128]{3,2,1,0:T(8,128)(2,1)}, u32[]{:S(2)}) copy-start(bf16[8,4,128,128]{3,2,1,0:T(8,128)(2,1)} %param.11) | copy-start | bytes 3145732
  0.0 10.8 %collective-permute-start = (bf16[1024,256]{1,0:T(8,128)(2,1)}, bf16[1024,256]{1,0:T(8,128)(2,1)S(1)}, u32[]{:S(2)}, u32[]{:S(2)}) collective-permute-start(bf16[1024,256]{1,0:T(8,128)(2,1)} %param.8), channel_id=1, source_target_pairs={{0,32},{32,64},{64,96},{96,128},{128,160},{160,192},{192,224},{1,3... | collective-permute-start | bytes 1572872 | tf_op jit(solution)/shard_map/ppermute | solution.py:32
  13.0 8.2 %copy-start.1 = (bf16[1024,512]{1,0:T(8,128)(2,1)}, bf16[1024,512]{1,0:T(8,128)(2,1)S(1)}, u32[]{:S(2)}) copy-start(bf16[1024,512]{1,0:T(8,128)(2,1)S(1)} %pad_maximum_fusion.own_ref.feat_ref) | copy-start | bytes 3145732
  13.0 10.0 %collective-permute-start.1 = (bf16[256,512]{1,0:T(8,128)(2,1)S(1)}, bf16[256,512]{1,0:T(8,128)(2,1)S(1)}, u32[]{:S(2)}, u32[]{:S(2)}) collective-permute-start(bf16[256,512]{1,0:T(8,128)(2,1)S(1)} %get-tuple-element.12), channel_id=1, source_target_pairs={{0,1},{1,2},{2,3},{3,4},{4,5},{5,6},{6,7},{7,8},{8,9},{9,10},{10,1... | collective-permute-start | bytes 786440 | tf_op jit(solution)/shard_map/ppermute | solution.py:195
  18.0 12.5 %collective-permute-start.2 = (bf16[256,512]{1,0:T(8,128)(2,1)S(1)}, bf16[256,512]{1,0:T(8,128)(2,1)S(1)}, u32[]{:S(2)}, u32[]{:S(2)}) collective-permute-start(bf16[256,512]{1,0:T(8,128)(2,1)S(1)} %get-tuple-element.11), channel_id=1, source_target_pairs={{1,0},{2,1},{3,2},{4,3},{5,4},{6,5},{7,6},{8,7},{9,8},{10,9},{11,1... | collective-permute-start | bytes 786440 | tf_op jit(solution)/shard_map/ppermute | solution.py:196
  23.0 7.4 %copy-start.2 = (bf16[256,512]{1,0:T(8,128)(2,1)}, bf16[256,512]{1,0:T(8,128)(2,1)S(1)}, u32[]{:S(2)}) copy-start(bf16[256,512]{1,0:T(8,128)(2,1)S(1)} %collective-permute-done.1.left_ref) | copy-start | bytes 786436
  30.5 0.7 %copy-start.4 = (bf16[256,512]{1,0:T(8,128)(2,1)}, bf16[256,512]{1,0:T(8,128)(2,1)S(1)}, u32[]{:S(2)}) copy-start(bf16[256,512]{1,0:T(8,128)(2,1)S(1)} %collective-permute-done.2.right_ref) | copy-start | bytes 786436
  36.5 8.3 %collective-permute-start.3 = (bf16[256,512]{1,0:T(8,128)(2,1)S(1)}, bf16[256,512]{1,0:T(8,128)(2,1)S(1)}, u32[]{:S(2)}, u32[]{:S(2)}) collective-permute-start(bf16[256,512]{1,0:T(8,128)(2,1)S(1)} %get-tuple-element.10), channel_id=1, source_target_pairs={{0,1},{1,2},{2,3},{3,4},{4,5},{5,6},{6,7},{7,8},{8,9},{9,10},{10,1... | collective-permute-start | bytes 786440 | tf_op jit(solution)/shard_map/ppermute | solution.py:198
  38.4 11.6 %collective-permute-start.4 = (bf16[256,512]{1,0:T(8,128)(2,1)S(1)}, bf16[256,512]{1,0:T(8,128)(2,1)S(1)}, u32[]{:S(2)}, u32[]{:S(2)}) collective-permute-start(bf16[256,512]{1,0:T(8,128)(2,1)S(1)} %get-tuple-element.9), channel_id=1, source_target_pairs={{1,0},{2,1},{3,2},{4,3},{5,4},{6,5},{7,6},{8,7},{9,8},{10,9},{11,1... | collective-permute-start | bytes 786440 | tf_op jit(solution)/shard_map/ppermute | solution.py:199
  44.8 5.3 %copy-start.3 = (bf16[256,512]{1,0:T(8,128)(2,1)}, bf16[256,512]{1,0:T(8,128)(2,1)S(1)}, u32[]{:S(2)}) copy-start(bf16[256,512]{1,0:T(8,128)(2,1)S(1)} %collective-permute-done.3.left_ref) | copy-start | bytes 786436
  50.0 0.7 %copy-start.5 = (bf16[256,512]{1,0:T(8,128)(2,1)}, bf16[256,512]{1,0:T(8,128)(2,1)S(1)}, u32[]{:S(2)}) copy-start(bf16[256,512]{1,0:T(8,128)(2,1)S(1)} %collective-permute-done.4.right_ref) | copy-start | bytes 786436

commit v5 on v4

--- a/solution.py
+++ b/solution.py
@@ -37,13 +37,12 @@
     row_ids = first_block + jnp.arange(block_count, dtype=jnp.int32)
     offset = col_ids - row_ids[:, None] + HB
     live_mask = jnp.arange(TPB, dtype=jnp.int32)[None, :] < live_count[:, None]
-    one_hot = (
-        offset[:, :, None] == jnp.arange(2 * HB + 1, dtype=jnp.int32)[None, None, :]
-    ) & live_mask[:, :, None]
-    band_tiles = jnp.einsum(
-        "bjo,bjpq->bopq", one_hot.astype(jnp.bfloat16), tile_set, preferred_element_type=jnp.float32
-    )
-    return band_tiles.astype(jnp.bfloat16)
+    tiles = tile_set.astype(jnp.float32)
+    parts = []
+    for o in range(2 * HB + 1):
+        pick = ((offset == o) & live_mask).astype(jnp.float32)
+        parts.append(jnp.sum(pick[:, :, None, None] * tiles, axis=1))
+    return jnp.concatenate(parts, axis=2).astype(jnp.bfloat16)
 
 
 def band_product(band_tiles, extended):
@@ -64,49 +63,46 @@
     return total
 
 
-def _source(b, o, nb, left_ref, own_ref, right_ref, rows):
-    j = b + o - HB
-    if j < 0:
-        return left_ref, (j + HB) * rows
-    if j >= nb:
-        return right_ref, (j - nb) * rows
-    return own_ref, j * rows
-
-
-def _band_sum(b, band_ref, left_ref, own_ref, right_ref):
-    nb = band_ref.shape[0]
-    rows = band_ref.shape[2]
-    acc = None
-    for o in range(2 * HB + 1):
-        src, r0 = _source(b, o, nb, left_ref, own_ref, right_ref, rows)
-        term = jnp.dot(band_ref[b, o], src[r0 : r0 + rows, :], preferred_element_type=jnp.float32)
-        acc = term if acc is None else acc + term
-    return acc
-
-
-def _first_kernel(band_ref, left_ref, own_ref, right_ref, out_ref):
-    nb, rows = band_ref.shape[0], band_ref.shape[2]
+def _assemble(ext_ref, left_ref, own_ref, right_ref):
+    rim = left_ref.shape[0]
+    rows = own_ref.shape[0]
+    ext_ref[0:rim, :] = left_ref[...]
+    ext_ref[rim : rim + rows, :] = own_ref[...]
+    ext_ref[rim + rows : 2 * rim + rows, :] = right_ref[...]
+
+
+def _band_block(b, band_ref, ext_ref):
+    rows = band_ref.shape[1]
+    reach = band_ref.shape[2]
+    return jnp.dot(
+        band_ref[b], ext_ref[b * rows : b * rows + reach, :], preferred_element_type=jnp.float32
+    )
+
+
+def _first_kernel(band_ref, left_ref, own_ref, right_ref, out_ref, ext_ref):
+    nb, rows = band_ref.shape[0], band_ref.shape[1]
+    _assemble(ext_ref, left_ref, own_ref, right_ref)
     for b in range(nb):
-        acc = _band_sum(b, band_ref, left_ref, own_ref, right_ref)
-        out_ref[b * rows : (b + 1) * rows, :] = acc.astype(out_ref.dtype)
-
-
-def _second_kernel(band_ref, left_ref, own_ref, right_ref, feat_ref, weight_ref, bias_ref, out_ref):
-    nb, rows = band_ref.shape[0], band_ref.shape[2]
+        out_ref[b * rows : (b + 1) * rows, :] = _band_block(b, band_ref, ext_ref).astype(out_ref.dtype)
+
+
+def _second_kernel(
+    band_ref, left_ref, own_ref, right_ref, feat_ref, weight_ref, bias_ref, out_ref, ext_ref, two_ref
+):
+    nb, rows = band_ref.shape[0], band_ref.shape[1]
     chan = weight_ref.shape[1]
     steps = own_ref.shape[1] // chan
+    _assemble(ext_ref, left_ref, own_ref, right_ref)
+    for b in range(nb):
+        lo, hi = b * rows, (b + 1) * rows
+        acc = _band_block(b, band_ref, ext_ref)
+        two_ref[lo:hi, :] = (2.0 * acc - feat_ref[lo:hi, :].astype(jnp.float32)).astype(two_ref.dtype)
     bias = bias_ref[...]
-    for b in range(nb):
-        acc = _band_sum(b, band_ref, left_ref, own_ref, right_ref)
-        lo, hi = b * rows, (b + 1) * rows
-        feat = feat_ref[lo:hi, :]
-        cheb_two = (2.0 * acc - feat.astype(jnp.float32)).astype(jnp.bfloat16)
-        one = own_ref[lo:hi, :]
-        for t in range(steps):
-            cols = slice(t * chan, (t + 1) * chan)
-            joined = jnp.concatenate([feat[:, cols], one[:, cols], cheb_two[:, cols]], axis=1)
-            res = jnp.dot(joined, weight_ref[...], preferred_element_type=jnp.float32) + bias
-            out_ref[lo:hi, cols] = jnp.maximum(res, 0.0).astype(out_ref.dtype)
+    for t in range(steps):
+        cols = slice(t * chan, (t + 1) * chan)
+        joined = jnp.concatenate([feat_ref[:, cols], own_ref[:, cols], two_ref[:, cols]], axis=1)
+        res = jnp.dot(joined, weight_ref[...], preferred_element_type=jnp.float32) + bias
+        out_ref[:, cols] = jnp.maximum(res, 0.0).astype(out_ref.dtype)
 
 
 def _vmem_specs(count):
@@ -115,12 +111,13 @@
 
 def first_product(band_tiles, left, own, right):
     rows, width = own.shape
-    flops = 2 * band_tiles.shape[0] * (2 * HB + 1) * band_tiles.shape[2] ** 2 * width
+    flops = 2 * band_tiles.shape[0] * band_tiles.shape[1] * band_tiles.shape[2] * width
     return pl.pallas_call(
         _first_kernel,
         out_shape=jax.ShapeDtypeStruct((rows, width), jnp.bfloat16),
         in_specs=_vmem_specs(4),
         out_specs=pl.BlockSpec(memory_space=pltpu.VMEM),
+        scratch_shapes=[pltpu.VMEM((rows + 2 * left.shape[0], width), own.dtype)],
         cost_estimate=pl.CostEstimate(flops=flops, transcendentals=0, bytes_accessed=6 * rows * width),
     )(band_tiles, left, own, right)
 
@@ -129,16 +126,19 @@
     rows, width = own.shape
     weight = cheb_weight.reshape(-1, cheb_weight.shape[2])
     bias = cheb_bias.reshape(1, -1)
-    flops = 2 * band_tiles.shape[0] * (2 * HB + 1) * band_tiles.shape[2] ** 2 * width
+    flops = 2 * band_tiles.shape[0] * band_tiles.shape[1] * band_tiles.shape[2] * width
     flops += 2 * rows * width * weight.shape[0]
     return pl.pallas_call(
         _second_kernel,
         out_shape=jax.ShapeDtypeStruct((rows, width), jnp.bfloat16),
         in_specs=_vmem_specs(7),
         out_specs=pl.BlockSpec(memory_space=pltpu.VMEM),
+        scratch_shapes=[
+            pltpu.VMEM((rows + 2 * left.shape[0], width), own.dtype),
+            pltpu.VMEM((rows, width), jnp.bfloat16),
+        ],
         cost_estimate=pl.CostEstimate(flops=flops, transcendentals=0, bytes_accessed=8 * rows * width),
     )(band_tiles, left, own, right, features, weight, bias)
-
 
 def fetch_rim(values, block_rows):
     return with_halo(values, (("node", 0),), HB * block_rows)

time: 59.6 us -> 58.3 us (0.978)
  the two profiles are of different devices: /device:TPU:110 before, /device:TPU:103 now
where the time goes in v5:
time: 58.3 us; the launch traced here: 57.8 us
  waiting for transfers between devices  20.4 us (35%)
  starting transfers between devices  15.6 us (27%)
  Pallas kernels  8.61 us (15%)
  local copies, waits for them, and re-layouts  7.03 us (12%)
  other arithmetic  4.52 us (8%)
  matrix products  1.41 us (2%)
    ppermute x1, waiting for transfers between devices, shards(): feat_right = lax.ppermute(flat_features[:rim], 'node', to_left)  7.42 us
    ppermute x1, waiting for transfers between devices, shards(): one_right = lax.ppermute(order_one[:rim], 'node', to_left)  5.25 us
    pallas_call x1, Pallas kernels, second_product(): pl.pallas_call(_second_kernel, out_shape=jax.ShapeDtypeStruct((rows, widt...  4.92 us
    ppermute x1, starting transfers between devices, shards(): feat_left = lax.ppermute(flat_features[row_count - rim:], 'node', to_right)  4.67 us
    ppermute x1, waiting for transfers between devices, shards(): one_left = lax.ppermute(order_one[row_count - rim:], 'node', to_right)  4.65 us
    ppermute x1, starting transfers between devices, passed_along(): return lax.ppermute(value, axis, pairs)  3.76 us
    pallas_call x1, Pallas kernels, first_product(): pl.pallas_call(_first_kernel, out_shape=jax.ShapeDtypeStruct((rows, width...  3.69 us
    ppermute x1, starting transfers between devices, shards(): one_right = lax.ppermute(order_one[:rim], 'node', to_left)  3.36 us
  transfers between devices with their start and end apart: 5, of which 5 were waited for; matrix products, arithmetic and copies ran while one was open for 11% of the time, Pallas kernels for 0%

profile of v5, /device:TPU:103, one launch (start us, length us, event | category | flops | bytes accessed | tf_op | source)
XLA Modules:
  0.0 57.8 jit_solution(12395825906093921212)
XLA Ops:
  0.0 3.8 %collective-permute-start = (bf16[1024,256]{1,0:T(8,128)(2,1)}, bf16[1024,256]{1,0:T(8,128)(2,1)S(1)}, u32[]{:S(2)}, u32[]{:S(2)}) collective-permute-start(bf16[1024,256]{1,0:T(8,128)(2,1)} %param.8), channel_id=1, source_target_pairs={{0,32},{32,64},{64,96},{96,128},{128,160},{160,192},{192,224},{1,3... | collective-permute-start | bytes 1572872 | tf_op jit(solution)/shard_map/ppermute | solution.py:32
  3.8 0.8 %slice_bitcast_fusion.2 = (bf16[64,256]{1,0:T(8,128)(2,1)S(1)}, bf16[64,256]{1,0:T(8,128)(2,1)S(1)}, bf16[64,256]{1,0:T(8,128)(2,1)S(1)}) fusion(bf16[3,64,256]{2,1,0:T(8,128)(2,1)} %param.9), kind=kLoop, calls=%fused_computation.72 | loop fusion | bytes 196608 | tf_op jit(solution)/shard_map/jit(kron)/mul | solution.py:150
  4.6 0.8 %fusion.64 = (f32[128]{0:T(128)S(1)}, f32[128]{0:T(128)S(1)}) fusion(f32[256]{0:T(256)} %param.10), kind=kLoop, calls=%fused_computation.100 | loop fusion | bytes 2048 | tf_op jit(solution)/shard_map/slice | solution.py:184
  5.3 0.7 %fusion.51 = (f32[8,4]{0,1:T(4,128)S(1)}, f32[8,4]{0,1:T(4,128)S(1)}, f32[8,4]{0,1:T(4,128)S(1)}, f32[8,4]{0,1:T(4,128)S(1)}, f32[8,4]{0,1:T(4,128)S(1)}) fusion(s32[8]{0:T(128)} %param.13, s32[8,4]{0,1:T(4,128)} %param.12, s32[8]{0:T(128)S(1)} %iota_add_fusion), kind=kLoop, calls=%fused_computation.80 | loop fusion | flops 576 | bytes 832 | tf_op jit(solution)/shard_map/convert_element_type | solution.py:43
  6.5 2.7 %fusion.4 = (bf16[8,128,128]{2,1,0:T(8,128)(2,1)S(1)}, bf16[8,128,128]{2,1,0:T(8,128)(2,1)S(1)}, bf16[8,128,128]{2,1,0:T(8,128)(2,1)S(1)}, bf16[8,128,128]{2,1,0:T(8,128)(2,1)S(1)}, bf16[8,128,128]{2,1,0:T(8,128)(2,1)S(1)}) fusion(bf16[8,4,128,128]{3,2,1,0:T(8,128)(2,1)} %param.11, f32[8,4]{1,0:T(8,128)S(1)} %copy.13, f32[8,4]{1,0:T(8,128)S(1)} %copy.10, ...), kind=kLoop, calls=%fused_computation.9 | loop fusion | flops 5111808 | bytes 2359936 | tf_op jit(solution)/shard_map/reduce_sum | solution.py:44
  9.3 0.4 broadcast_multiply_fusion.2
  9.9 0.3 collective-permute-done
  10.2 0.7 %fusion.5 = f32[1024,512]{1,0:T(8,128)S(1)} fusion(bf16[1024,128]{1,0:T(8,128)(2,1)S(1)} %get-tuple-element.20, bf16[1024,128]{1,0:T(8,128)(2,1)S(1)} %get-tuple-element.18, bf16[1024,128]{1,0:T(8,128)(2,1)S(1)} %get-tuple-element.19, bf16[128,512]{1,0:T(8,128)(2,1)S(1)} %fusion.45, bf16[128,512]{1,0:T(8,128)(2,1)S(1)} %bitcast.22, ...), kind=kOutput, calls=%fused_computation.10 | convolution fusion | flops 543162368 | bytes 3407872 | tf_op jit(solution)/shard_map/dot_general | solution.py:181
  10.9 0.7 %fusion.13 = f32[1024,512]{1,0:T(8,128)S(1)} fusion(bf16[1024,128]{1,0:T(8,128)(2,1)S(1)} %get-tuple-element.21, bf16[1024,128]{1,0:T(8,128)(2,1)S(1)} %get-tuple-element.19, bf16[1024,128]{1,0:T(8,128)(2,1)S(1)} %get-tuple-element.20, bf16[128,512]{1,0:T(8,128)(2,1)S(1)} %fusion.45, bf16[128,512]{1,0:T(8,128)(2,1)S(1)} %bitcast.23, ...), kind=kOutput, calls=%fused_computation.18 | convolution fusion | flops 543162368 | bytes 3407872 | tf_op jit(solution)/shard_map/dot_general | solution.py:181
  11.6 0.6 fusion.41
  12.4 4.7 %collective-permute-start.1 = (bf16[256,512]{1,0:T(8,128)(2,1)S(1)}, bf16[256,512]{1,0:T(8,128)(2,1)S(1)}, u32[]{:S(2)}, u32[]{:S(2)}) collective-permute-start(bf16[256,512]{1,0:T(8,128)(2,1)S(1)} %get-tuple-element.17), channel_id=1, source_target_pairs={{0,1},{1,2},{2,3},{3,4},{4,5},{5,6},{6,7},{7,8},{8,9},{9,10},{10,1... | collective-permute-start | bytes 786440 | tf_op jit(solution)/shard_map/ppermute | solution.py:195
  17.1 1.9 %collective-permute-start.2 = (bf16[256,512]{1,0:T(8,128)(2,1)S(1)}, bf16[256,512]{1,0:T(8,128)(2,1)S(1)}, u32[]{:S(2)}, u32[]{:S(2)}) collective-permute-start(bf16[256,512]{1,0:T(8,128)(2,1)S(1)} %get-tuple-element.16), channel_id=1, source_target_pairs={{1,0},{2,1},{3,2},{4,3},{5,4},{6,5},{7,6},{8,7},{9,8},{10,9},{11,1... | collective-permute-start | bytes 786440 | tf_op jit(solution)/shard_map/ppermute | solution.py:196
  19.2 2.8 %collective-permute-done.1.left_ref = bf16[256,512]{1,0:T(8,128)(2,1)S(1)} collective-permute-done((bf16[256,512]{1,0:T(8,128)(2,1)S(1)}, bf16[256,512]{1,0:T(8,128)(2,1)S(1)}, u32[]{:S(2)}, u32[]{:S(2)}) %collective-permute-start.1) | collective-permute-done | bytes 262176 | tf_op jit(solution)/shard_map/ppermute | solution.py:195
  22.0 7.4 %collective-permute-done.2.right_ref = bf16[256,512]{1,0:T(8,128)(2,1)S(1)} collective-permute-done((bf16[256,512]{1,0:T(8,128)(2,1)S(1)}, bf16[256,512]{1,0:T(8,128)(2,1)S(1)}, u32[]{:S(2)}, u32[]{:S(2)}) %collective-permute-start.2) | collective-permute-done | bytes 262176 | tf_op jit(solution)/shard_map/ppermute | solution.py:196
  29.4 0.7 %copy-done.4 = bf16[256,512]{1,0:T(8,128)(2,1)} copy-done((bf16[256,512]{1,0:T(8,128)(2,1)}, bf16[256,512]{1,0:T(8,128)(2,1)S(1)}, u32[]{:S(2)}) %copy-start.4) | copy-done | bytes 262168
  30.1 3.7 %shard_map.82.own_ref = bf16[1024,512]{1,0:T(8,128)(2,1)} custom-call(bf16[8,128,640]{2,1,0:T(8,128)(2,1)} %copy-done.1, bf16[256,512]{1,0:T(8,128)(2,1)} %copy-done.3, bf16[1024,512]{1,0:T(8,128)(2,1)} %copy-done, bf16[256,512]{1,0:T(8,128)(2,1)} %copy-done.4), custom_call_target="tpu_custom_call" | custom-call | flops 671088640 | bytes 3145728 | tf_op jit(solution)/shard_map/pallas_call | solution.py:115
  33.8 1.1 %fusion.60 = (bf16[256,512]{1,0:T(8,128)(2,1)S(1)}, bf16[256,512]{1,0:T(8,128)(2,1)S(1)}) fusion(bf16[1024,512]{1,0:T(8,128)(2,1)} %shard_map.82.own_ref), kind=kLoop, calls=%fused_computation.96 | loop fusion | bytes 1048576 | tf_op jit(solution)/shard_map/slice | solution.py:199
  34.9 1.9 %collective-permute-start.3 = (bf16[256,512]{1,0:T(8,128)(2,1)S(1)}, bf16[256,512]{1,0:T(8,128)(2,1)S(1)}, u32[]{:S(2)}, u32[]{:S(2)}) collective-permute-start(bf16[256,512]{1,0:T(8,128)(2,1)S(1)} %get-tuple-element.15), channel_id=1, source_target_pairs={{0,1},{1,2},{2,3},{3,4},{4,5},{5,6},{6,7},{7,8},{8,9},{9,10},{10,1... | collective-permute-start | bytes 786440 | tf_op jit(solution)/shard_map/ppermute | solution.py:198
  36.8 3.4 %collective-permute-start.4 = (bf16[256,512]{1,0:T(8,128)(2,1)S(1)}, bf16[256,512]{1,0:T(8,128)(2,1)S(1)}, u32[]{:S(2)}, u32[]{:S(2)}) collective-permute-start(bf16[256,512]{1,0:T(8,128)(2,1)S(1)} %get-tuple-element.14), channel_id=1, source_target_pairs={{1,0},{2,1},{3,2},{4,3},{5,4},{6,5},{7,6},{8,7},{9,8},{10,9},{11,1... | collective-permute-start | bytes 786440 | tf_op jit(solution)/shard_map/ppermute | solution.py:199
  40.2 4.6 %collective-permute-done.3.left_ref = bf16[256,512]{1,0:T(8,128)(2,1)S(1)} collective-permute-done((bf16[256,512]{1,0:T(8,128)(2,1)S(1)}, bf16[256,512]{1,0:T(8,128)(2,1)S(1)}, u32[]{:S(2)}, u32[]{:S(2)}) %collective-permute-start.3) | collective-permute-done | bytes 262176 | tf_op jit(solution)/shard_map/ppermute | solution.py:198
  44.8 5.2 %collective-permute-done.4.right_ref = bf16[256,512]{1,0:T(8,128)(2,1)S(1)} collective-permute-done((bf16[256,512]{1,0:T(8,128)(2,1)S(1)}, bf16[256,512]{1,0:T(8,128)(2,1)S(1)}, u32[]{:S(2)}, u32[]{:S(2)}) %collective-permute-start.4) | collective-permute-done | bytes 262176 | tf_op jit(solution)/shard_map/ppermute | solution.py:199
  50.1 0.7 %copy-done.6 = bf16[256,512]{1,0:T(8,128)(2,1)} copy-done((bf16[256,512]{1,0:T(8,128)(2,1)}, bf16[256,512]{1,0:T(8,128)(2,1)S(1)}, u32[]{:S(2)}) %copy-start.6) | copy-done | bytes 262168
  50.8 4.9 %shard_map.83 = bf16[1024,512]{1,0:T(8,128)(2,1)} custom-call(bf16[8,128,640]{2,1,0:T(8,128)(2,1)} %copy-done.1, bf16[256,512]{1,0:T(8,128)(2,1)} %copy-done.5, bf16[1024,512]{1,0:T(8,128)(2,1)} %shard_map.82.own_ref, bf16[256,512]{1,0:T(8,128)(2,1)} %copy-done.6, bf16[1024,512]{1,0:T(8,128)(2,1)} %copy-done, bf16[384,128]{1,0:T(8,128)(2,1)} %bitcast.26, ...), custom_call_target="tpu_custom_call" | custom-call | flops 1073741824 | bytes 4194304 | tf_op jit(solution)/shard_map/pallas_call | solution.py:131
  55.7 2.1 %reshape.105 = bf16[1024,4,128]{2,1,0:T(4,128)(2,1)} reshape(bf16[1024,512]{1,0:T(8,128)(2,1)} %shard_map.83) | data formatting | bytes 2097152 | tf_op jit(solution)/shard_map/reshape | solution.py:203
  (33 shorter events, 1.1 us)
Async XLA Ops:
  0.0 10.2 %collective-permute-start = (bf16[1024,256]{1,0:T(8,128)(2,1)}, bf16[1024,256]{1,0:T(8,128)(2,1)S(1)}, u32[]{:S(2)}, u32[]{:S(2)}) collective-permute-start(bf16[1024,256]{1,0:T(8,128)(2,1)} %param.8), channel_id=1, source_target_pairs={{0,32},{32,64},{64,96},{96,128},{128,160},{160,192},{192,224},{1,3... | collective-permute-start | bytes 1572872 | tf_op jit(solution)/shard_map/ppermute | solution.py:32
  6.5 3.4 %copy-start.2 = (bf16[1024,256]{1,0:T(8,128)(2,1)S(1)}, bf16[1024,256]{1,0:T(8,128)(2,1)}, u32[]{:S(2)}) copy-start(bf16[1024,256]{1,0:T(8,128)(2,1)} %param.8) | copy-start | bytes 1572868
  12.3 17.1 %copy-start = (bf16[1024,512]{1,0:T(8,128)(2,1)}, bf16[1024,512]{1,0:T(8,128)(2,1)S(1)}, u32[]{:S(2)}) copy-start(bf16[1024,512]{1,0:T(8,128)(2,1)S(1)} %pad_maximum_fusion.own_ref.feat_ref) | copy-start | bytes 3145732
  12.4 9.6 %collective-permute-start.1 = (bf16[256,512]{1,0:T(8,128)(2,1)S(1)}, bf16[256,512]{1,0:T(8,128)(2,1)S(1)}, u32[]{:S(2)}, u32[]{:S(2)}) collective-permute-start(bf16[256,512]{1,0:T(8,128)(2,1)S(1)} %get-tuple-element.17), channel_id=1, source_target_pairs={{0,1},{1,2},{2,3},{3,4},{4,5},{5,6},{6,7},{7,8},{8,9},{9,10},{10,1... | collective-permute-start | bytes 786440 | tf_op jit(solution)/shard_map/ppermute | solution.py:195
  17.1 12.4 %collective-permute-start.2 = (bf16[256,512]{1,0:T(8,128)(2,1)S(1)}, bf16[256,512]{1,0:T(8,128)(2,1)S(1)}, u32[]{:S(2)}, u32[]{:S(2)}) collective-permute-start(bf16[256,512]{1,0:T(8,128)(2,1)S(1)} %get-tuple-element.16), channel_id=1, source_target_pairs={{1,0},{2,1},{3,2},{4,3},{5,4},{6,5},{7,6},{8,7},{9,8},{10,9},{11,1... | collective-permute-start | bytes 786440 | tf_op jit(solution)/shard_map/ppermute | solution.py:196
  19.2 10.2 %copy-start.1 = (bf16[8,128,640]{2,1,0:T(8,128)(2,1)}, bf16[8,128,640]{2,1,0:T(8,128)(2,1)S(1)}, u32[]{:S(2)}) copy-start(bf16[8,128,640]{2,1,0:T(8,128)(2,1)S(1)} %convert_dynamic-update-slice_fusion.band_ref) | copy-start | bytes 3932164
  22.0 7.4 %copy-start.3 = (bf16[256,512]{1,0:T(8,128)(2,1)}, bf16[256,512]{1,0:T(8,128)(2,1)S(1)}, u32[]{:S(2)}) copy-start(bf16[256,512]{1,0:T(8,128)(2,1)S(1)} %collective-permute-done.1.left_ref) | copy-start | bytes 786436
  29.4 0.7 %copy-start.4 = (bf16[256,512]{1,0:T(8,128)(2,1)}, bf16[256,512]{1,0:T(8,128)(2,1)S(1)}, u32[]{:S(2)}) copy-start(bf16[256,512]{1,0:T(8,128)(2,1)S(1)} %collective-permute-done.2.right_ref) | copy-start | bytes 786436
  34.9 9.9 %collective-permute-start.3 = (bf16[256,512]{1,0:T(8,128)(2,1)S(1)}, bf16[256,512]{1,0:T(8,128)(2,1)S(1)}, u32[]{:S(2)}, u32[]{:S(2)}) collective-permute-start(bf16[256,512]{1,0:T(8,128)(2,1)S(1)} %get-tuple-element.15), channel_id=1, source_target_pairs={{0,1},{1,2},{2,3},{3,4},{4,5},{5,6},{6,7},{7,8},{8,9},{9,10},{10,1... | collective-permute-start | bytes 786440 | tf_op jit(solution)/shard_map/ppermute | solution.py:198
  36.8 13.3 %collective-permute-start.4 = (bf16[256,512]{1,0:T(8,128)(2,1)S(1)}, bf16[256,512]{1,0:T(8,128)(2,1)S(1)}, u32[]{:S(2)}, u32[]{:S(2)}) collective-permute-start(bf16[256,512]{1,0:T(8,128)(2,1)S(1)} %get-tuple-element.14), channel_id=1, source_target_pairs={{1,0},{2,1},{3,2},{4,3},{5,4},{6,5},{7,6},{8,7},{9,8},{10,9},{11,1... | collective-permute-start | bytes 786440 | tf_op jit(solution)/shard_map/ppermute | solution.py:199
  44.8 5.3 %copy-start.5 = (bf16[256,512]{1,0:T(8,128)(2,1)}, bf16[256,512]{1,0:T(8,128)(2,1)S(1)}, u32[]{:S(2)}) copy-start(bf16[256,512]{1,0:T(8,128)(2,1)S(1)} %collective-permute-done.3.left_ref) | copy-start | bytes 786436
  50.1 0.7 %copy-start.6 = (bf16[256,512]{1,0:T(8,128)(2,1)}, bf16[256,512]{1,0:T(8,128)(2,1)S(1)}, u32[]{:S(2)}) copy-start(bf16[256,512]{1,0:T(8,128)(2,1)S(1)} %collective-permute-done.4.right_ref) | copy-start | bytes 786436

commit v6 on v1

--- a/solution.py
+++ b/solution.py
@@ -92,43 +92,74 @@
     earlier = passed_along(inputs, "tm", 1)
     window = jnp.concatenate([earlier, inputs], axis=1)
     wpair = pair_weight(conv_weight)
-    pair_w = 2 * chan_in
-    pieces = []
-    for p in range(steps_dev // 2):
-        base = steps_dev * chan_in + p * pair_w
-        newest = window[:, base : base + pair_w]
-        middle = window[:, base - pair_w : base]
-        oldest = window[:, base - 2 * pair_w : base - pair_w]
-        lhs = jnp.concatenate([newest, middle, oldest, newest], axis=1)
-        mixed = jnp.dot(lhs, wpair, preferred_element_type=jnp.float32)
-        for tt in range(2):
-            lo = tt * 2 * chan_out
-            linear = mixed[:, lo : lo + chan_out] + conv_bias[:chan_out]
-            gate = mixed[:, lo + chan_out : lo + 2 * chan_out] + conv_bias[chan_out:]
-            pieces.append(linear * jax.nn.sigmoid(gate))
-    flat_features = jnp.concatenate(pieces, axis=1).astype(jnp.bfloat16)
+    rim = HB * block_rows
+
+    def conv(rows):
+        pair_w = 2 * chan_in
+        pieces = []
+        for p in range(steps_dev // 2):
+            base = steps_dev * chan_in + p * pair_w
+            newest = rows[:, base : base + pair_w]
+            middle = rows[:, base - pair_w : base]
+            oldest = rows[:, base - 2 * pair_w : base - pair_w]
+            lhs = jnp.concatenate([newest, middle, oldest, newest], axis=1)
+            mixed = jnp.dot(lhs, wpair, preferred_element_type=jnp.float32)
+            for tt in range(2):
+                lo = tt * 2 * chan_out
+                linear = mixed[:, lo : lo + chan_out] + conv_bias[:chan_out]
+                gate = mixed[:, lo + chan_out : lo + 2 * chan_out] + conv_bias[chan_out:]
+                pieces.append(linear * jax.nn.sigmoid(gate))
+        return jnp.concatenate(pieces, axis=1).astype(jnp.bfloat16)
+
+    node_count = lax.axis_size("node")
+    to_right = [(i, i + 1) for i in range(node_count - 1)]
+    to_left = [(i + 1, i) for i in range(node_count - 1)]
+    feat_head = conv(window[:rim])
+    feat_tail = conv(window[row_count - rim :])
+    feat_left = lax.ppermute(feat_tail, "node", to_right)
+    feat_right = lax.ppermute(feat_head, "node", to_left)
+    feat_mid = conv(window[rim : row_count - rim])
+    flat_features = jnp.concatenate([feat_head, feat_mid, feat_tail], axis=0)
     first_block = lax.axis_index("node") * block_count
+    band_tiles = build_band(tile_values, tile_cols, tile_count, first_block)
 
-    band_tiles = build_band(tile_values, tile_cols, tile_count, first_block)
-    extended = fetch_rim(flat_features, block_rows).reshape(
-        block_count + 2 * HB, block_rows, feat_width
-    )
-    order_one = band_product(band_tiles, extended).astype(jnp.bfloat16)
-    one_ext = fetch_rim(order_one.reshape(row_count, feat_width), block_rows).reshape(
-        block_count + 2 * HB, block_rows, feat_width
-    )
-    order_two = band_product(band_tiles, one_ext)
-    by_block = flat_features.reshape(block_count, block_rows, feat_width)
-    cheb_two = (2.0 * order_two - by_block.astype(jnp.float32)).astype(jnp.bfloat16)
-    joined = jnp.concatenate(
-        [flat_features, order_one.reshape(row_count, feat_width), cheb_two.reshape(row_count, feat_width)],
-        axis=1,
-    )
-    wfinal = jnp.concatenate([block_diag(cheb_weight[k], steps_dev) for k in range(3)], axis=0)
-    result = jnp.dot(joined, wfinal, preferred_element_type=jnp.float32)
-    result = result + jnp.tile(cheb_bias, steps_dev)
+    def blocks(*parts):
+        joined = jnp.concatenate(parts, axis=0) if len(parts) > 1 else parts[0]
+        return joined.reshape(-1, block_rows, feat_width)
+
+    def edges(band, left, own, right):
+        head = band_product(band[:HB], blocks(left, own[: 2 * rim]))
+        tail = band_product(band[block_count - HB :], blocks(own[row_count - 2 * rim :], right))
+        return head.reshape(rim, feat_width), tail.reshape(rim, feat_width)
+
+    one_head, one_tail = edges(band_tiles, feat_left, flat_features, feat_right)
+    one_head = one_head.astype(jnp.bfloat16)
+    one_tail = one_tail.astype(jnp.bfloat16)
+    one_left = lax.ppermute(one_tail, "node", to_right)
+    one_right = lax.ppermute(one_head, "node", to_left)
+    one_mid = band_product(band_tiles[HB : block_count - HB], blocks(flat_features))
+    one_mid = one_mid.reshape(row_count - 2 * rim, feat_width).astype(jnp.bfloat16)
+    order_one = jnp.concatenate([one_head, one_mid, one_tail], axis=0)
+
+    kron = [block_diag(cheb_weight[k], steps_dev) for k in range(3)]
+    early = jnp.dot(
+        jnp.concatenate([flat_features, order_one], axis=1),
+        jnp.concatenate(kron[:2], axis=0),
+        preferred_element_type=jnp.float32,
+    ) + jnp.tile(cheb_bias, steps_dev)
+
+    def finish(two, feat, part):
+        cheb_two = (2.0 * two - feat.astype(jnp.float32)).astype(jnp.bfloat16)
+        return part + jnp.dot(cheb_two, kron[2], preferred_element_type=jnp.float32)
+
+    two_mid = band_product(band_tiles[HB : block_count - HB], blocks(order_one))
+    two_mid = two_mid.reshape(row_count - 2 * rim, feat_width)
+    res_mid = finish(two_mid, feat_mid, early[rim : row_count - rim])
+    two_head, two_tail = edges(band_tiles, one_left, order_one, one_right)
+    res_head = finish(two_head, feat_head, early[:rim])
+    res_tail = finish(two_tail, feat_tail, early[row_count - rim :])
+    result = jnp.concatenate([res_head, res_mid, res_tail], axis=0)
     return jax.nn.relu(result).astype(jnp.bfloat16).reshape(row_count, steps_dev, chan_out)
-
 
 def solution(mesh):
     placed = (

time: 58 us -> 65 us (1.12)
  the two profiles are of different devices: /device:TPU:110 before, /device:TPU:147 now
where the time goes in v6:
time: 65 us; the launch traced here: 64.3 us
  matrix products  23.5 us (36%)
  starting transfers between devices  18.3 us (28%)
  local copies, waits for them, and re-layouts  10.7 us (16%)
  other arithmetic  9.12 us (14%)
  waiting for transfers between devices  1.78 us (3%)
  between operations  0.98 us (2%)
    dot_general x24, matrix products, band_product(): jnp.einsum('bpq,bqf->bpf', band_tiles[:, offset], extended[offset:offset...  11.3 us
    ppermute x1, starting transfers between devices, shards(): one_right = lax.ppermute(one_head, 'node', to_left)  6.25 us
    dot_general x3, matrix products, finish(): return part + jnp.dot(cheb_two, kron[2], preferred_element_type=jnp.float32)  4.34 us
    ppermute x1, starting transfers between devices, passed_along(): return lax.ppermute(value, axis, pairs)  3.61 us
    slice x2, local copies, waits for them, and re-layouts, conv(): newest = rows[:, base:base + pair_w]  3.31 us
    ppermute x1, starting transfers between devices, shards(): one_left = lax.ppermute(one_tail, 'node', to_right)  3.13 us
    ppermute x1, starting transfers between devices, shards(): feat_left = lax.ppermute(feat_tail, 'node', to_right)  3.12 us
    dot_general x6, matrix products, conv(): mixed = jnp.dot(lhs, wpair, preferred_element_type=jnp.float32)  2.99 us
  transfers between devices with their start and end apart: 5, of which 1 were waited for; matrix products, arithmetic and copies ran while one was open for 39% of the time, Pallas kernels for 0%

profile of v6, /device:TPU:147, one launch (start us, length us, event | category | flops | bytes accessed | tf_op | source)
XLA Modules:
  0.0 64.3 jit_solution(6921836783337203497)
XLA Ops:
  0.0 3.6 %collective-permute-start = (bf16[1024,256]{1,0:T(8,128)(2,1)}, bf16[1024,256]{1,0:T(8,128)(2,1)S(1)}, u32[]{:S(2)}, u32[]{:S(2)}) collective-permute-start(bf16[1024,256]{1,0:T(8,128)(2,1)} %param.8), channel_id=1, source_target_pairs={{0,32},{32,64},{64,96},{96,128},{128,160},{160,192},{192,224},{1,3... | collective-permute-start | bytes 1572872 | tf_op jit(solution)/shard_map/ppermute | solution.py:30
  3.6 1.6 %fusion.281 = (bf16[256,128]{1,0:T(8,128)(2,1)S(1)}, bf16[256,128]{1,0:T(8,128)(2,1)}, bf16[256,128]{1,0:T(8,128)(2,1)S(1)}, bf16[256,128]{1,0:T(8,128)(2,1)S(1)}) fusion(bf16[1024,256]{1,0:T(8,128)(2,1)} %param.8), kind=kLoop, calls=%fused_computation.377 | loop fusion | bytes 524288 | tf_op jit(solution)/shard_map/slice | solution.py:102
  5.2 1.7 %fusion.283 = (bf16[512,128]{1,0:T(8,128)(2,1)}, bf16[512,128]{1,0:T(8,128)(2,1)}) fusion(bf16[1024,256]{1,0:T(8,128)(2,1)} %param.8), kind=kLoop, calls=%fused_computation.379 | loop fusion | bytes 524288 | tf_op jit(solution)/shard_map/slice | solution.py:102
  8.5 1.3 %convolution_convert_fusion = bf16[8,5,128,128]{3,1,2,0:T(8,128)(2,1)S(1)} fusion(bf16[8,4,128,128]{3,2,1,0:T(8,128)(2,1)S(1)} %copy-done, s32[8,4]{1,0:T(8,128)S(1)} %copy.16, pred[8,4]{1,0:T(8,128)(4,1)S(1)} %iota_compare_fusion.2), kind=kOutput, calls=%fused_computation.32 | convolution fusion | flops 5898560 | bytes 2359456 | tf_op jit(solution)/shard_map/bjo,bjpq->bopq/dot_general | solution.py:41
  9.8 1.1 %fusion.275 = (bf16[2,1,128,128]{3,1,2,0:T(2,128)(2,1)S(1)}, bf16[2,1,128,128]{3,1,2,0:T(2,128)(2,1)S(1)}, bf16[2,1,128,128]{3,1,2,0:T(2,128)(2,1)S(1)}, bf16[2,...) fusion(bf16[8,5,128,128]{3,1,2,0:T(8,128)(2,1)S(1)} %convolutio, ...), kind=kLoop, calls=%fused_computation.371 | loop fusion | bytes 1310720 | tf_op jit(solution)/shard_map/slice | solution.py:58
  11.9 1.3 %fusion.276 = (bf16[4,1,128,128]{3,1,2,0:T(2,128)(2,1)S(1)}, bf16[4,1,128,128]{3,1,2,0:T(2,128)(2,1)S(1)}, bf16[4,1,128,128]{3,1,2,0:T(2,128)(2,1)S(1)}, bf16[4,...) fusion(bf16[8,5,128,128]{3,1,2,0:T(8,128)(2,1)S(1)} %convolution_convert_fusion), kind=kLoop, calls=%fused_computation.372 | loop fusion | bytes 1310720 | tf_op jit(solution)/shard_map/slice | solution.py:58
  14.7 1.2 %fusion.111 = f32[256,512]{1,0:T(8,128)S(1)} fusion(bf16[256,128]{1,0:T(8,128)(2,1)S(1)} %copy-done.29, bf16[256,128]{1,0:T(8,128)(2,1)S(1)} %get-tuple-element.51, bf16[256,128]{1,0:T(8,128)(2,1)} %copy-done.30, bf16[128,512]{1,0:T(8,128)(2,1)} %copy-done.24, bf16[128,512]{1,0:T(8,128)(2,1)S(1)} %bitcast.275, bf16[128,512]{1,0:T(8,128)(2,1)S(1)} %bitcast.269, ...), kind=kOutput, calls=%fused_computation.163 | convolution fusion | flops 137363456 | bytes 1245184 | tf_op jit(solution)/shard_map/dot_general | solution.py:106
  18.1 2.8 %maximum_maximum_fusion.2 = (bf16[768,512]{1,0:T(8,128)(2,1)S(1)}, bf16[768,512]{1,0:T(8,128)(2,1)S(1)}) fusion(bf16[256,128]{1,0:T(8,128)(2,1)S(1)} %get-tuple-element.71, bf16[256,128]{1,0:T(8,128)(2,1)S(1)} %get-tuple-element.72, bf16[256,128]{1,0:T(8,128)(2,1)S(1)} %get-tuple-element.33, bf16[256,128]{1,0:T(8,128)(2,1)S(1)} %get-tuple-element.32, ...), kind=kLoop, calls=%fused_computation.86 | loop fusion | flops 12582912 | bytes 2621440 | tf_op jit(solution)/shard_map/concatenate | solution.py:122
  21.0 2.2 %collective-permute-start.2 = (bf16[256,512]{1,0:T(8,128)(2,1)S(1)}, bf16[256,512]{1,0:T(8,128)(2,1)S(1)}, u32[]{:S(2)}, u32[]{:S(2)}) collective-permute-start(bf16[256,512]{1,0:T(8,128)(2,1)S(1)} %pad_maximum_fusion.9), channel_id=1, source_target_pairs={{1,0},{2,1},{3,2},{4,3},{5,4},{6,5},{7,6},{8,7},{9,8},{10,9},{11,1... | collective-permute-start | bytes 786440 | tf_op jit(solution)/shard_map/ppermute | solution.py:120
  23.3 3.1 %collective-permute-start.1 = (bf16[256,512]{1,0:T(8,128)(2,1)S(1)}, bf16[256,512]{1,0:T(8,128)(2,1)S(1)}, u32[]{:S(2)}, u32[]{:S(2)}) collective-permute-start(bf16[256,512]{1,0:T(8,128)(2,1)S(1)} %pad_maximum_fusion.10), channel_id=1, source_target_pairs={{0,1},{1,2},{2,3},{3,4},{4,5},{5,6},{6,7},{7,8},{8,9},{9,10},{10,1... | collective-permute-start | bytes 786440 | tf_op jit(solution)/shard_map/ppermute | solution.py:119
  29.0 1.8 %collective-permute-done.2 = bf16[256,512]{1,0:T(8,128)(2,1)S(1)} collective-permute-done((bf16[256,512]{1,0:T(8,128)(2,1)S(1)}, bf16[256,512]{1,0:T(8,128)(2,1)S(1)}, u32[]{:S(2)}, u32[]{:S(2)}) %collective-permute-start.2) | collective-permute-done | bytes 262176 | tf_op jit(solution)/shard_map/ppermute | solution.py:120
  31.3 3.1 %collective-permute-start.3 = (bf16[256,512]{1,0:T(8,128)(2,1)S(1)}, bf16[256,512]{1,0:T(8,128)(2,1)}, u32[]{:S(2)}, u32[]{:S(2)}) collective-permute-start(bf16[256,512]{1,0:T(8,128)(2,1)S(1)} %bitcast.204), channel_id=1, source_target_pairs={{0,1},{1,2},{2,3},{3,4},{4,5},{5,6},{6,7},{7,8},{8,9},{9,10},{10,1... | collective-permute-start | bytes 786440 | tf_op jit(solution)/shard_map/ppermute | solution.py:138
  35.4 6.2 %collective-permute-start.4 = (bf16[256,512]{1,0:T(8,128)(2,1)S(1)}, bf16[256,512]{1,0:T(8,128)(2,1)}, u32[]{:S(2)}, u32[]{:S(2)}) collective-permute-start(bf16[256,512]{1,0:T(8,128)(2,1)S(1)} %bitcast.200), channel_id=1, source_target_pairs={{1,0},{2,1},{3,2},{4,3},{5,4},{6,5},{7,6},{8,7},{9,8},{10,9},{11,1... | collective-permute-start | bytes 786440 | tf_op jit(solution)/shard_map/ppermute | solution.py:139
  45.2 1.3 %fusion.31 = f32[1024,512]{0,1:T(8,128)S(1)} fusion(bf16[256,512]{1,0:T(8,128)(2,1)S(1)} %bitcast.207, bf16[512,512]{1,0:T(8,128)(2,1)S(1)} %bitcast.193, bf16[256,512]{1,0:T(8,128)(2,1)S(1)} %bitcast.203, bf16[256,128]{1,0:T(8,128)(2,1)S(1)} %get-tuple-element.71, bf16[256,128]{1,0:T(8,128)(2,1)S(1)} %get-tuple-element.72, ...), kind=kOutput, calls=%fused_computation.33 | convolution fusion | flops 1107820544 | bytes 5244928 | tf_op jit(solution)/shard_map/dot_general | solution.py:145
  46.5 1.5 %convolution_add_fusion = bf16[512,512]{0,1:T(8,128)(2,1)} fusion(bf16[512,512]{1,0:T(8,128)(2,1)S(1)} %bitcast.255, f32[1024,512]{0,1:T(8,128)S(1)} %fusion.31, bf16[64,8,4,128]{3,2,1,0:T(4,128)(2,1)S(1)} %bitcast.194), kind=kOutput, calls=%fused_computation.34 | convolution fusion | flops 268959744 | bytes 2621440 | tf_op jit(solution)/shard_map/dot_general | solution.py:153
  49.0 2.1 %copy.21 = bf16[512,4,128]{2,1,0:T(4,128)(2,1)} copy(bf16[512,4,128]{0,2,1:T(8,128)(2,1)} %bitcast.208) | data formatting | bytes 1048576 | tf_op jit(solution)/shard_map/concatenate | solution.py:161
  51.2 2.2 %convolution_add_fusion.10 = f32[2,128,512]{2,1,0:T(8,128)} fusion(f32[2,128,512]{2,1,0:T(8,128)} %convolution_add_fusion.11, bf16[2,128,512]{2,1,0:T(8,128)(2,1)S(1)} %fusion.47, bf16[2,1,128,128]{3,1,2,0:T(2,128)(2,1)} %copy-done.19), kind=kOutput, calls=%fused_computation.51 | convolution fusion | flops 33685504 | bytes 1376256 | tf_op jit(solution)/shard_map/bpq,bqf->bpf/dot_general | solution.py:56
  53.4 1.8 %pad_maximum_fusion.4 = (bf16[256,512]{1,0:T(8,128)(2,1)}, bf16[256,512]{1,0:T(8,128)(2,1)S(1)}) fusion(bf16[256,512]{1,0:T(8,128)(2,1)} %collective-permute-done.4, bf16[512,512]{1,0:T(8,128)(2,1)} %copy-done.4, bf16[512,512]{1,0:T(8,128)(2,1)S(1)} %get-tuple-element.42, bf16[256,512]{1,0:T(8,128)(2,1)} %collective-permute-done.3), kind=kLoop, calls=%fused_computation.119 | loop fusion | flops 1048576 | bytes 2097152 | tf_op jit(solution)/shard_map/concatenate | solution.py:127
  55.4 1.2 %fusion.43 = f32[2,128,512]{2,1,0:T(8,128)S(1)} fusion(f32[2,128,512]{2,1,0:T(8,128)S(1)} %copy-done.5, f32[2,128,512]{2,1,0:T(8,128)S(1)} %fusion.221, bf16[2,128,512]{2,1,0:T(8,128)(2,1)} %bitcast.35, bf16[2,1,128,128]{3,1,2,0:T(2,128)(2,1)S(1)} %copy-done.21), kind=kOutput, calls=%fused_computation.58 | convolution fusion | flops 33816576 | bytes 1900544 | tf_op jit(solution)/shard_map/bpq,bqf->bpf/dot_general | solution.py:49
  57.1 1.4 %convolution_add_fusion.22 = bf16[256,512]{0,1:T(8,128)(2,1)S(1)} fusion(bf16[256,512]{1,0:T(8,128)(2,1)S(1)} %bitcast.259, f32[1024,512]{0,1:T(8,128)} %copy-done.1, bf16[64,8,4,128]{3,2,1,0:T(4,128)(2,1)S(1)} %bitcast.195), kind=kOutput, calls=%fused_computation.68 | convolution fusion | flops 134479872 | bytes 1572864 | tf_op jit(solution)/shard_map/dot_general | solution.py:153
  58.8 1.2 %fusion.200 = f32[2,128,512]{2,1,0:T(8,128)S(1)} fusion(bf16[2,128,512]{2,1,0:T(8,128)(2,1)} %bitcast.49, bf16[2,1,128,128]{3,1,2,0:T(2,128)(2,1)S(1)} %copy-done.12), kind=kOutput, calls=%fused_computation.276 | convolution fusion | flops 33554432 | bytes 851968 | tf_op jit(solution)/shard_map/bpq,bqf->bpf/dot_general | solution.py:56
  60.0 1.2 %fusion.48 = bf16[2,128,512]{2,1,0:T(8,128)(2,1)S(1)} fusion(f32[2,128,512]{2,1,0:T(8,128)S(1)} %fusion.200, f32[2,128,512]{2,1,0:T(8,128)S(1)} %copy-done.3, bf16[2,128,512]{2,1,0:T(8,128)(2,1)} %bitcast.246, bf16[2,128,128]{2,1,0:T(8,128)(2,1)S(1)} %bitcast.229, bf16[2,128,128]{2,1,0:T(8,128)(2,1)S(1)} %bitcast.231, ...), kind=kOutput, calls=%fused_computation.71 | convolution fusion | flops 35258368 | bytes 1900544 | tf_op jit(solution)/shard_map/bpq,bqf->bpf/dot_general | solution.py:56
  61.2 1.4 %convolution_add_fusion.21 = bf16[256,512]{0,1:T(8,128)(2,1)S(1)} fusion(bf16[256,512]{1,0:T(8,128)(2,1)S(1)} %bitcast.245, f32[1024,512]{0,1:T(8,128)} %copy-done.1, bf16[64,8,4,128]{3,2,1,0:T(4,128)(2,1)S(1)} %bitcast.196), kind=kOutput, calls=%fused_computation.67 | convolution fusion | flops 134479872 | bytes 1572864 | tf_op jit(solution)/shard_map/dot_general | solution.py:153
  62.8 1.5 %fusion.30 = bf16[1024,4,128]{2,1,0:T(4,128)(2,1)} fusion(bf16[256,4,128]{2,1,0:T(4,128)(2,1)S(1)} %copy.22, bf16[512,4,128]{2,1,0:T(4,128)(2,1)S(1)} %copy-done.2, bf16[256,4,128]{2,1,0:T(4,128)(2,1)S(1)} %copy.20), kind=kLoop, calls=%fused_computation.31 | loop fusion | flops 3670016 | bytes 2097152 | tf_op jit(solution)/shard_map/convert_element_type | solution.py:162
  (141 shorter events, 15.5 us)
Async XLA Ops:
  0.0 8.5 %copy-start = (bf16[8,4,128,128]{3,2,1,0:T(8,128)(2,1)S(1)}, bf16[8,4,128,128]{3,2,1,0:T(8,128)(2,1)}, u32[]{:S(2)}) copy-start(bf16[8,4,128,128]{3,2,1,0:T(8,128)(2,1)} %param.11) | copy-start | bytes 3145732
  0.0 8.3 %copy-start.31 = (s32[8,4]{0,1:T(4,128)S(1)}, s32[8,4]{0,1:T(4,128)}, u32[]{:S(2)}) copy-start(s32[8,4]{0,1:T(4,128)} %param.12) | copy-start | bytes 388
  0.0 8.4 %copy-start.34 = (s32[8]{0:T(128)S(1)}, s32[8]{0:T(128)}, u32[]{:S(2)}) copy-start(s32[8]{0:T(128)} %param.13) | copy-start | bytes 100
  0.0 13.2 %collective-permute-start = (bf16[1024,256]{1,0:T(8,128)(2,1)}, bf16[1024,256]{1,0:T(8,128)(2,1)S(1)}, u32[]{:S(2)}, u32[]{:S(2)}) collective-permute-start(bf16[1024,256]{1,0:T(8,128)(2,1)} %param.8), channel_id=1, source_target_pairs={{0,32},{32,64},{64,96},{96,128},{128,160},{160,192},{192,224},{1,3... | collective-permute-start | bytes 1572872 | tf_op jit(solution)/shard_map/ppermute | solution.py:30
  5.2 8.7 %copy-start.30 = (bf16[256,128]{1,0:T(8,128)(2,1)}, bf16[256,128]{1,0:T(8,128)(2,1)S(1)}, u32[]{:S(2)}) copy-start(bf16[256,128]{1,0:T(8,128)(2,1)S(1)} %get-tuple-element.54) | copy-start | bytes 196612
  8.3 5.6 %copy-start.24 = (bf16[128,512]{1,0:T(8,128)(2,1)}, bf16[128,512]{1,0:T(8,128)(2,1)S(1)}, u32[]{:S(2)}) copy-start(bf16[128,512]{1,0:T(8,128)(2,1)S(1)} %fusion.139) | copy-start | bytes 393220
  10.9 17.9 %copy-start.19 = (bf16[2,1,128,128]{3,1,2,0:T(2,128)(2,1)}, bf16[2,1,128,128]{3,1,2,0:T(2,128)(2,1)S(1)}, u32[]{:S(2)}) copy-start(bf16[2,1,128,128]{3,1,2,0:T(2,128)(2,1)S(1)} %get-tuple-element.7) | copy-start | bytes 196612
  10.9 19.9 %copy-start.11 = (bf16[2,1,128,128]{3,1,2,0:T(2,128)(2,1)}, bf16[2,1,128,128]{3,1,2,0:T(2,128)(2,1)S(1)}, u32[]{:S(2)}) copy-start(bf16[2,1,128,128]{3,1,2,0:T(2,128)(2,1)S(1)} %get-tuple-element.6) | copy-start | bytes 196612
  11.0 20.1 %copy-start.15 = (bf16[2,1,128,128]{3,1,2,0:T(2,128)(2,1)}, bf16[2,1,128,128]{3,1,2,0:T(2,128)(2,1)S(1)}, u32[]{:S(2)}) copy-start(bf16[2,1,128,128]{3,1,2,0:T(2,128)(2,1)S(1)} %get-tuple-element.5) | copy-start | bytes 196612
  11.0 23.5 %copy-start.13 = (bf16[2,1,128,128]{3,1,2,0:T(2,128)(2,1)}, bf16[2,1,128,128]{3,1,2,0:T(2,128)(2,1)S(1)}, u32[]{:S(2)}) copy-start(bf16[2,1,128,128]{3,1,2,0:T(2,128)(2,1)S(1)} %get-tuple-element.13) | copy-start | bytes 196612
  11.0 23.7 %copy-start.20 = (bf16[2,1,128,128]{3,1,2,0:T(2,128)(2,1)}, bf16[2,1,128,128]{3,1,2,0:T(2,128)(2,1)S(1)}, u32[]{:S(2)}) copy-start(bf16[2,1,128,128]{3,1,2,0:T(2,128)(2,1)S(1)} %get-tuple-element.14) | copy-start | bytes 196612
  11.0 23.9 %copy-start.17 = (bf16[2,1,128,128]{3,1,2,0:T(2,128)(2,1)}, bf16[2,1,128,128]{3,1,2,0:T(2,128)(2,1)S(1)}, u32[]{:S(2)}) copy-start(bf16[2,1,128,128]{3,1,2,0:T(2,128)(2,1)S(1)} %get-tuple-element.11) | copy-start | bytes 196612
  11.0 24.2 %copy-start.22 = (bf16[2,1,128,128]{3,1,2,0:T(2,128)(2,1)}, bf16[2,1,128,128]{3,1,2,0:T(2,128)(2,1)S(1)}, u32[]{:S(2)}) copy-start(bf16[2,1,128,128]{3,1,2,0:T(2,128)(2,1)S(1)} %get-tuple-element.10) | copy-start | bytes 196612
  17.9 27.3 %copy-start.7 = (bf16[256,128]{1,0:T(8,128)(2,1)}, bf16[256,128]{1,0:T(8,128)(2,1)S(1)}, u32[]{:S(2)}) copy-start(bf16[256,128]{1,0:T(8,128)(2,1)S(1)} %get-tuple-element.73) | copy-start | bytes 196612
  18.0 27.2 %copy-start.9 = (bf16[256,128]{1,0:T(8,128)(2,1)}, bf16[256,128]{1,0:T(8,128)(2,1)S(1)}, u32[]{:S(2)}) copy-start(bf16[256,128]{1,0:T(8,128)(2,1)S(1)} %get-tuple-element.74) | copy-start | bytes 196612
  21.0 9.8 %collective-permute-start.2 = (bf16[256,512]{1,0:T(8,128)(2,1)S(1)}, bf16[256,512]{1,0:T(8,128)(2,1)S(1)}, u32[]{:S(2)}, u32[]{:S(2)}) collective-permute-start(bf16[256,512]{1,0:T(8,128)(2,1)S(1)} %pad_maximum_fusion.9), channel_id=1, source_target_pairs={{1,0},{2,1},{3,2},{4,3},{5,4},{6,5},{7,6},{8,7},{9,8},{10,9},{11,1... | collective-permute-start | bytes 786440 | tf_op jit(solution)/shard_map/ppermute | solution.py:120
  23.3 11.1 %collective-permute-start.1 = (bf16[256,512]{1,0:T(8,128)(2,1)S(1)}, bf16[256,512]{1,0:T(8,128)(2,1)S(1)}, u32[]{:S(2)}, u32[]{:S(2)}) collective-permute-start(bf16[256,512]{1,0:T(8,128)(2,1)S(1)} %pad_maximum_fusion.10), channel_id=1, source_target_pairs={{0,1},{1,2},{2,3},{3,4},{4,5},{5,6},{6,7},{7,8},{8,9},{9,10},{10,1... | collective-permute-start | bytes 786440 | tf_op jit(solution)/shard_map/ppermute | solution.py:119
  31.3 22.1 %collective-permute-start.3 = (bf16[256,512]{1,0:T(8,128)(2,1)S(1)}, bf16[256,512]{1,0:T(8,128)(2,1)}, u32[]{:S(2)}, u32[]{:S(2)}) collective-permute-start(bf16[256,512]{1,0:T(8,128)(2,1)S(1)} %bitcast.204), channel_id=1, source_target_pairs={{0,1},{1,2},{2,3},{3,4},{4,5},{5,6},{6,7},{7,8},{8,9},{9,10},{10,1... | collective-permute-start | bytes 786440 | tf_op jit(solution)/shard_map/ppermute | solution.py:138
  35.4 18.0 %collective-permute-start.4 = (bf16[256,512]{1,0:T(8,128)(2,1)S(1)}, bf16[256,512]{1,0:T(8,128)(2,1)}, u32[]{:S(2)}, u32[]{:S(2)}) collective-permute-start(bf16[256,512]{1,0:T(8,128)(2,1)S(1)} %bitcast.200), channel_id=1, source_target_pairs={{1,0},{2,1},{3,2},{4,3},{5,4},{6,5},{7,6},{8,7},{9,8},{10,9},{11,1... | collective-permute-start | bytes 786440 | tf_op jit(solution)/shard_map/ppermute | solution.py:139
  51.2 4.1 %copy-start.14 = (bf16[2,1,128,128]{3,1,2,0:T(2,128)(2,1)S(1)}, bf16[2,1,128,128]{3,1,2,0:T(2,128)(2,1)}, u32[]{:S(2)}) copy-start(bf16[2,1,128,128]{3,1,2,0:T(2,128)(2,1)} %copy-done.13) | copy-start | bytes 196612
  51.2 4.3 %copy-start.5 = (f32[2,128,512]{2,1,0:T(8,128)S(1)}, f32[2,128,512]{2,1,0:T(8,128)}, u32[]{:S(2)}) copy-start(f32[2,128,512]{2,1,0:T(8,128)} %fusion.217) | copy-start | bytes 1572868
  51.2 4.3 %copy-start.21 = (bf16[2,1,128,128]{3,1,2,0:T(2,128)(2,1)S(1)}, bf16[2,1,128,128]{3,1,2,0:T(2,128)(2,1)}, u32[]{:S(2)}) copy-start(bf16[2,1,128,128]{3,1,2,0:T(2,128)(2,1)} %copy-done.20) | copy-start | bytes 196612
  53.4 3.3 %copy-start.6 = (bf16[256,512]{1,0:T(8,128)(2,1)S(1)}, bf16[256,512]{1,0:T(8,128)(2,1)}, u32[]{:S(2)}) copy-start(bf16[256,512]{1,0:T(8,128)(2,1)} %get-tuple-element.40) | copy-start | bytes 786436
  53.4 3.3 %copy-start.18 = (bf16[2,1,128,128]{3,1,2,0:T(2,128)(2,1)S(1)}, bf16[2,1,128,128]{3,1,2,0:T(2,128)(2,1)}, u32[]{:S(2)}) copy-start(bf16[2,1,128,128]{3,1,2,0:T(2,128)(2,1)} %copy-done.17) | copy-start | bytes 196612
  (16 other events, 28.8 us)

commit v7 on v3

--- a/solution.py
+++ b/solution.py
@@ -108,34 +108,70 @@
             pieces.append(linear * jax.nn.sigmoid(gate))
     flat_features = jnp.concatenate(pieces, axis=1).astype(jnp.bfloat16)
     first_block = lax.axis_index("node") * block_count
-
     band_tiles = build_band(tile_values, tile_cols, tile_count, first_block)
     node_count = lax.axis_size("node")
     to_right = [(i, i + 1) for i in range(node_count - 1)]
     to_left = [(i + 1, i) for i in range(node_count - 1)]
-    band_left = lax.ppermute(band_tiles[block_count - HB :], "node", to_right)
-    band_right = lax.ppermute(band_tiles[:HB], "node", to_left)
-    reach = 2 * HB * block_rows
-    feat_left = lax.ppermute(flat_features[row_count - reach :], "node", to_right)
-    feat_right = lax.ppermute(flat_features[:reach], "node", to_left)
-    feat_ext = jnp.concatenate([feat_left, flat_features, feat_right], axis=0).reshape(
-        block_count + 4 * HB, block_rows, feat_width
-    )
-    band_ext = jnp.concatenate([band_left, band_tiles, band_right], axis=0)
-    one_ext = band_product(band_ext, feat_ext).astype(jnp.bfloat16)
-    order_two = band_product(band_tiles, one_ext)
-    order_one = one_ext[HB : HB + block_count]
-    by_block = flat_features.reshape(block_count, block_rows, feat_width)
-    cheb_two = (2.0 * order_two - by_block.astype(jnp.float32)).astype(jnp.bfloat16)
-    joined = jnp.concatenate(
-        [flat_features, order_one.reshape(row_count, feat_width), cheb_two.reshape(row_count, feat_width)],
-        axis=1,
-    )
-    wfinal = jnp.concatenate([block_diag(cheb_weight[k], steps_dev) for k in range(3)], axis=0)
-    result = jnp.dot(joined, wfinal, preferred_element_type=jnp.float32)
-    result = result + jnp.tile(cheb_bias, steps_dev)
+    rim = HB * block_rows
+    edge_ids = list(range(HB)) + list(range(block_count - HB, block_count))
+    halo_band = []
+    for b in edge_ids:
+        terms = []
+        for o in range(2 * HB + 1):
+            j = b + o
+            if j < HB or j >= block_count + HB:
+                terms.append(band_tiles[b, o])
+        while len(terms) < HB:
+            terms.append(jnp.zeros_like(band_tiles[0, 0]))
+        halo_band.append(jnp.stack(terms))
+    halo_band = jnp.stack(halo_band)
+
+    def halo_blocks(left, right):
+        lb = left.reshape(HB, block_rows, feat_width)
+        rb = right.reshape(HB, block_rows, feat_width)
+        picks = []
+        for b in edge_ids:
+            terms = []
+            for o in range(2 * HB + 1):
+                j = b + o
+                if j < HB:
+                    terms.append(lb[j])
+                elif j >= block_count + HB:
+                    terms.append(rb[j - block_count - HB])
+            while len(terms) < HB:
+                terms.append(terms[-1])
+            picks.append(jnp.stack(terms))
+        return jnp.stack(picks)
+
+    def halo_part(left, right):
+        part = jnp.einsum(
+            "bkpq,bkqf->bpf", halo_band, halo_blocks(left, right), preferred_element_type=jnp.float32
+        )
+        middle = jnp.zeros((block_count - 2 * HB, block_rows, feat_width), jnp.float32)
+        return jnp.concatenate([part[:HB], middle, part[HB:]], axis=0)
+
+    def own_part(values):
+        padded = jnp.pad(values.reshape(block_count, block_rows, feat_width), ((HB, HB), (0, 0), (0, 0)))
+        return band_product(band_tiles, padded)
+
+    feat_left = lax.ppermute(flat_features[row_count - rim :], "node", to_right)
+    feat_right = lax.ppermute(flat_features[:rim], "node", to_left)
+    one_own = own_part(flat_features)
+    order_one = (one_own + halo_part(feat_left, feat_right)).astype(jnp.bfloat16)
+    order_one = order_one.reshape(row_count, feat_width)
+    one_left = lax.ppermute(order_one[row_count - rim :], "node", to_right)
+    one_right = lax.ppermute(order_one[:rim], "node", to_left)
+    two_own = own_part(order_one)
+    kron = [block_diag(cheb_weight[k], steps_dev) for k in range(3)]
+    early = jnp.dot(
+        jnp.concatenate([flat_features, order_one], axis=1),
+        jnp.concatenate(kron[:2], axis=0),
+        preferred_element_type=jnp.float32,
+    ) + jnp.tile(cheb_bias, steps_dev)
+    order_two = (two_own + halo_part(one_left, one_right)).reshape(row_count, feat_width)
+    cheb_two = (2.0 * order_two - flat_features.astype(jnp.float32)).astype(jnp.bfloat16)
+    result = early + jnp.dot(cheb_two, kron[2], preferred_element_type=jnp.float32)
     return jax.nn.relu(result).astype(jnp.bfloat16).reshape(row_count, steps_dev, chan_out)
-
 
 def solution(mesh):
     placed = (

time: 74.2 us -> 53.8 us (0.73)
  the two profiles are of different devices: /device:TPU:110 before, /device:TPU:144 now
where the time goes in v7:
time: 53.8 us; the launch traced here: 53.4 us
  waiting for transfers between devices  18 us (33%)
  starting transfers between devices  14.2 us (26%)
  matrix products  10.5 us (20%)
  local copies, waits for them, and re-layouts  7.94 us (15%)
  other arithmetic  2.33 us (4%)
    ppermute x1, waiting for transfers between devices, shards(): feat_left = lax.ppermute(flat_features[row_count - rim:], 'node', to_right)  7.8 us
    ppermute x1, waiting for transfers between devices, shards(): one_left = lax.ppermute(order_one[row_count - rim:], 'node', to_right)  5.18 us
    ppermute x1, starting transfers between devices, shards(): feat_right = lax.ppermute(flat_features[:rim], 'node', to_left)  4.21 us
    dot_general x8, matrix products, band_product(): jnp.einsum('bpq,bqf->bpf', band_tiles[:, offset], extended[offset:offset...  4.19 us
    ppermute x1, starting transfers between devices, shards(): one_left = lax.ppermute(order_one[row_count - rim:], 'node', to_right)  4.1 us
    ppermute x1, waiting for transfers between devices, shards(): feat_right = lax.ppermute(flat_features[:rim], 'node', to_left)  2.74 us
    slice x1, local copies, waits for them, and re-layouts, band_product(): band_tiles[:, offset]  2.65 us
    ppermute x1, waiting for transfers between devices, shards(): one_right = lax.ppermute(order_one[:rim], 'node', to_left)  2.32 us
  transfers between devices with their start and end apart: 5, of which 4 were waited for; matrix products, arithmetic and copies ran while one was open for 23% of the time, Pallas kernels for 0%

profile of v7, /device:TPU:144, one launch (start us, length us, event | category | flops | bytes accessed | tf_op | source)
XLA Modules:
  0.0 53.4 jit_solution(7988244123553267284)
XLA Ops:
  0.0 2.1 %collective-permute-start = (bf16[1024,256]{1,0:T(8,128)(2,1)}, bf16[1024,256]{1,0:T(8,128)(2,1)S(1)}, u32[]{:S(2)}, u32[]{:S(2)}) collective-permute-start(bf16[1024,256]{1,0:T(8,128)(2,1)} %param.8), channel_id=1, source_target_pairs={{0,32},{32,64},{64,96},{96,128},{128,160},{160,192},{192,224},{1,3... | collective-permute-start | bytes 1572872 | tf_op jit(solution)/shard_map/ppermute | solution.py:30
  2.1 1.1 %fusion.132 = (bf16[1024,128]{1,0:T(8,128)(2,1)S(1)}, bf16[1024,128]{1,0:T(8,128)(2,1)S(1)}) fusion(bf16[1024,256]{1,0:T(8,128)(2,1)} %param.8), kind=kLoop, calls=%fused_computation.214 | loop fusion | bytes 1048576 | tf_op jit(solution)/shard_map/slice | solution.py:99
  3.2 0.8 %fusion.134 = (f32[128]{0:T(128)S(1)}, f32[128]{0:T(128)S(1)}) fusion(f32[256]{0:T(256)} %param.10), kind=kLoop, calls=%fused_computation.216 | loop fusion | bytes 2048 | tf_op jit(solution)/shard_map/slice | solution.py:106
  4.0 0.8 %slice_bitcast_fusion.13 = (bf16[64,256]{1,0:T(8,128)(2,1)S(1)}, bf16[64,256]{1,0:T(8,128)(2,1)S(1)}, bf16[64,256]{1,0:T(8,128)(2,1)S(1)}) fusion(bf16[3,64,256]{2,1,0:T(8,128)(2,1)} %param.9), kind=kLoop, calls=%fused_computation.171 | loop fusion | bytes 196608 | tf_op jit(solution)/shard_map/jit(kron)/mul | solution.py:72
  5.5 1.3 %convolution_convert_fusion = bf16[8,5,128,128]{3,1,2,0:T(8,128)(2,1)S(1)} fusion(bf16[8,4,128,128]{3,2,1,0:T(8,128)(2,1)S(1)} %copy-done, s32[8,4]{1,0:T(8,128)S(1)} %copy.42, pred[8,4]{1,0:T(8,128)(4,1)S(1)} %iota_compare_fusion.2), kind=kOutput, calls=%fused_computation.7 | convolution fusion | flops 5898560 | bytes 2359456 | tf_op jit(solution)/shard_map/bjo,bjpq->bopq/dot_general | solution.py:41
  7.4 0.7 %broadcast_multiply_fusion = (bf16[4,128,4,128]{3,2,1,0:T(4,128)(2,1)S(1)}, bf16[4,128,4,128]{3,2,1,0:T(4,128)(2,1)S(1)}, bf16[4,128,4,128]{3,2,1,0:T(4,128)(2,1)S(1)}) fusion(bf16[128,128]{1,0:T(8,128)(2,1)S(1)} %get-tuple-element.52, bf16[4,4]{1,0:T(4,128)(2,1)S(1)} %fusion.107, bf16[128,128]{1,0:T(8,128)(2,1)S(1)} %get-tuple-element.54, ...), kind=kLoop, calls=%fused_computation.130 | loop fusion | flops 786432 | bytes 1671200 | tf_op jit(solution)/shard_map/jit(kron)/mul | solution.py:80
  8.2 2.6 %fusion.127 = (bf16[8,1,128,128]{3,1,2,0:T(2,128)(2,1)S(1)}, bf16[8,1,128,128]{3,1,2,0:T(2,128)(2,1)S(1)}, bf16[8,1,128,128]{3,1,2,0:T(2,128)(2,1)S(1)}, bf16[8,...) fusion(bf16[8,5,128,128]{3,1,2,0:T(8,128)(2,1)S(1)} %convolution_convert_fusion), kind=kLoop, calls=%fused_computation.209 | loop fusion | bytes 2621440 | tf_op jit(solution)/shard_map/slice | solution.py:58
  10.9 0.7 %fusion.10 = f32[1024,512]{1,0:T(8,128)S(1)} fusion(bf16[1024,128]{1,0:T(8,128)(2,1)S(1)} %get-tuple-element.33, bf16[1024,128]{1,0:T(8,128)(2,1)S(1)} %get-tuple-element.35, bf16[1024,128]{1,0:T(8,128)(2,1)S(1)} %get-tuple-element.34, bf16[128,512]{1,0:T(8,128)(2,1)S(1)} %fusion.91, bf16[128,512]{1,0:T(8,128)(2,1)S(1)} %bitcast.159, ...), kind=kOutput, calls=%fused_computation.24 | convolution fusion | flops 543162368 | bytes 3407872 | tf_op jit(solution)/shard_map/dot_general | solution.py:103
  12.0 0.7 %fusion.18 = f32[1024,512]{1,0:T(8,128)S(1)} fusion(bf16[1024,128]{1,0:T(8,128)(2,1)S(1)} %get-tuple-element.32, bf16[1024,128]{1,0:T(8,128)(2,1)S(1)} %get-tuple-element.34, bf16[1024,128]{1,0:T(8,128)(2,1)S(1)} %get-tuple-element.33, bf16[128,512]{1,0:T(8,128)(2,1)S(1)} %fusion.91, bf16[128,512]{1,0:T(8,128)(2,1)S(1)} %bitcast.160, ...), kind=kOutput, calls=%fused_computation.32 | convolution fusion | flops 543162368 | bytes 3407872 | tf_op jit(solution)/shard_map/dot_general | solution.py:103
  13.2 4.2 %collective-permute-start.2 = (bf16[256,512]{1,0:T(8,128)(2,1)S(1)}, bf16[256,512]{1,0:T(8,128)(2,1)S(1)}, u32[]{:S(2)}, u32[]{:S(2)}) collective-permute-start(bf16[256,512]{1,0:T(8,128)(2,1)S(1)} %get-tuple-element.31), channel_id=1, source_target_pairs={{1,0},{2,1},{3,2},{4,3},{5,4},{6,5},{7,6},{8,7},{9,8},{10,9},{11,1... | collective-permute-start | bytes 786440 | tf_op jit(solution)/shard_map/ppermute | solution.py:158
  17.4 1.9 %collective-permute-start.1 = (bf16[256,512]{1,0:T(8,128)(2,1)S(1)}, bf16[256,512]{1,0:T(8,128)(2,1)S(1)}, u32[]{:S(2)}, u32[]{:S(2)}) collective-permute-start(bf16[256,512]{1,0:T(8,128)(2,1)S(1)} %get-tuple-element.30), channel_id=1, source_target_pairs={{0,1},{1,2},{2,3},{3,4},{4,5},{5,6},{6,7},{7,8},{8,9},{9,10},{10,1... | collective-permute-start | bytes 786440 | tf_op jit(solution)/shard_map/ppermute | solution.py:157
  19.4 0.4 fusion.85
  21.1 2.7 %collective-permute-done.2 = bf16[256,512]{1,0:T(8,128)(2,1)S(1)} collective-permute-done((bf16[256,512]{1,0:T(8,128)(2,1)S(1)}, bf16[256,512]{1,0:T(8,128)(2,1)S(1)}, u32[]{:S(2)}, u32[]{:S(2)}) %collective-permute-start.2) | collective-permute-done | bytes 262176 | tf_op jit(solution)/shard_map/ppermute | solution.py:158
  23.8 7.8 %collective-permute-done.1 = bf16[256,512]{1,0:T(8,128)(2,1)S(1)} collective-permute-done((bf16[256,512]{1,0:T(8,128)(2,1)S(1)}, bf16[256,512]{1,0:T(8,128)(2,1)S(1)}, u32[]{:S(2)}, u32[]{:S(2)}) %collective-permute-start.1) | collective-permute-done | bytes 262176 | tf_op jit(solution)/shard_map/ppermute | solution.py:157
  32.2 0.6 %fusion = bf16[8,128,512]{2,1,0:T(8,128)(2,1)S(1)} fusion(f32[2,128,512]{2,1,0:T(8,128)S(1)} %get-tuple-element.29, f32[2,128,512]{2,1,0:T(8,128)S(1)} %get-tuple-element.28, f32[8,128,512]{2,1,0:T(8,128)S(1)} %fusion.6, f32[8,128,512]{2,1,0:T(8,128)S(1)} %fusion.85, f32[8,128,512]{2,1,0:T(8,128)S(1)} %fusion.4, f32[8,128,512]{2,1,0:T(8,128)S(1)} %fusion.5, ...), kind=kOutput, calls=%fused_computation.1 | convolution fusion | flops 138412032 | bytes 11796512 | tf_op jit(solution)/shard_map/bpq,bqf->bpf/dot_general | solution.py:56
  33.3 0.4 fusion.83
  34.1 1.9 %collective-permute-start.4 = (bf16[256,512]{1,0:T(8,128)(2,1)S(1)}, bf16[256,512]{1,0:T(8,128)(2,1)S(1)}, u32[]{:S(2)}, u32[]{:S(2)}) collective-permute-start(bf16[256,512]{1,0:T(8,128)(2,1)S(1)} %bitcast.158), channel_id=1, source_target_pairs={{1,0},{2,1},{3,2},{4,3},{5,4},{6,5},{7,6},{8,7},{9,8},{10,9},{11,1... | collective-permute-start | bytes 786440 | tf_op jit(solution)/shard_map/ppermute | solution.py:163
  36.0 4.1 %collective-permute-start.3 = (bf16[256,512]{1,0:T(8,128)(2,1)S(1)}, bf16[256,512]{1,0:T(8,128)(2,1)S(1)}, u32[]{:S(2)}, u32[]{:S(2)}) collective-permute-start(bf16[256,512]{1,0:T(8,128)(2,1)S(1)} %bitcast.157), channel_id=1, source_target_pairs={{0,1},{1,2},{2,3},{3,4},{4,5},{5,6},{6,7},{7,8},{8,9},{9,10},{10,1... | collective-permute-start | bytes 786440 | tf_op jit(solution)/shard_map/ppermute | solution.py:162
  40.3 1.3 %fusion.33 = f32[1024,512]{0,1:T(8,128)S(1)} fusion(bf16[1024,1024]{1,0:T(8,128)(2,1)S(1)} %constant_dynamic-update-slice_fusion, bf16[512,512]{1,0:T(8,128)(2,1)S(1)} %get-tuple-element.74, bf16[512,512]{1,0:T(8,128)(2,1)S(1)} %get-tuple-element.75), kind=kOutput, calls=%fused_computation.48 | convolution fusion | flops 1075838976 | bytes 5242880 | tf_op jit(solution)/shard_map/dot_general | solution.py:166
  42.0 2.3 %collective-permute-done.4 = bf16[256,512]{1,0:T(8,128)(2,1)S(1)} collective-permute-done((bf16[256,512]{1,0:T(8,128)(2,1)S(1)}, bf16[256,512]{1,0:T(8,128)(2,1)S(1)}, u32[]{:S(2)}, u32[]{:S(2)}) %collective-permute-start.4) | collective-permute-done | bytes 262176 | tf_op jit(solution)/shard_map/ppermute | solution.py:163
  44.4 5.2 %collective-permute-done.3 = bf16[256,512]{1,0:T(8,128)(2,1)S(1)} collective-permute-done((bf16[256,512]{1,0:T(8,128)(2,1)S(1)}, bf16[256,512]{1,0:T(8,128)(2,1)S(1)}, u32[]{:S(2)}, u32[]{:S(2)}) %collective-permute-start.3) | collective-permute-done | bytes 262176 | tf_op jit(solution)/shard_map/ppermute | solution.py:162
  50.1 1.1 %fusion.3 = bf16[8,128,512]{2,1,0:T(8,128)(2,1)S(1)} fusion(f32[2,128,512]{2,1,0:T(8,128)S(1)} %get-tuple-element.25, f32[2,128,512]{2,1,0:T(8,128)S(1)} %get-tuple-element.24, f32[8,128,512]{2,1,0:T(8,128)S(1)} %fusion.9, f32[8,128,512]{2,1,0:T(8,128)S(1)} %fusion.83, f32[8,128,512]{2,1,0:T(8,128)S(1)} %fusion.7, f32[8,128,512]{2,1,0:T(8,128)S(1)} %fusion.8, ...), kind=kOutput, calls=%fused_computation.5 | convolution fusion | flops 143654912 | bytes 12845088 | tf_op jit(solution)/shard_map/bpq,bqf->bpf/dot_general | solution.py:56
  51.2 0.8 %maximum_convert_fusion = bf16[1024,512]{0,1:T(8,128)(2,1)S(1)} fusion(f32[1024,512]{0,1:T(8,128)S(1)} %fusion.33, bf16[1024,512]{1,0:T(8,128)(2,1)S(1)} %bitcast.151, f32[512]{0:T(512)S(1)} %broadcast_bitcast_fusion, bf16[64,8,4,128]{3,2,1,0:T(4,128)(2,1)S(1)} %bitcast.153), kind=kOutput, calls=%fused_computation.6 | convolution fusion | flops 538968064 | bytes 4720640 | tf_op jit(solution)/shard_map/dot_general | solution.py:173
  52.0 1.4 %copy.44 = bf16[1024,4,128]{2,1,0:T(4,128)(2,1)} copy(bf16[1024,4,128]{0,2,1:T(8,128)(2,1)S(1)} %bitcast.152) | data formatting | bytes 2097152 | tf_op jit(solution)/shard_map/reshape | solution.py:174
  (62 shorter events, 6.0 us)
Async XLA Ops:
  0.0 5.5 %copy-start = (bf16[8,4,128,128]{3,2,1,0:T(8,128)(2,1)S(1)}, bf16[8,4,128,128]{3,2,1,0:T(8,128)(2,1)}, u32[]{:S(2)}) copy-start(bf16[8,4,128,128]{3,2,1,0:T(8,128)(2,1)} %param.11) | copy-start | bytes 3145732
  0.0 5.3 %copy-start.2 = (s32[8,4]{0,1:T(4,128)S(1)}, s32[8,4]{0,1:T(4,128)}, u32[]{:S(2)}) copy-start(s32[8,4]{0,1:T(4,128)} %param.12) | copy-start | bytes 388
  0.0 5.4 %copy-start.4 = (s32[8]{0:T(128)S(1)}, s32[8]{0:T(128)}, u32[]{:S(2)}) copy-start(s32[8]{0:T(128)} %param.13) | copy-start | bytes 100
  0.0 10.8 %collective-permute-start = (bf16[1024,256]{1,0:T(8,128)(2,1)}, bf16[1024,256]{1,0:T(8,128)(2,1)S(1)}, u32[]{:S(2)}, u32[]{:S(2)}) collective-permute-start(bf16[1024,256]{1,0:T(8,128)(2,1)} %param.8), channel_id=1, source_target_pairs={{0,32},{32,64},{64,96},{96,128},{128,160},{160,192},{192,224},{1,3... | collective-permute-start | bytes 1572872 | tf_op jit(solution)/shard_map/ppermute | solution.py:30
  5.5 1.7 %copy-start.1 = (bf16[3,128,128]{2,1,0:T(8,128)(2,1)S(1)}, bf16[3,128,128]{2,1,0:T(8,128)(2,1)}, u32[]{:S(2)}) copy-start(bf16[3,128,128]{2,1,0:T(8,128)(2,1)} %param.14) | copy-start | bytes 294916
  5.5 1.7 %copy-start.3 = (f32[128]{0:T(128)S(1)}, f32[128]{0:T(128)}, u32[]{:S(2)}) copy-start(f32[128]{0:T(128)} %param.15) | copy-start | bytes 1540
  13.2 10.7 %collective-permute-start.2 = (bf16[256,512]{1,0:T(8,128)(2,1)S(1)}, bf16[256,512]{1,0:T(8,128)(2,1)S(1)}, u32[]{:S(2)}, u32[]{:S(2)}) collective-permute-start(bf16[256,512]{1,0:T(8,128)(2,1)S(1)} %get-tuple-element.31), channel_id=1, source_target_pairs={{1,0},{2,1},{3,2},{4,3},{5,4},{6,5},{7,6},{8,7},{9,8},{10,9},{11,1... | collective-permute-start | bytes 786440 | tf_op jit(solution)/shard_map/ppermute | solution.py:158
  17.4 14.3 %collective-permute-start.1 = (bf16[256,512]{1,0:T(8,128)(2,1)S(1)}, bf16[256,512]{1,0:T(8,128)(2,1)S(1)}, u32[]{:S(2)}, u32[]{:S(2)}) collective-permute-start(bf16[256,512]{1,0:T(8,128)(2,1)S(1)} %get-tuple-element.30), channel_id=1, source_target_pairs={{0,1},{1,2},{2,3},{3,4},{4,5},{5,6},{6,7},{7,8},{8,9},{9,10},{10,1... | collective-permute-start | bytes 786440 | tf_op jit(solution)/shard_map/ppermute | solution.py:157
  34.1 10.2 %collective-permute-start.4 = (bf16[256,512]{1,0:T(8,128)(2,1)S(1)}, bf16[256,512]{1,0:T(8,128)(2,1)S(1)}, u32[]{:S(2)}, u32[]{:S(2)}) collective-permute-start(bf16[256,512]{1,0:T(8,128)(2,1)S(1)} %bitcast.158), channel_id=1, source_target_pairs={{1,0},{2,1},{3,2},{4,3},{5,4},{6,5},{7,6},{8,7},{9,8},{10,9},{11,1... | collective-permute-start | bytes 786440 | tf_op jit(solution)/shard_map/ppermute | solution.py:163
  36.0 13.5 %collective-permute-start.3 = (bf16[256,512]{1,0:T(8,128)(2,1)S(1)}, bf16[256,512]{1,0:T(8,128)(2,1)S(1)}, u32[]{:S(2)}, u32[]{:S(2)}) collective-permute-start(bf16[256,512]{1,0:T(8,128)(2,1)S(1)} %bitcast.157), channel_id=1, source_target_pairs={{0,1},{1,2},{2,3},{3,4},{4,5},{5,6},{6,7},{7,8},{8,9},{9,10},{10,1... | collective-permute-start | bytes 786440 | tf_op jit(solution)/shard_map/ppermute | solution.py:162

commit v8 on v7

--- a/solution.py
+++ b/solution.py
@@ -5,23 +5,6 @@
 
 HB = 2
 TPB = 4
-
-
-def with_halo(cells, sides, width):
-    for axis, dim in sides:
-        count = lax.axis_size(axis)
-        ends = count - 1
-        head = lax.slice_in_dim(cells, 0, width, axis=dim)
-        tail = lax.slice_in_dim(cells, cells.shape[dim] - width, cells.shape[dim], axis=dim)
-        cells = jnp.concatenate(
-            [
-                lax.ppermute(tail, axis, [(i, (i + 1) % count) for i in range(ends)]),
-                cells,
-                lax.ppermute(head, axis, [((i + 1) % count, i) for i in range(ends)]),
-            ],
-            axis=dim,
-        )
-    return cells
 
 
 def passed_along(value, axis, by):
@@ -62,10 +45,6 @@
     return total
 
 
-def fetch_rim(values, block_rows):
-    return with_halo(values, (("node", 0),), HB * block_rows)
-
-
 def pair_weight(conv_weight):
     taps, chan_in, width = conv_weight.shape
     eye = jnp.eye(2, dtype=conv_weight.dtype)
@@ -80,7 +59,7 @@
     return jnp.kron(jnp.eye(steps, dtype=weight.dtype), weight)
 
 
-def shards(
+def stage(
     inputs, conv_weight, conv_bias, tile_values, tile_cols, tile_count, cheb_weight, cheb_bias
 ):
     row_count, flat_width = inputs.shape
@@ -89,30 +68,38 @@
     steps_dev = flat_width // chan_in
     block_count, block_rows = (tile_values.shape[0], tile_values.shape[2])
     feat_width = steps_dev * chan_out
-    earlier = passed_along(inputs, "tm", 1)
-    window = jnp.concatenate([earlier, inputs], axis=1)
+    rim = HB * block_rows
     wpair = pair_weight(conv_weight)
-    pair_w = 2 * chan_in
-    pieces = []
-    for p in range(steps_dev // 2):
-        base = steps_dev * chan_in + p * pair_w
-        newest = window[:, base : base + pair_w]
-        middle = window[:, base - pair_w : base]
-        oldest = window[:, base - 2 * pair_w : base - pair_w]
-        lhs = jnp.concatenate([newest, middle, oldest, newest], axis=1)
-        mixed = jnp.dot(lhs, wpair, preferred_element_type=jnp.float32)
-        for tt in range(2):
-            lo = tt * 2 * chan_out
-            linear = mixed[:, lo : lo + chan_out] + conv_bias[:chan_out]
-            gate = mixed[:, lo + chan_out : lo + 2 * chan_out] + conv_bias[chan_out:]
-            pieces.append(linear * jax.nn.sigmoid(gate))
-    flat_features = jnp.concatenate(pieces, axis=1).astype(jnp.bfloat16)
+
+    def conv(window):
+        pair_w = 2 * chan_in
+        pieces = []
+        for p in range(steps_dev // 2):
+            base = steps_dev * chan_in + p * pair_w
+            newest = window[:, base : base + pair_w]
+            middle = window[:, base - pair_w : base]
+            oldest = window[:, base - 2 * pair_w : base - pair_w]
+            lhs = jnp.concatenate([newest, middle, oldest, newest], axis=1)
+            mixed = jnp.dot(lhs, wpair, preferred_element_type=jnp.float32)
+            for tt in range(2):
+                lo = tt * 2 * chan_out
+                linear = mixed[:, lo : lo + chan_out] + conv_bias[:chan_out]
+                gate = mixed[:, lo + chan_out : lo + 2 * chan_out] + conv_bias[chan_out:]
+                pieces.append(linear * jax.nn.sigmoid(gate))
+        return jnp.concatenate(pieces, axis=1).astype(jnp.bfloat16)
+
+    edge_in = jnp.concatenate([inputs[:rim], inputs[row_count - rim :]], axis=0)
+    mid_in = inputs[rim : row_count - rim]
+    edge_prev = passed_along(edge_in, "tm", 1)
+    mid_prev = passed_along(mid_in, "tm", 1)
+    feat_edge = conv(jnp.concatenate([edge_prev, edge_in], axis=1))
+    feat_head = feat_edge[:rim]
+    feat_tail = feat_edge[rim:]
     first_block = lax.axis_index("node") * block_count
     band_tiles = build_band(tile_values, tile_cols, tile_count, first_block)
     node_count = lax.axis_size("node")
     to_right = [(i, i + 1) for i in range(node_count - 1)]
     to_left = [(i + 1, i) for i in range(node_count - 1)]
-    rim = HB * block_rows
     edge_ids = list(range(HB)) + list(range(block_count - HB, block_count))
     halo_band = []
     for b in edge_ids:
@@ -154,8 +141,13 @@
         padded = jnp.pad(values.reshape(block_count, block_rows, feat_width), ((HB, HB), (0, 0), (0, 0)))
         return band_product(band_tiles, padded)
 
-    feat_left = lax.ppermute(flat_features[row_count - rim :], "node", to_right)
-    feat_right = lax.ppermute(flat_features[:rim], "node", to_left)
+    feat_left = lax.ppermute(feat_tail, "node", to_right)
+    feat_right = lax.ppermute(feat_head, "node", to_left)
+    mid_window, _ = lax.optimization_barrier(
+        (jnp.concatenate([mid_prev, mid_in], axis=1), feat_edge)
+    )
+    feat_mid = conv(mid_window)
+    flat_features = jnp.concatenate([feat_head, feat_mid, feat_tail], axis=0)
     one_own = own_part(flat_features)
     order_one = (one_own + halo_part(feat_left, feat_right)).astype(jnp.bfloat16)
     order_one = order_one.reshape(row_count, feat_width)
@@ -173,6 +165,7 @@
     result = early + jnp.dot(cheb_two, kron[2], preferred_element_type=jnp.float32)
     return jax.nn.relu(result).astype(jnp.bfloat16).reshape(row_count, steps_dev, chan_out)
 
+
 def solution(mesh):
     placed = (
         P("node", "tm"),
@@ -185,5 +178,5 @@
         P(),
     )
     return jax.shard_map(
-        shards, mesh=mesh, in_specs=placed, out_specs=P("node", "tm", None), check_vma=False
+        stage, mesh=mesh, in_specs=placed, out_specs=P("node", "tm", None), check_vma=False
     )

time: 53.8 us -> 73.4 us (1.36)
  the two profiles are of different devices: /device:TPU:144 before, /device:TPU:128 now
where the time goes in v8:
time: 73.4 us; the launch traced here: 72.8 us
  local copies, waits for them, and re-layouts  21 us (29%)
  starting transfers between devices  18.2 us (25%)
  matrix products  17.6 us (24%)
  waiting for transfers between devices  9.89 us (13%)
  other arithmetic  5.47 us (7%)
  between operations  0.74 us (1%)
    dot_general x8, matrix products, band_product(): jnp.einsum('bpq,bqf->bpf', band_tiles[:, offset], extended[offset:offset...  7.66 us
    ppermute x1, waiting for transfers between devices, stage(): one_left = lax.ppermute(order_one[row_count - rim:], 'node', to_right)  7.06 us
    ppermute x2, starting transfers between devices, passed_along(): return lax.ppermute(value, axis, pairs)  5.52 us
    unnamed x64, local copies, waits for them, and re-layouts  5.38 us
    ppermute x1, starting transfers between devices, stage(): one_right = lax.ppermute(order_one[:rim], 'node', to_left)  4.44 us
    ppermute x1, starting transfers between devices, stage(): feat_right = lax.ppermute(feat_head, 'node', to_left)  4.2 us
    slice x1, local copies, waits for them, and re-layouts, band_product(): band_tiles[:, offset]  3.38 us
    dot_general x1, matrix products, stage(): jnp.dot(jnp.concatenate([flat_features, order_one], axis=1), jnp.concaten...  3.05 us
  transfers between devices with their start and end apart: 6, of which 2 were waited for; matrix products, arithmetic and copies ran while one was open for 34% of the time, Pallas kernels for 0%

profile of v8, /device:TPU:128, one launch (start us, length us, event | category | flops | bytes accessed | tf_op | source)
XLA Modules:
  0.0 72.8 jit_solution(15748203817317580892)
XLA Ops:
  0.0 1.1 %fusion.187 = (bf16[256,256]{1,0:T(8,128)(2,1)S(1)}, bf16[256,256]{1,0:T(8,128)(2,1)S(1)}) fusion(bf16[1024,256]{1,0:T(8,128)(2,1)} %param.8), kind=kLoop, calls=%fused_computation.279 | loop fusion | bytes 524288 | tf_op jit(solution)/shard_map/slice | solution.py:91
  1.1 1.8 %collective-permute-start = (bf16[512,256]{1,0:T(8,128)(2,1)S(1)}, bf16[512,256]{1,0:T(8,128)(2,1)S(1)}, u32[]{:S(2)}, u32[]{:S(2)}) collective-permute-start(bf16[512,256]{1,0:T(8,128)(2,1)S(1)} %pad_maximum_fusion.4), channel_id=1, source_target_pairs={{0,32},{32,64},{64,96},{96,128},{128,160},{160,192},{192,224},{1,3... | collective-permute-start | bytes 786440 | tf_op jit(solution)/shard_map/ppermute | solution.py:13
  2.9 1.0 %slice.289 = bf16[512,256]{1,0:T(8,128)(2,1)S(1)} slice(bf16[1024,256]{1,0:T(8,128)(2,1)} %param.8), slice={[256:768], [0:256]} | slice | bytes 524288 | tf_op jit(solution)/shard_map/slice | solution.py:92
  3.9 3.8 %collective-permute-start.1 = (bf16[512,256]{1,0:T(8,128)(2,1)S(1)}, bf16[512,256]{1,0:T(8,128)(2,1)S(1)}, u32[]{:S(2)}, u32[]{:S(2)}) collective-permute-start(bf16[512,256]{1,0:T(8,128)(2,1)S(1)} %slice.289), channel_id=1, source_target_pairs={{0,32},{32,64},{64,96},{96,128},{128,160},{160,192},{192,224},{1,3... | collective-permute-start | bytes 786440 | tf_op jit(solution)/shard_map/ppermute | solution.py:13
  7.9 1.3 %convolution_convert_fusion = bf16[8,5,128,128]{3,1,2,0:T(8,128)(2,1)S(1)} fusion(bf16[8,4,128,128]{3,2,1,0:T(8,128)(2,1)S(1)} %copy-done, s32[8,4]{1,0:T(8,128)S(1)} %copy.72, pred[8,4]{1,0:T(8,128)(4,1)S(1)} %iota_compare_fusion.2), kind=kOutput, calls=%fused_computation.21 | convolution fusion | flops 5898560 | bytes 2359456 | tf_op jit(solution)/shard_map/bjo,bjpq->bopq/dot_general | solution.py:24
  9.5 3.4 %fusion.180 = (bf16[8,1,128,128]{3,1,2,0:T(2,128)(2,1)}, bf16[8,1,128,128]{3,1,2,0:T(2,128)(2,1)}, bf16[8,1,128,128]{3,1,2,0:T(2,128)(2,1)}, bf16[8,1,128,128]{3,1,2,0:T(2,128)(2,1)}, bf16[8,1,128,128]{3,1,2,0:T(2,128)(2,1)}) fusion(bf16[8,5,128,128]{3,1,2,0:T(8,128)(2,1)S(1)} %convolution_convert_fusion), kind=kLoop, calls=%fused_computation.272 | loop fusion | bytes 2621440 | tf_op jit(solution)/shard_map/slice | solution.py:41
  16.2 1.5 %broadcast_multiply_fusion = (bf16[4,128,4,128]{3,2,1,0:T(4,128)(2,1)}, bf16[4,128,4,128]{3,2,1,0:T(4,128)(2,1)S(1)}, bf16[4,128,4,128]{3,2,1,0:T(4,128)(2,1)S(1)}) fusion(bf16[128,128]{1,0:T(8,128)(2,1)S(1)} %get-tuple-element.60, bf16[4,4]{1,0:T(4,128)(2,1)S(1)} %fusion.162, bf16[128,128]{1,0:T(8,128)(2,1)S(1)} %get-tuple-element.62, ...), kind=kLoop, calls=%fused_computation.186 | loop fusion | flops 786432 | bytes 1671200 | tf_op jit(solution)/shard_map/jit(kron)/mul | solution.py:59
  17.7 1.2 %copy_bitcast_fusion = (bf16[512,512]{1,0:T(8,128)(2,1)}, bf16[512,512]{1,0:T(8,128)(2,1)}) fusion(bf16[64,8,4,128]{3,2,1,0:T(4,128)(2,1)S(1)} %bitcast.140, bf16[64,8,4,128]{3,2,1,0:T(4,128)(2,1)S(1)} %bitcast.141), kind=kLoop, calls=%fused_computation.59 | loop fusion | bytes 2097152 | tf_op jit(solution)/shard_map/jit(kron)/mul | solution.py:59
  21.1 4.2 %collective-permute-start.3 = (bf16[256,512]{0,1:T(8,128)(2,1)}, bf16[256,512]{0,1:T(8,128)(2,1)}, u32[]{:S(2)}, u32[]{:S(2)}) collective-permute-start(bf16[256,512]{0,1:T(8,128)(2,1)} %get-tuple-element.37), channel_id=1, source_target_pairs={{1,0},{2,1},{3,2},{4,3},{5,4},{6,5},{7,6},{8,7},{9,8},{10,9},{11,1... | collective-permute-start | bytes 786440 | tf_op jit(solution)/shard_map/ppermute | solution.py:145
  25.3 1.9 %collective-permute-start.2 = (bf16[256,512]{0,1:T(8,128)(2,1)S(1)}, bf16[256,512]{0,1:T(8,128)(2,1)}, u32[]{:S(2)}, u32[]{:S(2)}) collective-permute-start(bf16[256,512]{0,1:T(8,128)(2,1)S(1)} %get-tuple-element.36), channel_id=1, source_target_pairs={{0,1},{1,2},{2,3},{3,4},{4,5},{5,6},{6,7},{7,8},{8,9},{9,10},{10,1... | collective-permute-start | bytes 786440 | tf_op jit(solution)/shard_map/ppermute | solution.py:144
  29.5 1.1 %pad_maximum_fusion = bf16[1024,512]{0,1:T(8,128)(2,1)S(1)} fusion(bf16[256,512]{0,1:T(8,128)(2,1)S(1)} %get-tuple-element.36, bf16[512,128]{0,1:T(8,128)(2,1)S(1)} %get-tuple-element.69, bf16[512,128]{0,1:T(8,128)(2,1)S(1)} %get-tuple-element.70, bf16[512,128]{0,1:T(8,128)(2,1)S(1)} %get-tuple-element.19, bf16[512,128]{0,1:T(8,128)(2,1)S(1)} %get-tuple-element.18, ...), kind=kLoop, calls=%fused_computation.38 | loop fusion | flops 6291456 | bytes 2097152 | tf_op jit(solution)/shard_map/concatenate | solution.py:150
  31.2 1.5 %fusion.20 = f32[8,128,512]{2,1,0:T(8,128)S(1)} fusion(bf16[8,128,512]{2,1,0:T(8,128)(2,1)S(1)} %bitcast.134, bf16[8,1,128,128]{3,1,2,0:T(2,128)(2,1)} %get-tuple-element.8), kind=kOutput, calls=%fused_computation.34 | convolution fusion | flops 134217728 | bytes 3407872 | tf_op jit(solution)/shard_map/bpq,bqf->bpf/dot_general | solution.py:39
  34.7 1.1 %slice_bitcast_fusion.4 = (bf16[1,128,512]{1,2,0:T(8,128)(2,1)S(1)}, bf16[1,128,512]{1,2,0:T(8,128)(2,1)S(1)}) fusion(bf16[256,512]{0,1:T(8,128)(2,1)} %collective-permute-done.3), kind=kLoop, calls=%fused_computation.205 | loop fusion | bytes 524288 | tf_op jit(solution)/shard_map/slice | solution.py:127
  35.7 2.8 %collective-permute-done.2 = bf16[256,512]{0,1:T(8,128)(2,1)} collective-permute-done((bf16[256,512]{0,1:T(8,128)(2,1)S(1)}, bf16[256,512]{0,1:T(8,128)(2,1)}, u32[]{:S(2)}, u32[]{:S(2)}) %collective-permute-start.2) | collective-permute-done | bytes 262176 | tf_op jit(solution)/shard_map/ppermute | solution.py:144
  38.5 1.0 %slice_bitcast_fusion.7 = (bf16[1,128,512]{1,2,0:T(8,128)(2,1)S(1)}, bf16[1,128,512]{1,2,0:T(8,128)(2,1)S(1)}) fusion(bf16[256,512]{0,1:T(8,128)(2,1)} %collective-permute-done.2), kind=kLoop, calls=%fused_computation.208 | loop fusion | bytes 524288 | tf_op jit(solution)/shard_map/slice | solution.py:125
  42.6 1.8 %fusion.23 = f32[8,128,512]{2,1,0:T(8,128)} fusion(bf16[8,128,512]{2,1,0:T(8,128)(2,1)S(1)} %fusion, bf16[8,1,128,128]{3,1,2,0:T(2,128)(2,1)S(1)} %copy-done.10), kind=kOutput, calls=%fused_computation.37 | convolution fusion | flops 134217728 | bytes 3407872 | tf_op jit(solution)/shard_map/bpq,bqf->bpf/dot_general | solution.py:39
  44.4 1.8 %fusion.128 = f32[8,128,512]{2,1,0:T(8,128)} fusion(bf16[8,128,512]{2,1,0:T(8,128)(2,1)S(1)} %fusion, bf16[8,1,128,128]{3,1,2,0:T(2,128)(2,1)S(1)} %copy-done.9), kind=kOutput, calls=%fused_computation.178 | convolution fusion | flops 134217728 | bytes 3407872 | tf_op jit(solution)/shard_map/bpq,bqf->bpf/dot_general | solution.py:39
  46.2 1.7 %fusion.21 = f32[8,128,512]{2,1,0:T(8,128)} fusion(bf16[8,128,512]{2,1,0:T(8,128)(2,1)S(1)} %fusion, bf16[8,1,128,128]{3,1,2,0:T(2,128)(2,1)S(1)} %copy-done.8), kind=kOutput, calls=%fused_computation.35 | convolution fusion | flops 134217728 | bytes 3407872 | tf_op jit(solution)/shard_map/bpq,bqf->bpf/dot_general | solution.py:32
  47.9 1.3 %copy.84 = bf16[1024,512]{0,1:T(8,128)(2,1)} copy(bf16[1024,512]{1,0:T(8,128)(2,1)S(1)} %bitcast.133) | data formatting | bytes 2097152 | tf_op jit(solution)/shard_map/reshape | solution.py:153
  49.2 4.4 %collective-permute-start.5 = (bf16[256,512]{1,0:T(8,128)(2,1)}, bf16[256,512]{1,0:T(8,128)(2,1)S(1)}, u32[]{:S(2)}, u32[]{:S(2)}) collective-permute-start(bf16[256,512]{1,0:T(8,128)(2,1)} %bitcast.149), channel_id=1, source_target_pairs={{1,0},{2,1},{3,2},{4,3},{5,4},{6,5},{7,6},{8,7},{9,8},{10,9},{11,1... | collective-permute-start | bytes 786440 | tf_op jit(solution)/shard_map/ppermute | solution.py:155
  53.7 2.1 %collective-permute-start.4 = (bf16[256,512]{1,0:T(8,128)(2,1)}, bf16[256,512]{1,0:T(8,128)(2,1)S(1)}, u32[]{:S(2)}, u32[]{:S(2)}) collective-permute-start(bf16[256,512]{1,0:T(8,128)(2,1)} %bitcast.148), channel_id=1, source_target_pairs={{0,1},{1,2},{2,3},{3,4},{4,5},{5,6},{6,7},{7,8},{8,9},{9,10},{10,1... | collective-permute-start | bytes 786440 | tf_op jit(solution)/shard_map/ppermute | solution.py:154
  55.8 3.1 %fusion.1 = f32[1024,512]{0,1:T(8,128)S(1)} fusion(bf16[1024,512]{0,1:T(8,128)(2,1)} %copy.84, bf16[256,512]{0,1:T(8,128)(2,1)S(1)} %get-tuple-element.36, bf16[512,128]{0,1:T(8,128)(2,1)} %copy-done.13, bf16[512,128]{0,1:T(8,128)(2,1)} %copy-done.14, bf16[512,128]{0,1:T(8,128)(2,1)} %copy-done.12, bf16[512,128]{0,1:T(8,128)(2,1)S(1)} %get-tuple-element.18, ...), kind=kOutput, calls=%fused_computation.2 | convolution fusion | flops 1090519040 | bytes 5242880 | tf_op jit(solution)/shard_map/dot_general | solution.py:158
  59.4 7.1 %collective-permute-done.4 = bf16[256,512]{1,0:T(8,128)(2,1)S(1)} collective-permute-done((bf16[256,512]{1,0:T(8,128)(2,1)}, bf16[256,512]{1,0:T(8,128)(2,1)S(1)}, u32[]{:S(2)}, u32[]{:S(2)}) %collective-permute-start.4) | collective-permute-done | bytes 262176 | tf_op jit(solution)/shard_map/ppermute | solution.py:154
  71.4 1.4 %copy.79 = bf16[1024,4,128]{2,1,0:T(4,128)(2,1)} copy(bf16[1024,4,128]{0,2,1:T(8,128)(2,1)S(1)} %bitcast.143) | data formatting | bytes 2097152 | tf_op jit(solution)/shard_map/reshape | solution.py:166
  (119 shorter events, 19.0 us)
Async XLA Ops:
  0.0 7.9 %copy-start = (bf16[8,4,128,128]{3,2,1,0:T(8,128)(2,1)S(1)}, bf16[8,4,128,128]{3,2,1,0:T(8,128)(2,1)}, u32[]{:S(2)}) copy-start(bf16[8,4,128,128]{3,2,1,0:T(8,128)(2,1)} %param.11) | copy-start | bytes 3145732
  0.0 7.7 %copy-start.25 = (s32[8,4]{0,1:T(4,128)S(1)}, s32[8,4]{0,1:T(4,128)}, u32[]{:S(2)}) copy-start(s32[8,4]{0,1:T(4,128)} %param.12) | copy-start | bytes 388
  0.0 7.8 %copy-start.28 = (s32[8]{0:T(128)S(1)}, s32[8]{0:T(128)}, u32[]{:S(2)}) copy-start(s32[8]{0:T(128)} %param.13) | copy-start | bytes 100
  1.1 17.8 %collective-permute-start = (bf16[512,256]{1,0:T(8,128)(2,1)S(1)}, bf16[512,256]{1,0:T(8,128)(2,1)S(1)}, u32[]{:S(2)}, u32[]{:S(2)}) collective-permute-start(bf16[512,256]{1,0:T(8,128)(2,1)S(1)} %pad_maximum_fusion.4), channel_id=1, source_target_pairs={{0,32},{32,64},{64,96},{96,128},{128,160},{160,192},{192,224},{1,3... | collective-permute-start | bytes 786440 | tf_op jit(solution)/shard_map/ppermute | solution.py:13
  3.9 23.4 %collective-permute-start.1 = (bf16[512,256]{1,0:T(8,128)(2,1)S(1)}, bf16[512,256]{1,0:T(8,128)(2,1)S(1)}, u32[]{:S(2)}, u32[]{:S(2)}) collective-permute-start(bf16[512,256]{1,0:T(8,128)(2,1)S(1)} %slice.289), channel_id=1, source_target_pairs={{0,32},{32,64},{64,96},{96,128},{128,160},{160,192},{192,224},{1,3... | collective-permute-start | bytes 786440 | tf_op jit(solution)/shard_map/ppermute | solution.py:13
  9.5 3.5 %copy-start.15 = (bf16[3,64,256]{2,1,0:T(8,128)(2,1)S(1)}, bf16[3,64,256]{2,1,0:T(8,128)(2,1)}, u32[]{:S(2)}) copy-start(bf16[3,64,256]{2,1,0:T(8,128)(2,1)} %param.9) | copy-start | bytes 294916
  9.5 4.0 %copy-start.26 = (f32[256]{0:T(256)S(1)}, f32[256]{0:T(256)}, u32[]{:S(2)}) copy-start(f32[256]{0:T(256)} %param.10) | copy-start | bytes 3076
  9.5 5.3 %copy-start.16 = (bf16[3,128,128]{2,1,0:T(8,128)(2,1)S(1)}, bf16[3,128,128]{2,1,0:T(8,128)(2,1)}, u32[]{:S(2)}) copy-start(bf16[3,128,128]{2,1,0:T(8,128)(2,1)} %param.14) | copy-start | bytes 294916
  12.9 1.9 %copy-start.27 = (f32[128]{0:T(128)S(1)}, f32[128]{0:T(128)}, u32[]{:S(2)}) copy-start(f32[128]{0:T(128)} %param.15) | copy-start | bytes 1540
  21.1 13.6 %collective-permute-start.3 = (bf16[256,512]{0,1:T(8,128)(2,1)}, bf16[256,512]{0,1:T(8,128)(2,1)}, u32[]{:S(2)}, u32[]{:S(2)}) collective-permute-start(bf16[256,512]{0,1:T(8,128)(2,1)} %get-tuple-element.37), channel_id=1, source_target_pairs={{1,0},{2,1},{3,2},{4,3},{5,4},{6,5},{7,6},{8,7},{9,8},{10,9},{11,1... | collective-permute-start | bytes 786440 | tf_op jit(solution)/shard_map/ppermute | solution.py:145
  25.3 13.3 %collective-permute-start.2 = (bf16[256,512]{0,1:T(8,128)(2,1)S(1)}, bf16[256,512]{0,1:T(8,128)(2,1)}, u32[]{:S(2)}, u32[]{:S(2)}) collective-permute-start(bf16[256,512]{0,1:T(8,128)(2,1)S(1)} %get-tuple-element.36), channel_id=1, source_target_pairs={{0,1},{1,2},{2,3},{3,4},{4,5},{5,6},{6,7},{7,8},{8,9},{9,10},{10,1... | collective-permute-start | bytes 786440 | tf_op jit(solution)/shard_map/ppermute | solution.py:144
  34.6 5.0 %copy-start.17 = (bf16[1,2,128,128]{3,2,1,0:T(8,128)(2,1)S(1)}, bf16[1,2,128,128]{3,2,1,0:T(8,128)(2,1)}, u32[]{:S(2)}) copy-start(bf16[1,2,128,128]{3,2,1,0:T(8,128)(2,1)} %pad_bitcast_fusion) | copy-start | bytes 196612
  34.6 5.0 %copy-start.19 = (bf16[1,2,128,128]{3,2,1,0:T(8,128)(2,1)S(1)}, bf16[1,2,128,128]{3,2,1,0:T(8,128)(2,1)}, u32[]{:S(2)}) copy-start(bf16[1,2,128,128]{3,2,1,0:T(8,128)(2,1)} %pad_bitcast_fusion.1) | copy-start | bytes 196612
  34.6 5.0 %copy-start.21 = (bf16[1,2,128,128]{3,2,1,0:T(8,128)(2,1)S(1)}, bf16[1,2,128,128]{3,2,1,0:T(8,128)(2,1)}, u32[]{:S(2)}) copy-start(bf16[1,2,128,128]{3,2,1,0:T(8,128)(2,1)} %maximum_bitcast_fusion.1) | copy-start | bytes 196612
  34.6 5.0 %copy-start.23 = (bf16[1,2,128,128]{3,2,1,0:T(8,128)(2,1)S(1)}, bf16[1,2,128,128]{3,2,1,0:T(8,128)(2,1)}, u32[]{:S(2)}) copy-start(bf16[1,2,128,128]{3,2,1,0:T(8,128)(2,1)} %maximum_bitcast_fusion) | copy-start | bytes 196612
  49.2 10.1 %collective-permute-start.5 = (bf16[256,512]{1,0:T(8,128)(2,1)}, bf16[256,512]{1,0:T(8,128)(2,1)S(1)}, u32[]{:S(2)}, u32[]{:S(2)}) collective-permute-start(bf16[256,512]{1,0:T(8,128)(2,1)} %bitcast.149), channel_id=1, source_target_pairs={{1,0},{2,1},{3,2},{4,3},{5,4},{6,5},{7,6},{8,7},{9,8},{10,9},{11,1... | collective-permute-start | bytes 786440 | tf_op jit(solution)/shard_map/ppermute | solution.py:155
  53.7 12.8 %collective-permute-start.4 = (bf16[256,512]{1,0:T(8,128)(2,1)}, bf16[256,512]{1,0:T(8,128)(2,1)S(1)}, u32[]{:S(2)}, u32[]{:S(2)}) collective-permute-start(bf16[256,512]{1,0:T(8,128)(2,1)} %bitcast.148), channel_id=1, source_target_pairs={{0,1},{1,2},{2,3},{3,4},{4,5},{5,6},{6,7},{7,8},{8,9},{9,10},{10,1... | collective-permute-start | bytes 786440 | tf_op jit(solution)/shard_map/ppermute | solution.py:154
  55.8 3.1 %copy-start.7 = (bf16[8,1,128,128]{3,1,2,0:T(2,128)(2,1)S(1)}, bf16[8,1,128,128]{3,1,2,0:T(2,128)(2,1)}, u32[]{:S(2)}) copy-start(bf16[8,1,128,128]{3,1,2,0:T(2,128)(2,1)} %get-tuple-element.10) | copy-start | bytes 786436
  59.3 7.3 %copy-start.18 = (bf16[1,2,128,128]{3,2,1,0:T(8,128)(2,1)S(1)}, bf16[1,2,128,128]{3,2,1,0:T(8,128)(2,1)}, u32[]{:S(2)}) copy-start(bf16[1,2,128,128]{3,2,1,0:T(8,128)(2,1)} %pad_bitcast_fusion) | copy-start | bytes 196612
  59.3 7.3 %copy-start.20 = (bf16[1,2,128,128]{3,2,1,0:T(8,128)(2,1)S(1)}, bf16[1,2,128,128]{3,2,1,0:T(8,128)(2,1)}, u32[]{:S(2)}) copy-start(bf16[1,2,128,128]{3,2,1,0:T(8,128)(2,1)} %pad_bitcast_fusion.1) | copy-start | bytes 196612
  59.3 7.3 %copy-start.22 = (bf16[1,2,128,128]{3,2,1,0:T(8,128)(2,1)S(1)}, bf16[1,2,128,128]{3,2,1,0:T(8,128)(2,1)}, u32[]{:S(2)}) copy-start(bf16[1,2,128,128]{3,2,1,0:T(8,128)(2,1)} %maximum_bitcast_fusion.1) | copy-start | bytes 196612
  59.3 7.3 %copy-start.24 = (bf16[1,2,128,128]{3,2,1,0:T(8,128)(2,1)S(1)}, bf16[1,2,128,128]{3,2,1,0:T(8,128)(2,1)}, u32[]{:S(2)}) copy-start(bf16[1,2,128,128]{3,2,1,0:T(8,128)(2,1)} %maximum_bitcast_fusion) | copy-start | bytes 196612
  66.6 2.3 %copy-start.3 = (f32[8,128,512]{2,1,0:T(8,128)S(1)}, f32[8,128,512]{2,1,0:T(8,128)}, u32[]{:S(2)}) copy-start(f32[8,128,512]{2,1,0:T(8,128)} %fusion.21) | copy-start | bytes 6291460
  67.0 2.6 %copy-start.1 = (f32[8,128,512]{2,1,0:T(8,128)S(1)}, f32[8,128,512]{2,1,0:T(8,128)}, u32[]{:S(2)}) copy-start(f32[8,128,512]{2,1,0:T(8,128)} %fusion.23) | copy-start | bytes 6291460
  (11 other events, 12.0 us)

commit v9 on v7

--- a/solution.py
+++ b/solution.py
@@ -5,23 +5,6 @@
 
 HB = 2
 TPB = 4
-
-
-def with_halo(cells, sides, width):
-    for axis, dim in sides:
-        count = lax.axis_size(axis)
-        ends = count - 1
-        head = lax.slice_in_dim(cells, 0, width, axis=dim)
-        tail = lax.slice_in_dim(cells, cells.shape[dim] - width, cells.shape[dim], axis=dim)
-        cells = jnp.concatenate(
-            [
-                lax.ppermute(tail, axis, [(i, (i + 1) % count) for i in range(ends)]),
-                cells,
-                lax.ppermute(head, axis, [((i + 1) % count, i) for i in range(ends)]),
-            ],
-            axis=dim,
-        )
-    return cells
 
 
 def passed_along(value, axis, by):
@@ -62,10 +45,6 @@
     return total
 
 
-def fetch_rim(values, block_rows):
-    return with_halo(values, (("node", 0),), HB * block_rows)
-
-
 def pair_weight(conv_weight):
     taps, chan_in, width = conv_weight.shape
     eye = jnp.eye(2, dtype=conv_weight.dtype)
@@ -80,7 +59,7 @@
     return jnp.kron(jnp.eye(steps, dtype=weight.dtype), weight)
 
 
-def shards(
+def stage(
     inputs, conv_weight, conv_bias, tile_values, tile_cols, tile_count, cheb_weight, cheb_bias
 ):
     row_count, flat_width = inputs.shape
@@ -173,6 +152,7 @@
     result = early + jnp.dot(cheb_two, kron[2], preferred_element_type=jnp.float32)
     return jax.nn.relu(result).astype(jnp.bfloat16).reshape(row_count, steps_dev, chan_out)
 
+
 def solution(mesh):
     placed = (
         P("node", "tm"),
@@ -185,5 +165,5 @@
         P(),
     )
     return jax.shard_map(
-        shards, mesh=mesh, in_specs=placed, out_specs=P("node", "tm", None), check_vma=False
+        stage, mesh=mesh, in_specs=placed, out_specs=P("node", "tm", None), check_vma=False
     )

time: 53.8 us -> 53.8 us (level)
  no operation moved by 1% of the time
where the time goes in v9:
time: 53.8 us; the launch traced here: 53.4 us
  waiting for transfers between devices  18 us (33%)
  starting transfers between devices  14.2 us (26%)
  matrix products  10.5 us (20%)
  local copies, waits for them, and re-layouts  7.94 us (15%)
  other arithmetic  2.33 us (4%)
    ppermute x1, waiting for transfers between devices, stage(): feat_left = lax.ppermute(flat_features[row_count - rim:], 'node', to_right)  7.8 us
    ppermute x1, waiting for transfers between devices, stage(): one_left = lax.ppermute(order_one[row_count - rim:], 'node', to_right)  5.18 us
    ppermute x1, starting transfers between devices, stage(): feat_right = lax.ppermute(flat_features[:rim], 'node', to_left)  4.21 us
    dot_general x8, matrix products, band_product(): jnp.einsum('bpq,bqf->bpf', band_tiles[:, offset], extended[offset:offset...  4.19 us
    ppermute x1, starting transfers between devices, stage(): one_left = lax.ppermute(order_one[row_count - rim:], 'node', to_right)  4.1 us
    ppermute x1, waiting for transfers between devices, stage(): feat_right = lax.ppermute(flat_features[:rim], 'node', to_left)  2.74 us
    slice x1, local copies, waits for them, and re-layouts, band_product(): band_tiles[:, offset]  2.65 us
    ppermute x1, waiting for transfers between devices, stage(): one_right = lax.ppermute(order_one[:rim], 'node', to_left)  2.32 us
  transfers between devices with their start and end apart: 5, of which 4 were waited for; matrix products, arithmetic and copies ran while one was open for 23% of the time, Pallas kernels for 0%

profile of v9, /device:TPU:144, one launch (start us, length us, event | category | flops | bytes accessed | tf_op | source)
XLA Modules:
  0.0 53.4 jit_solution(7988244123553267284)
XLA Ops:
  0.0 2.1 %collective-permute-start = (bf16[1024,256]{1,0:T(8,128)(2,1)}, bf16[1024,256]{1,0:T(8,128)(2,1)S(1)}, u32[]{:S(2)}, u32[]{:S(2)}) collective-permute-start(bf16[1024,256]{1,0:T(8,128)(2,1)} %param.8), channel_id=1, source_target_pairs={{0,32},{32,64},{64,96},{96,128},{128,160},{160,192},{192,224},{1,3... | collective-permute-start | bytes 1572872 | tf_op jit(solution)/shard_map/ppermute | solution.py:13
  2.1 1.1 %fusion.132 = (bf16[1024,128]{1,0:T(8,128)(2,1)S(1)}, bf16[1024,128]{1,0:T(8,128)(2,1)S(1)}) fusion(bf16[1024,256]{1,0:T(8,128)(2,1)} %param.8), kind=kLoop, calls=%fused_computation.214 | loop fusion | bytes 1048576 | tf_op jit(solution)/shard_map/slice | solution.py:78
  3.2 0.8 %fusion.134 = (f32[128]{0:T(128)S(1)}, f32[128]{0:T(128)S(1)}) fusion(f32[256]{0:T(256)} %param.10), kind=kLoop, calls=%fused_computation.216 | loop fusion | bytes 2048 | tf_op jit(solution)/shard_map/slice | solution.py:85
  4.0 0.8 %slice_bitcast_fusion.13 = (bf16[64,256]{1,0:T(8,128)(2,1)S(1)}, bf16[64,256]{1,0:T(8,128)(2,1)S(1)}, bf16[64,256]{1,0:T(8,128)(2,1)S(1)}) fusion(bf16[3,64,256]{2,1,0:T(8,128)(2,1)} %param.9), kind=kLoop, calls=%fused_computation.171 | loop fusion | bytes 196608 | tf_op jit(solution)/shard_map/jit(kron)/mul | solution.py:51
  5.5 1.3 %convolution_convert_fusion = bf16[8,5,128,128]{3,1,2,0:T(8,128)(2,1)S(1)} fusion(bf16[8,4,128,128]{3,2,1,0:T(8,128)(2,1)S(1)} %copy-done, s32[8,4]{1,0:T(8,128)S(1)} %copy.42, pred[8,4]{1,0:T(8,128)(4,1)S(1)} %iota_compare_fusion.2), kind=kOutput, calls=%fused_computation.7 | convolution fusion | flops 5898560 | bytes 2359456 | tf_op jit(solution)/shard_map/bjo,bjpq->bopq/dot_general | solution.py:24
  7.4 0.7 %broadcast_multiply_fusion = (bf16[4,128,4,128]{3,2,1,0:T(4,128)(2,1)S(1)}, bf16[4,128,4,128]{3,2,1,0:T(4,128)(2,1)S(1)}, bf16[4,128,4,128]{3,2,1,0:T(4,128)(2,1)S(1)}) fusion(bf16[128,128]{1,0:T(8,128)(2,1)S(1)} %get-tuple-element.52, bf16[4,4]{1,0:T(4,128)(2,1)S(1)} %fusion.107, bf16[128,128]{1,0:T(8,128)(2,1)S(1)} %get-tuple-element.54, ...), kind=kLoop, calls=%fused_computation.130 | loop fusion | flops 786432 | bytes 1671200 | tf_op jit(solution)/shard_map/jit(kron)/mul | solution.py:59
  8.2 2.6 %fusion.127 = (bf16[8,1,128,128]{3,1,2,0:T(2,128)(2,1)S(1)}, bf16[8,1,128,128]{3,1,2,0:T(2,128)(2,1)S(1)}, bf16[8,1,128,128]{3,1,2,0:T(2,128)(2,1)S(1)}, bf16[8,...) fusion(bf16[8,5,128,128]{3,1,2,0:T(8,128)(2,1)S(1)} %convolution_convert_fusion), kind=kLoop, calls=%fused_computation.209 | loop fusion | bytes 2621440 | tf_op jit(solution)/shard_map/slice | solution.py:41
  10.9 0.7 %fusion.10 = f32[1024,512]{1,0:T(8,128)S(1)} fusion(bf16[1024,128]{1,0:T(8,128)(2,1)S(1)} %get-tuple-element.33, bf16[1024,128]{1,0:T(8,128)(2,1)S(1)} %get-tuple-element.35, bf16[1024,128]{1,0:T(8,128)(2,1)S(1)} %get-tuple-element.34, bf16[128,512]{1,0:T(8,128)(2,1)S(1)} %fusion.91, bf16[128,512]{1,0:T(8,128)(2,1)S(1)} %bitcast.159, ...), kind=kOutput, calls=%fused_computation.24 | convolution fusion | flops 543162368 | bytes 3407872 | tf_op jit(solution)/shard_map/dot_general | solution.py:82
  12.0 0.7 %fusion.18 = f32[1024,512]{1,0:T(8,128)S(1)} fusion(bf16[1024,128]{1,0:T(8,128)(2,1)S(1)} %get-tuple-element.32, bf16[1024,128]{1,0:T(8,128)(2,1)S(1)} %get-tuple-element.34, bf16[1024,128]{1,0:T(8,128)(2,1)S(1)} %get-tuple-element.33, bf16[128,512]{1,0:T(8,128)(2,1)S(1)} %fusion.91, bf16[128,512]{1,0:T(8,128)(2,1)S(1)} %bitcast.160, ...), kind=kOutput, calls=%fused_computation.32 | convolution fusion | flops 543162368 | bytes 3407872 | tf_op jit(solution)/shard_map/dot_general | solution.py:82
  13.2 4.2 %collective-permute-start.2 = (bf16[256,512]{1,0:T(8,128)(2,1)S(1)}, bf16[256,512]{1,0:T(8,128)(2,1)S(1)}, u32[]{:S(2)}, u32[]{:S(2)}) collective-permute-start(bf16[256,512]{1,0:T(8,128)(2,1)S(1)} %get-tuple-element.31), channel_id=1, source_target_pairs={{1,0},{2,1},{3,2},{4,3},{5,4},{6,5},{7,6},{8,7},{9,8},{10,9},{11,1... | collective-permute-start | bytes 786440 | tf_op jit(solution)/shard_map/ppermute | solution.py:137
  17.4 1.9 %collective-permute-start.1 = (bf16[256,512]{1,0:T(8,128)(2,1)S(1)}, bf16[256,512]{1,0:T(8,128)(2,1)S(1)}, u32[]{:S(2)}, u32[]{:S(2)}) collective-permute-start(bf16[256,512]{1,0:T(8,128)(2,1)S(1)} %get-tuple-element.30), channel_id=1, source_target_pairs={{0,1},{1,2},{2,3},{3,4},{4,5},{5,6},{6,7},{7,8},{8,9},{9,10},{10,1... | collective-permute-start | bytes 786440 | tf_op jit(solution)/shard_map/ppermute | solution.py:136
  19.4 0.4 fusion.85
  21.1 2.7 %collective-permute-done.2 = bf16[256,512]{1,0:T(8,128)(2,1)S(1)} collective-permute-done((bf16[256,512]{1,0:T(8,128)(2,1)S(1)}, bf16[256,512]{1,0:T(8,128)(2,1)S(1)}, u32[]{:S(2)}, u32[]{:S(2)}) %collective-permute-start.2) | collective-permute-done | bytes 262176 | tf_op jit(solution)/shard_map/ppermute | solution.py:137
  23.8 7.8 %collective-permute-done.1 = bf16[256,512]{1,0:T(8,128)(2,1)S(1)} collective-permute-done((bf16[256,512]{1,0:T(8,128)(2,1)S(1)}, bf16[256,512]{1,0:T(8,128)(2,1)S(1)}, u32[]{:S(2)}, u32[]{:S(2)}) %collective-permute-start.1) | collective-permute-done | bytes 262176 | tf_op jit(solution)/shard_map/ppermute | solution.py:136
  32.2 0.6 %fusion = bf16[8,128,512]{2,1,0:T(8,128)(2,1)S(1)} fusion(f32[2,128,512]{2,1,0:T(8,128)S(1)} %get-tuple-element.29, f32[2,128,512]{2,1,0:T(8,128)S(1)} %get-tuple-element.28, f32[8,128,512]{2,1,0:T(8,128)S(1)} %fusion.6, f32[8,128,512]{2,1,0:T(8,128)S(1)} %fusion.85, f32[8,128,512]{2,1,0:T(8,128)S(1)} %fusion.4, f32[8,128,512]{2,1,0:T(8,128)S(1)} %fusion.5, ...), kind=kOutput, calls=%fused_computation.1 | convolution fusion | flops 138412032 | bytes 11796512 | tf_op jit(solution)/shard_map/bpq,bqf->bpf/dot_general | solution.py:39
  33.3 0.4 fusion.83
  34.1 1.9 %collective-permute-start.4 = (bf16[256,512]{1,0:T(8,128)(2,1)S(1)}, bf16[256,512]{1,0:T(8,128)(2,1)S(1)}, u32[]{:S(2)}, u32[]{:S(2)}) collective-permute-start(bf16[256,512]{1,0:T(8,128)(2,1)S(1)} %bitcast.158), channel_id=1, source_target_pairs={{1,0},{2,1},{3,2},{4,3},{5,4},{6,5},{7,6},{8,7},{9,8},{10,9},{11,1... | collective-permute-start | bytes 786440 | tf_op jit(solution)/shard_map/ppermute | solution.py:142
  36.0 4.1 %collective-permute-start.3 = (bf16[256,512]{1,0:T(8,128)(2,1)S(1)}, bf16[256,512]{1,0:T(8,128)(2,1)S(1)}, u32[]{:S(2)}, u32[]{:S(2)}) collective-permute-start(bf16[256,512]{1,0:T(8,128)(2,1)S(1)} %bitcast.157), channel_id=1, source_target_pairs={{0,1},{1,2},{2,3},{3,4},{4,5},{5,6},{6,7},{7,8},{8,9},{9,10},{10,1... | collective-permute-start | bytes 786440 | tf_op jit(solution)/shard_map/ppermute | solution.py:141
  40.3 1.3 %fusion.33 = f32[1024,512]{0,1:T(8,128)S(1)} fusion(bf16[1024,1024]{1,0:T(8,128)(2,1)S(1)} %constant_dynamic-update-slice_fusion, bf16[512,512]{1,0:T(8,128)(2,1)S(1)} %get-tuple-element.74, bf16[512,512]{1,0:T(8,128)(2,1)S(1)} %get-tuple-element.75), kind=kOutput, calls=%fused_computation.48 | convolution fusion | flops 1075838976 | bytes 5242880 | tf_op jit(solution)/shard_map/dot_general | solution.py:145
  42.0 2.3 %collective-permute-done.4 = bf16[256,512]{1,0:T(8,128)(2,1)S(1)} collective-permute-done((bf16[256,512]{1,0:T(8,128)(2,1)S(1)}, bf16[256,512]{1,0:T(8,128)(2,1)S(1)}, u32[]{:S(2)}, u32[]{:S(2)}) %collective-permute-start.4) | collective-permute-done | bytes 262176 | tf_op jit(solution)/shard_map/ppermute | solution.py:142
  44.4 5.2 %collective-permute-done.3 = bf16[256,512]{1,0:T(8,128)(2,1)S(1)} collective-permute-done((bf16[256,512]{1,0:T(8,128)(2,1)S(1)}, bf16[256,512]{1,0:T(8,128)(2,1)S(1)}, u32[]{:S(2)}, u32[]{:S(2)}) %collective-permute-start.3) | collective-permute-done | bytes 262176 | tf_op jit(solution)/shard_map/ppermute | solution.py:141
  50.1 1.1 %fusion.3 = bf16[8,128,512]{2,1,0:T(8,128)(2,1)S(1)} fusion(f32[2,128,512]{2,1,0:T(8,128)S(1)} %get-tuple-element.25, f32[2,128,512]{2,1,0:T(8,128)S(1)} %get-tuple-element.24, f32[8,128,512]{2,1,0:T(8,128)S(1)} %fusion.9, f32[8,128,512]{2,1,0:T(8,128)S(1)} %fusion.83, f32[8,128,512]{2,1,0:T(8,128)S(1)} %fusion.7, f32[8,128,512]{2,1,0:T(8,128)S(1)} %fusion.8, ...), kind=kOutput, calls=%fused_computation.5 | convolution fusion | flops 143654912 | bytes 12845088 | tf_op jit(solution)/shard_map/bpq,bqf->bpf/dot_general | solution.py:39
  51.2 0.8 %maximum_convert_fusion = bf16[1024,512]{0,1:T(8,128)(2,1)S(1)} fusion(f32[1024,512]{0,1:T(8,128)S(1)} %fusion.33, bf16[1024,512]{1,0:T(8,128)(2,1)S(1)} %bitcast.151, f32[512]{0:T(512)S(1)} %broadcast_bitcast_fusion, bf16[64,8,4,128]{3,2,1,0:T(4,128)(2,1)S(1)} %bitcast.153), kind=kOutput, calls=%fused_computation.6 | convolution fusion | flops 538968064 | bytes 4720640 | tf_op jit(solution)/shard_map/dot_general | solution.py:152
  52.0 1.4 %copy.44 = bf16[1024,4,128]{2,1,0:T(4,128)(2,1)} copy(bf16[1024,4,128]{0,2,1:T(8,128)(2,1)S(1)} %bitcast.152) | data formatting | bytes 2097152 | tf_op jit(solution)/shard_map/reshape | solution.py:153
  (62 shorter events, 6.0 us)
Async XLA Ops:
  0.0 5.5 %copy-start = (bf16[8,4,128,128]{3,2,1,0:T(8,128)(2,1)S(1)}, bf16[8,4,128,128]{3,2,1,0:T(8,128)(2,1)}, u32[]{:S(2)}) copy-start(bf16[8,4,128,128]{3,2,1,0:T(8,128)(2,1)} %param.11) | copy-start | bytes 3145732
  0.0 5.3 %copy-start.2 = (s32[8,4]{0,1:T(4,128)S(1)}, s32[8,4]{0,1:T(4,128)}, u32[]{:S(2)}) copy-start(s32[8,4]{0,1:T(4,128)} %param.12) | copy-start | bytes 388
  0.0 5.4 %copy-start.4 = (s32[8]{0:T(128)S(1)}, s32[8]{0:T(128)}, u32[]{:S(2)}) copy-start(s32[8]{0:T(128)} %param.13) | copy-start | bytes 100
  0.0 10.8 %collective-permute-start = (bf16[1024,256]{1,0:T(8,128)(2,1)}, bf16[1024,256]{1,0:T(8,128)(2,1)S(1)}, u32[]{:S(2)}, u32[]{:S(2)}) collective-permute-start(bf16[1024,256]{1,0:T(8,128)(2,1)} %param.8), channel_id=1, source_target_pairs={{0,32},{32,64},{64,96},{96,128},{128,160},{160,192},{192,224},{1,3... | collective-permute-start | bytes 1572872 | tf_op jit(solution)/shard_map/ppermute | solution.py:13
  5.5 1.7 %copy-start.1 = (bf16[3,128,128]{2,1,0:T(8,128)(2,1)S(1)}, bf16[3,128,128]{2,1,0:T(8,128)(2,1)}, u32[]{:S(2)}) copy-start(bf16[3,128,128]{2,1,0:T(8,128)(2,1)} %param.14) | copy-start | bytes 294916
  5.5 1.7 %copy-start.3 = (f32[128]{0:T(128)S(1)}, f32[128]{0:T(128)}, u32[]{:S(2)}) copy-start(f32[128]{0:T(128)} %param.15) | copy-start | bytes 1540
  13.2 10.7 %collective-permute-start.2 = (bf16[256,512]{1,0:T(8,128)(2,1)S(1)}, bf16[256,512]{1,0:T(8,128)(2,1)S(1)}, u32[]{:S(2)}, u32[]{:S(2)}) collective-permute-start(bf16[256,512]{1,0:T(8,128)(2,1)S(1)} %get-tuple-element.31), channel_id=1, source_target_pairs={{1,0},{2,1},{3,2},{4,3},{5,4},{6,5},{7,6},{8,7},{9,8},{10,9},{11,1... | collective-permute-start | bytes 786440 | tf_op jit(solution)/shard_map/ppermute | solution.py:137
  17.4 14.3 %collective-permute-start.1 = (bf16[256,512]{1,0:T(8,128)(2,1)S(1)}, bf16[256,512]{1,0:T(8,128)(2,1)S(1)}, u32[]{:S(2)}, u32[]{:S(2)}) collective-permute-start(bf16[256,512]{1,0:T(8,128)(2,1)S(1)} %get-tuple-element.30), channel_id=1, source_target_pairs={{0,1},{1,2},{2,3},{3,4},{4,5},{5,6},{6,7},{7,8},{8,9},{9,10},{10,1... | collective-permute-start | bytes 786440 | tf_op jit(solution)/shard_map/ppermute | solution.py:136
  34.1 10.2 %collective-permute-start.4 = (bf16[256,512]{1,0:T(8,128)(2,1)S(1)}, bf16[256,512]{1,0:T(8,128)(2,1)S(1)}, u32[]{:S(2)}, u32[]{:S(2)}) collective-permute-start(bf16[256,512]{1,0:T(8,128)(2,1)S(1)} %bitcast.158), channel_id=1, source_target_pairs={{1,0},{2,1},{3,2},{4,3},{5,4},{6,5},{7,6},{8,7},{9,8},{10,9},{11,1... | collective-permute-start | bytes 786440 | tf_op jit(solution)/shard_map/ppermute | solution.py:142
  36.0 13.5 %collective-permute-start.3 = (bf16[256,512]{1,0:T(8,128)(2,1)S(1)}, bf16[256,512]{1,0:T(8,128)(2,1)S(1)}, u32[]{:S(2)}, u32[]{:S(2)}) collective-permute-start(bf16[256,512]{1,0:T(8,128)(2,1)S(1)} %bitcast.157), channel_id=1, source_target_pairs={{0,1},{1,2},{2,3},{3,4},{4,5},{5,6},{6,7},{7,8},{8,9},{9,10},{10,1... | collective-permute-start | bytes 786440 | tf_op jit(solution)/shard_map/ppermute | solution.py:141
